TPU v7x, 128 devices: a whole 4x4x4 slice. The times are simulated.
128 devices in a mesh: aux: 8 (over y, core), occ: 16 (over x, z).
Axes of the slice: x: 4, y: 4, z: 4, core: 2. Of those that a mesh axis runs over, the one named last changes fastest.
Arguments:
- three_center: bfloat16 [1536, 64, 8192], P('occ', None, 'aux'), may hold values from -0.5 to 0.5
- coefficients: bfloat16 [1536, 64, 64], P('occ'), may hold values from -0.75 to 0.75
- target: int32 [1536], P('occ'), may hold values from 0 to 63, as said below
- domain_slot: int32 [1536], P('occ'), may hold values from 0 to 15
- owner_order: int32 [64], replicated, may hold values from 0 to 63, each once
Outputs:
- exchange_tiles: float32 [1024, 64, 1024], P('aux', 'occ')
Inputs may be any that keep to these rules, and one draw needn't show every extreme that they name: `target`: among the 96 tiles of one index of occ, at most 2 name the same occupied tile; some occupied tiles are named exactly 2 times by every index of occ. `owner_order`: each occupied tile appears exactly once.
All inputs are finite; a program needn't handle non-finite values.
Results may differ from a plain program's by a relative error of at most 0.0015.
Values may be sent and summed in bfloat16 or wider, within the bound.
No kernel may reach another device: no remote copies, remote signals or barrier semaphores. Data moves between devices by JAX's collectives and lax.ppermute only.
A program may use at most 192 MiB of HBM per device.

v0:
```python
import jax
import jax.numpy as jnp
from jax import lax
from jax.sharding import PartitionSpec as P

DOM = 16
CAP = 2


def domain_sums(pieces):
    received, labels = pieces
    onehot = (labels[..., None] == jnp.arange(DOM, dtype=jnp.int32)).astype(jnp.bfloat16)
    summed = jnp.einsum(
        "skce,skcmw->kemw", onehot, received, preferred_element_type=jnp.float32
    ).astype(jnp.bfloat16)
    return summed.reshape(summed.shape[0], summed.shape[1] * summed.shape[2], summed.shape[3])


def per_device(three_center, coefficients, target, domain_slot, owner_order):
    pair_count, tile_width, col_width = three_center.shape
    aux_count = col_width // tile_width
    occ_count = lax.axis_size("occ")
    tile_count = owner_order.shape[0]
    owned_tiles = tile_count // occ_count
    tile_ids = jnp.arange(tile_count, dtype=jnp.int32)
    position = jnp.sum(
        jnp.where(owner_order[None, :] == tile_ids[:, None], tile_ids[None, :], 0), axis=1
    )
    pair_ids = jnp.arange(pair_count, dtype=jnp.int32)
    earlier = (target[:, None] == target[None, :]) & (pair_ids[:, None] > pair_ids[None, :])
    buffer_slot = jnp.take(position, target) * CAP + jnp.sum(earlier.astype(jnp.int32), axis=1)
    labels = jnp.full((tile_count * CAP,), -1, jnp.int32).at[buffer_slot].set(domain_slot)
    labels = labels.reshape(occ_count, owned_tiles, CAP)
    blocks = jnp.einsum(
        "pmav,pvi->pmai",
        three_center.reshape(pair_count, tile_width, aux_count, tile_width),
        coefficients,
        preferred_element_type=jnp.float32,
    )
    blocks = blocks.astype(jnp.bfloat16).reshape(pair_count, tile_width, col_width)
    buffer = (
        jnp.zeros((tile_count * CAP, tile_width, col_width), jnp.bfloat16)
        .at[buffer_slot]
        .set(blocks)
    )
    buffer = buffer.reshape(occ_count, owned_tiles, CAP, tile_width, col_width)
    fitted = domain_sums(
        (
            lax.all_to_all(buffer, "occ", split_axis=0, concat_axis=0, tiled=True),
            lax.all_to_all(labels, "occ", split_axis=0, concat_axis=0, tiled=True),
        )
    )
    domain_rows = fitted.shape[1]
    held_rows = domain_rows // lax.axis_size("aux")
    partial_gram = jnp.einsum("krw,kcw->rkc", fitted, fitted, preferred_element_type=jnp.float32)
    summed = lax.psum_scatter(
        partial_gram.reshape(held_rows * lax.axis_size("aux"), owned_tiles * domain_rows),
        "aux",
        scatter_dimension=0,
        tiled=True,
    )
    return summed.reshape(summed.shape[0], owned_tiles, domain_rows)


def solution(mesh):
    in_specs = (P("occ", None, "aux"), P("occ", None, None), P("occ"), P("occ"), P())
    out_specs = P("aux", "occ", None)
    return jax.shard_map(
        per_device, mesh=mesh, in_specs=in_specs, out_specs=out_specs, check_vma=False
    )
```

profile of v0, /device:TPU:0, one launch (start us, length us, event | category | flops | bytes accessed | tf_op | source)
XLA Modules:
  0.0 686.5 jit_solution(6649366894771858481)
XLA Ops:
  6.5 0.7 compare_select_fusion.1
  7.2 0.9 convert_reduce_fusion
  8.1 0.8 select_reduce_fusion
  8.9 1.2 gather_fusion
  10.1 0.7 compare_select_fusion
  10.8 1.0 scatter_custom_fusion
  12.0 0.8 copy.38
  12.8 8.0 %all-to-all-start = ((s32[16,4,2]{1,2,0:T(2,128)}), s32[16,4,2]{1,2,0:T(2,128)S(1)}, u32[]{:S(2)}, u32[]{:S(2)}) async-start(s32[16,4,2]{1,2,0:T(2,128)} %copy.38), calls=%async_computation | async-start | bytes 32768 | tf_op jit(solution)/shard_map/all_to_all | solution.py:50
  20.8 21.5 %copy.40 = bf16[96,64,1024]{0,2,1:T(8,128)(2,1)} copy(bf16[96,64,1024]{2,1,0:T(8,128)(2,1)} %param.5) | data formatting | bytes 25165824 | tf_op args[0]
  42.3 40.3 %copy.41 = bf16[96,64,16,64]{3,1,2,0:T(8,128)(2,1)} copy(bf16[96,64,16,64]{0,3,2,1:T(8,128)(2,1)} %bitcast.23) | data formatting | bytes 25165824 | tf_op jit(solution)/shard_map/reshape | solution.py:36
  82.6 2.3 copy.49
  84.9 17.9 %convolution_convert_fusion = bf16[96,64,16,64]{3,1,2,0:T(8,128)(2,1)} fusion(bf16[96,64,16,64]{3,1,2,0:T(8,128)(2,1)} %copy.41, bf16[96,64,64,1]{2,1,3,0:T(8,128)(2,1)S(1)} %copy.49), kind=kOutput, calls=%fused_computation.6 | convolution fusion | flops 811597824 | bytes 25952256 | tf_op jit(solution)/shard_map/pmav,pvi->pmai/dot_general | solution.py:34
  102.8 35.8 %copy.43 = bf16[96,64,16,64]{0,3,2,1:T(8,128)(2,1)} copy(bf16[96,64,16,64]{3,1,2,0:T(8,128)(2,1)} %convolution_convert_fusion) | data formatting | bytes 25165824 | tf_op jit(solution)/shard_map/convert_element_type | solution.py:40
  138.6 22.3 %copy.44 = bf16[96,64,1024]{2,1,0:T(8,128)(2,1)} copy(bf16[96,64,1024]{0,2,1:T(8,128)(2,1)} %bitcast.22) | data formatting | bytes 25165824 | tf_op jit(solution)/shard_map/reshape | solution.py:40
  160.9 6.0 broadcast_in_dim.42
  166.9 32.9 %scatter_fusion = bf16[128,64,1024]{2,1,0:T(8,128)(2,1)} fusion(bf16[128,64,1024]{2,1,0:T(8,128)(2,1)} %broadcast_in_dim.42, s32[96]{0:T(128)S(1)} %compare_select_fusion, bf16[96,64,1024]{2,1,0:T(8,128)(2,1)} %copy.44), kind=kCustom, calls=%fused_computation.2 | custom fusion | bytes 37749120 | tf_op jit(solution)/shard_map/scatter | solution.py:44
  199.8 30.8 %copy.45 = bf16[16,4,2,64,1024]{4,2,3,1,0:T(2,128)(2,1)} copy(bf16[16,4,2,64,1024]{4,3,2,1,0:T(8,128)(2,1)} %bitcast.21) | data formatting | bytes 33554432 | tf_op jit(solution)/shard_map/reshape | solution.py:46
  230.6 7.3 %all-to-all-start.1 = ((bf16[16,4,2,64,1024]{4,2,3,1,0:T(2,128)(2,1)}), bf16[16,4,2,64,1024]{4,2,3,1,0:T(2,128)(2,1)}, u32[]{:S(2)}, u32[]{:S(2)}) async-start(bf16[16,4,2,64,1024]{4,2,3,1,0:T(2,128)(2,1)} %copy.45), calls=%async_computation.1 | async-start | bytes 33554432 | tf_op jit(solution)/shard_map/all_to_all | solution.py:49
  238.2 291.7 %all-to-all-done.1 = bf16[16,4,2,64,1024]{4,2,3,1,0:T(2,128)(2,1)} async-done(((bf16[16,4,2,64,1024]{4,2,3,1,0:T(2,128)(2,1)}), bf16[16,4,2,64,1024]{4,2,3,1,0:T(2,128)(2,1)}, u32[]{:S(2)}, u32[]{:S(2)}) %all-to-all-start.1) | async-done | bytes 16777248 | tf_op jit(solution)/shard_map/all_to_all | solution.py:49
  529.9 18.5 %bitcast_convert_fusion = bf16[4,16,64,1024]{3,1,2,0:T(8,128)(2,1)} fusion(bf16[16,4,2,64,1024]{4,2,3,1,0:T(2,128)(2,1)} %all-to-all-done.1, s32[16,4,2]{0,2,1:T(2,128)S(1)} %copy.39), kind=kOutput, calls=%fused_computation.3 | convolution fusion | flops 272631808 | bytes 25166336 | tf_op jit(solution)/shard_map/skce,skcmw->kemw/dot_general | solution.py:13
  548.4 11.6 %copy.47 = bf16[4,16,64,1024]{3,2,1,0:T(8,128)(2,1)} copy(bf16[4,16,64,1024]{3,1,2,0:T(8,128)(2,1)} %bitcast_convert_fusion) | data formatting | bytes 16777216 | tf_op jit(solution)/shard_map/convert_element_type | solution.py:15
  560.0 17.0 %fusion.10 = f32[4,1024,1024]{2,1,0:T(8,128)} fusion(bf16[4,1024,1024]{2,1,0:T(8,128)(2,1)} %bitcast.25), kind=kOutput, calls=%fused_computation.21 | convolution fusion | flops 8589934592 | bytes 25165824 | tf_op jit(solution)/shard_map/krw,kcw->rkc/dot_general | solution.py:55
  577.0 99.5 %reduce-scatter.2.cloned.1.call-done = f32[128,4096]{0,1:T(8,128)} async-done(((f32[1024,4096]{0,1:T(8,128)}), f32[128,4096]{0,1:T(8,128)}) %reduce-scatter.2.cloned.1.call-update) | async-done | bytes 2097168 | tf_op jit(solution)/shard_map/reduce_scatter | solution.py:56
  676.6 3.0 copy.54
  (8 shorter events, 0.5 us)
Async XLA Ops:
  12.8 217.8 %all-to-all-start = ((s32[16,4,2]{1,2,0:T(2,128)}), s32[16,4,2]{1,2,0:T(2,128)S(1)}, u32[]{:S(2)}, u32[]{:S(2)}) async-start(s32[16,4,2]{1,2,0:T(2,128)} %copy.38), calls=%async_computation | async-start | bytes 32768 | tf_op jit(solution)/shard_map/all_to_all | solution.py:50
  42.3 40.3 %copy-start = (bf16[96,64,64]{0,2,1:T(8,128)(2,1)S(1)}, bf16[96,64,64]{0,2,1:T(8,128)(2,1)}, u32[]{:S(2)}) copy-start(bf16[96,64,64]{0,2,1:T(8,128)(2,1)} %param.6) | copy-start | bytes 2359300
  230.6 299.4 %all-to-all-start.1 = ((bf16[16,4,2,64,1024]{4,2,3,1,0:T(2,128)(2,1)}), bf16[16,4,2,64,1024]{4,2,3,1,0:T(2,128)(2,1)}, u32[]{:S(2)}, u32[]{:S(2)}) async-start(bf16[16,4,2,64,1024]{4,2,3,1,0:T(2,128)(2,1)} %copy.45), calls=%async_computation.1 | async-start | bytes 33554432 | tf_op jit(solution)/shard_map/all_to_all | solution.py:49
  237.9 438.7 %reduce-scatter.2.cloned.1.call-start = ((), (), s32[]{:S(2)}) async-start(), calls=%async_computation.3 | async-start | bytes 18874368 | tf_op jit(solution)/shard_map/reduce_scatter | solution.py:56
Sparse Core Ops, SparseCore 0:
  577.1 99.3 reduce-scatter.1
where the time goes:
time: 690 us; the launch traced here: 686 us
  waiting for transfers between devices  391 us (57%)
  local copies, waits for them, and re-layouts  210 us (30%)
  matrix products  53.3 us (8%)
  starting transfers between devices  15.5 us (2%)
  between operations  13.5 us (2%)
    all_to_all x1, waiting for transfers between devices, per_device(): lax.all_to_all(buffer, 'occ', split_axis=0, concat_axis=0, tiled=True)  292 us
    reduce_scatter x1, waiting for transfers between devices, per_device(): lax.psum_scatter(partial_gram.reshape(held_rows * lax.axis_size('aux'), o...  99.5 us
    reshape x1, local copies, waits for them, and re-layouts, per_device(): three_center.reshape(pair_count, tile_width, aux_count, tile_width)  40.3 us
    convert_element_type x1, local copies, waits for them, and re-layouts, per_device(): blocks.astype(jnp.bfloat16).reshape(pair_count, tile_width, col_width)  35.8 us
    scatter x1, local copies, waits for them, and re-layouts, per_device(): buffer = jnp.zeros((tile_count * CAP, tile_width, col_width), jnp.bfloat1...  32.9 us
    reshape x1, local copies, waits for them, and re-layouts, per_device(): buffer = buffer.reshape(occ_count, owned_tiles, CAP, tile_width, col_width)  30.8 us
    unnamed x4, local copies, waits for them, and re-layouts  23.8 us
    reshape x1, local copies, waits for them, and re-layouts, per_device(): blocks.astype(jnp.bfloat16).reshape(pair_count, tile_width, col_width)  22.3 us
  transfers between devices with their start and end apart: 3, of which 2 were waited for; matrix products, arithmetic and copies ran while one was open for 31% of the time, Pallas kernels for 0%

commit v1 on v0

v1 whole, which is shorter than its diff:
```python
import math

import jax
import jax.numpy as jnp
from jax import lax
from jax.experimental import pallas as pl
from jax.experimental.pallas import tpu as pltpu
from jax.sharding import PartitionSpec as P

DOM = 16
CAP = 2
LANES = 256


def _transform_kernel(slot_ref, empty_ref, tc_ref, w_ref, out_hbm, buf, zero, sems):
    step = pl.program_id(0)
    steps = pl.num_programs(0)
    per = tc_ref.shape[0]
    epr = sems.shape[1] - per
    rows, width = tc_ref.shape[1], tc_ref.shape[2]
    groups = width // LANES
    half = w_ref.shape[1]
    side = buf.at[step % 2]

    @pl.when(step == 0)
    def _():
        zero[...] = jnp.zeros_like(zero)

    def copies(at, parity):
        held = buf.at[parity]
        out = [
            pltpu.make_async_copy(held.at[j], out_hbm.at[slot_ref[at * per + j]], sems.at[parity, j])
            for j in range(per)
        ]
        out += [
            pltpu.make_async_copy(zero, out_hbm.at[empty_ref[at * epr + j]], sems.at[parity, per + j])
            for j in range(epr)
        ]
        return out

    @pl.when(step >= 2)
    def _():
        for cp in copies(step - 2, step % 2):
            cp.wait()

    pad = jnp.zeros((half, half), w_ref.dtype)
    for j in range(per):
        w2 = w_ref[j]
        w4 = jnp.concatenate(
            [jnp.concatenate([w2, pad], axis=1), jnp.concatenate([pad, w2], axis=1)], axis=0
        )
        x = tc_ref[j]
        stacked = jnp.concatenate([x[:, g * LANES:(g + 1) * LANES] for g in range(groups)], axis=0)
        y = jnp.dot(stacked, w4, preferred_element_type=jnp.float32).astype(buf.dtype)
        for g in range(groups):
            side[j, :, g * LANES:(g + 1) * LANES] = y[g * rows:(g + 1) * rows]

    for cp in copies(step, step % 2):
        cp.start()

    @pl.when(step == steps - 1)
    def _():
        for cp in copies(step - 1, (step + 1) % 2):
            cp.wait()
        for cp in copies(step, step % 2):
            cp.wait()


def transform_into_slots(three_center, coefficients, buffer_slot, empty_slot, slot_count):
    pair_count, rows, width = three_center.shape
    tile = coefficients.shape[1]
    empty_count = empty_slot.shape[0]
    steps = math.gcd(pair_count, empty_count)
    steps = 8 if steps % 8 == 0 else steps
    per = pair_count // steps
    epr = empty_count // steps
    zeros = jnp.zeros_like(coefficients)
    w2 = jnp.concatenate(
        [
            jnp.concatenate([coefficients, zeros], axis=2),
            jnp.concatenate([zeros, coefficients], axis=2),
        ],
        axis=1,
    )
    grid_spec = pltpu.PrefetchScalarGridSpec(
        num_scalar_prefetch=2,
        grid=(steps,),
        in_specs=[
            pl.BlockSpec((per, rows, width), lambda i, s, e: (i, 0, 0)),
            pl.BlockSpec((per, 2 * tile, 2 * tile), lambda i, s, e: (i, 0, 0)),
        ],
        out_specs=pl.BlockSpec(memory_space=pl.ANY),
        scratch_shapes=[
            pltpu.VMEM((2, per, rows, width), three_center.dtype),
            pltpu.VMEM((rows, width), three_center.dtype),
            pltpu.SemaphoreType.DMA((2, per + epr)),
        ],
    )
    block_bytes = rows * width * 2
    return pl.pallas_call(
        _transform_kernel,
        grid_spec=grid_spec,
        out_shape=jax.ShapeDtypeStruct((slot_count, rows, width), three_center.dtype),
        compiler_params=pltpu.CompilerParams(dimension_semantics=("arbitrary",)),
        cost_estimate=pl.CostEstimate(
            flops=2 * pair_count * rows * width * 4 * tile,
            transcendentals=0,
            bytes_accessed=(pair_count + slot_count) * block_bytes,
        ),
    )(buffer_slot, empty_slot, three_center, w2)


def _gram_kernel(lab_ref, x_ref, o_ref, acc):
    k = pl.program_id(0)
    sources, cap = x_ref.shape[0], x_ref.shape[1]
    per_source = lab_ref.shape[0] // sources
    acc[...] = jnp.zeros_like(acc)
    for s in range(sources):
        for c in range(cap):
            e = lab_ref[s * per_source + k * cap + c]

            @pl.when(e >= 0)
            def _():
                acc[e] += x_ref[s, c].astype(jnp.float32)

    dom, rows, width = acc.shape
    fitted = acc[...].astype(x_ref.dtype).reshape(dom * rows, width)
    o_ref[...] = lax.dot_general(
        fitted, fitted, (((1,), (1,)), ((), ())), preferred_element_type=jnp.float32
    )


def domain_gram(received, labels, dom):
    sources, slots, rows, width = received.shape
    owned = slots // CAP
    domain_rows = dom * rows
    grid_spec = pltpu.PrefetchScalarGridSpec(
        num_scalar_prefetch=1,
        grid=(owned,),
        in_specs=[pl.BlockSpec((sources, CAP, rows, width), lambda k, lab: (0, k, 0, 0))],
        out_specs=pl.BlockSpec((domain_rows, domain_rows), lambda k, lab: (0, k)),
        scratch_shapes=[pltpu.VMEM((dom, rows, width), jnp.float32)],
    )
    return pl.pallas_call(
        _gram_kernel,
        grid_spec=grid_spec,
        out_shape=jax.ShapeDtypeStruct((domain_rows, owned * domain_rows), jnp.float32),
        compiler_params=pltpu.CompilerParams(
            dimension_semantics=("arbitrary",), vmem_limit_bytes=60 * 1024 * 1024
        ),
        cost_estimate=pl.CostEstimate(
            flops=2 * owned * domain_rows * domain_rows * width,
            transcendentals=0,
            bytes_accessed=sources * slots * rows * width * 2 + owned * domain_rows * domain_rows * 4,
        ),
    )(labels.reshape(-1), received)


def per_device(three_center, coefficients, target, domain_slot, owner_order):
    pair_count, tile_width, col_width = three_center.shape
    occ_count = lax.axis_size("occ")
    tile_count = owner_order.shape[0]
    owned_tiles = tile_count // occ_count
    slot_count = tile_count * CAP
    tile_ids = jnp.arange(tile_count, dtype=jnp.int32)
    position = jnp.sum(
        jnp.where(owner_order[None, :] == tile_ids[:, None], tile_ids[None, :], 0), axis=1
    )
    pair_ids = jnp.arange(pair_count, dtype=jnp.int32)
    earlier = (target[:, None] == target[None, :]) & (pair_ids[:, None] > pair_ids[None, :])
    buffer_slot = jnp.take(position, target) * CAP + jnp.sum(earlier.astype(jnp.int32), axis=1)
    labels = jnp.full((slot_count,), -1, jnp.int32).at[buffer_slot].set(domain_slot)
    empty_count = slot_count - pair_count
    empty_slot = jnp.nonzero(labels < 0, size=empty_count, fill_value=0)[0].astype(jnp.int32)
    labels = labels.reshape(occ_count, owned_tiles * CAP)

    buffer = transform_into_slots(three_center, coefficients, buffer_slot, empty_slot, slot_count)
    buffer = buffer.reshape(occ_count, owned_tiles * CAP * tile_width, col_width)
    received = lax.all_to_all(buffer, "occ", split_axis=0, concat_axis=0, tiled=True)
    received_labels = lax.all_to_all(labels, "occ", split_axis=0, concat_axis=0, tiled=True)
    received = received.reshape(occ_count, owned_tiles * CAP, tile_width, col_width)

    partial_gram = domain_gram(received, received_labels, DOM)
    domain_rows = partial_gram.shape[0]
    summed = lax.psum_scatter(partial_gram, "aux", scatter_dimension=0, tiled=True)
    return summed.reshape(summed.shape[0], owned_tiles, domain_rows)


def solution(mesh):
    in_specs = (P("occ", None, "aux"), P("occ", None, None), P("occ"), P("occ"), P())
    out_specs = P("aux", "occ", None)
    return jax.shard_map(
        per_device, mesh=mesh, in_specs=in_specs, out_specs=out_specs, check_vma=False
    )
```

time: 690 us -> 475 us (0.69)
  local copies, waits for them, and re-layouts: 210 us -> 11.2 us
  matrix products: 53.3 us -> 0 us
  Pallas kernels: 0 us -> 34.5 us
  other arithmetic: 3 us -> 10.1 us
    reshape x5 -> x2, local copies, waits for them, and re-layouts: 94.3 us -> 0.72 us  [the longest x1 0.6 us: domain_gram(): labels.reshape(-1)]
    dot_general x3 -> x0, matrix products: 53.3 us -> none  [the longest x1 18.5 us: domain_sums(): jnp.einsum('skce,skcmw->kemw', onehot, received, preferred_element_type=j...]
    convert_element_type x2 -> x0, local copies, waits for them, and re-layouts: 47.4 us -> none  [the longest x1 35.8 us: per_device(): blocks.astype(jnp.bfloat16).reshape(pair_count, tile_width, col_width)]
    pallas_call x0 -> x2, Pallas kernels: none -> 34.5 us  [the longest x1 18.8 us: domain_gram(): pl.pallas_call(_gram_kernel, grid_spec=grid_spec, out_shape=jax.ShapeDtyp...]
    scatter x2 -> x1, local copies, waits for them, and re-layouts: 33.9 us -> 1 us  [per_device(): jnp.full((slot_count,), -1, jnp.int32).at[buffer_slot].set(domain_slot)]
    unnamed x4 -> x1, local copies, waits for them, and re-layouts: 23.8 us -> 3.3 us
  transfers between devices with their start and end apart: 3 -> 3, of which waited for: 2 -> 2; matrix products, arithmetic and copies ran while one was open for 31% -> 2% of each run, Pallas kernels for 0% -> 3%
where the time goes in v1:
time: 475 us; the launch traced here: 474 us
  waiting for transfers between devices  390 us (82%)
  Pallas kernels  34.5 us (7%)
  starting transfers between devices  15.3 us (3%)
  between operations  13.5 us (3%)
  local copies, waits for them, and re-layouts  11.2 us (2%)
  other arithmetic  10.1 us (2%)
    all_to_all x1, waiting for transfers between devices, per_device(): lax.all_to_all(buffer, 'occ', split_axis=0, concat_axis=0, tiled=True)  290 us
    reduce_scatter x1, waiting for transfers between devices, per_device(): lax.psum_scatter(partial_gram, 'aux', scatter_dimension=0, tiled=True)  99.5 us
    pallas_call x1, Pallas kernels, domain_gram(): pl.pallas_call(_gram_kernel, grid_spec=grid_spec, out_shape=jax.ShapeDtyp...  18.8 us
    pallas_call x1, Pallas kernels, transform_into_slots(): pl.pallas_call(_transform_kernel, grid_spec=grid_spec, out_shape=jax.Shap...  15.8 us
  transfers between devices with their start and end apart: 3, of which 2 were waited for; matrix products, arithmetic and copies ran while one was open for 2% of the time, Pallas kernels for 3%

profile of v1, /device:TPU:0, one launch (start us, length us, event | category | flops | bytes accessed | tf_op | source)
XLA Modules:
  0.0 474.4 jit_solution(3900605075662077192)
XLA Ops:
  6.5 0.9 convert_reduce_fusion
  7.4 0.7 compare_select_fusion.2
  8.1 0.8 select_reduce_fusion
  8.9 1.2 gather_fusion
  10.1 1.2 compare_select_fusion.1
  11.3 1.0 scatter_custom_fusion
  12.3 0.7 all_to_all.9
  13.0 8.0 %all-to-all-start = ((s32[16,1,8]{2,1,0:T(1,128)}), s32[16,1,8]{2,1,0:T(1,128)S(1)}, u32[]{:S(2)}, u32[]{:S(2)}) async-start(s32[16,1,8]{2,1,0:T(1,128)} %bitcast), calls=%async_computation | async-start | bytes 16384 | tf_op jit(solution)/shard_map/all_to_all | solution.py:180
  21.0 0.7 fusion.7
  21.7 0.1 copy.20
  21.8 0.2 reduce-window.14
  22.1 1.4 scatter_custom_fusion.1
  23.8 3.3 copy.22
  27.1 2.2 fusion.2.w_ref
  29.3 1.2 compare_select_fusion.5.empty_ref
  30.5 15.8 %shard_map.55 = bf16[128,64,1024]{2,1,0:T(8,128)(2,1)} custom-call(s32[96]{0:T(128)} %get-tuple-element.6.slot_ref, s32[32]{0:T(128)} %compare_select_fusion.5.empty_ref, bf16[96,64,1024]{2,1,0:T(8,128)(2,1)} %tc_ref.1, bf16[96,128,128]{2,1,0:T(8,128)(2,1)} %fusion.2.w_ref), custom_call_target="tpu_custom_call" | custom-call | flops 3221225472 | bytes 29360128 | tf_op jit(solution)/shard_map/pallas_call | solution.py:100
  46.3 7.3 %all-to-all-start.1 = ((bf16[16,512,1024]{2,1,0:T(8,128)(2,1)}), bf16[16,512,1024]{2,1,0:T(8,128)(2,1)}, u32[]{:S(2)}, u32[]{:S(2)}) async-start(bf16[16,512,1024]{2,1,0:T(8,128)(2,1)} %bitcast.7), calls=%async_computation.1 | async-start | bytes 33554432 | tf_op jit(solution)/shard_map/all_to_all | solution.py:179
  53.6 0.5 broadcast.68
  54.1 0.7 reduce.6
  54.8 0.6 reshape.82.lab_ref
  55.4 290.2 %all-to-all-done.1 = bf16[16,512,1024]{2,1,0:T(8,128)(2,1)} async-done(((bf16[16,512,1024]{2,1,0:T(8,128)(2,1)}), bf16[16,512,1024]{2,1,0:T(8,128)(2,1)}, u32[]{:S(2)}, u32[]{:S(2)}) %all-to-all-start.1) | async-done | bytes 16777248 | tf_op jit(solution)/shard_map/all_to_all | solution.py:179
  345.7 18.8 %shard_map.56 = f32[1024,4096]{1,0:T(8,128)} custom-call(s32[128]{0:T(128)} %reshape.82.lab_ref, bf16[16,8,64,1024]{3,2,1,0:T(8,128)(2,1)} %bitcast.4.x_ref), custom_call_target="tpu_custom_call" | custom-call | flops 8589934592 | bytes 33554432 | tf_op jit(solution)/shard_map/pallas_call | solution.py:144
  364.5 99.5 %reduce-scatter.2.cloned.1.call-done = f32[128,4096]{1,0:T(8,128)} async-done(((f32[1024,4096]{1,0:T(8,128)}), f32[128,4096]{1,0:T(8,128)}) %reduce-scatter.2.cloned.1.call-update) | async-done | bytes 2097168 | tf_op jit(solution)/shard_map/reduce_scatter | solution.py:185
  463.9 3.6 reshape.88
  (10 shorter events, 0.4 us)
Async XLA Ops:
  13.0 33.2 %all-to-all-start = ((s32[16,1,8]{2,1,0:T(1,128)}), s32[16,1,8]{2,1,0:T(1,128)S(1)}, u32[]{:S(2)}, u32[]{:S(2)}) async-start(s32[16,1,8]{2,1,0:T(1,128)} %bitcast), calls=%async_computation | async-start | bytes 16384 | tf_op jit(solution)/shard_map/all_to_all | solution.py:180
  46.3 299.4 %all-to-all-start.1 = ((bf16[16,512,1024]{2,1,0:T(8,128)(2,1)}), bf16[16,512,1024]{2,1,0:T(8,128)(2,1)}, u32[]{:S(2)}, u32[]{:S(2)}) async-start(bf16[16,512,1024]{2,1,0:T(8,128)(2,1)} %bitcast.7), calls=%async_computation.1 | async-start | bytes 33554432 | tf_op jit(solution)/shard_map/all_to_all | solution.py:179
  53.6 410.3 %reduce-scatter.2.cloned.1.call-start = ((), (), s32[]{:S(2)}) async-start(), calls=%async_computation.3 | async-start | bytes 18874368 | tf_op jit(solution)/shard_map/reduce_scatter | solution.py:185
Sparse Core Ops, SparseCore 0:
  364.6 99.2 reduce-scatter.1

commit v2 on v1

--- a/solution.py
+++ b/solution.py
@@ -12,7 +12,10 @@
 LANES = 256
 
 
-def _transform_kernel(slot_ref, empty_ref, tc_ref, w_ref, out_hbm, buf, zero, sems):
+def _transform_kernel(slot_ref, empty_ref, tc_ref, w_ref, *rest):
+    chunks = (len(rest) - 3)
+    outs, (buf, zero, sems) = rest[:chunks], rest[chunks:]
+    chunk_slots = outs[0].shape[0]
     step = pl.program_id(0)
     steps = pl.num_programs(0)
     per = tc_ref.shape[0]
@@ -26,22 +29,28 @@
     def _():
         zero[...] = jnp.zeros_like(zero)
 
-    def copies(at, parity):
+    def each_copy(at, parity, act):
         held = buf.at[parity]
-        out = [
-            pltpu.make_async_copy(held.at[j], out_hbm.at[slot_ref[at * per + j]], sems.at[parity, j])
-            for j in range(per)
-        ]
-        out += [
-            pltpu.make_async_copy(zero, out_hbm.at[empty_ref[at * epr + j]], sems.at[parity, per + j])
-            for j in range(epr)
-        ]
-        return out
+        for j in range(per + epr):
+            if j < per:
+                src, g = held.at[j], slot_ref[at * per + j]
+            else:
+                src, g = zero, empty_ref[at * epr + j - per]
+            chunk, local = g // chunk_slots, g % chunk_slots
+            for kk in range(chunks):
+                @pl.when(chunk == kk)
+                def _():
+                    act(pltpu.make_async_copy(src, outs[kk].at[local], sems.at[parity, j]))
+
+    def start(cp):
+        cp.start()
+
+    def wait(cp):
+        cp.wait()
 
     @pl.when(step >= 2)
     def _():
-        for cp in copies(step - 2, step % 2):
-            cp.wait()
+        each_copy(step - 2, step % 2, wait)
 
     pad = jnp.zeros((half, half), w_ref.dtype)
     for j in range(per):
@@ -55,18 +64,15 @@
         for g in range(groups):
             side[j, :, g * LANES:(g + 1) * LANES] = y[g * rows:(g + 1) * rows]
 
-    for cp in copies(step, step % 2):
-        cp.start()
+    each_copy(step, step % 2, start)
 
     @pl.when(step == steps - 1)
     def _():
-        for cp in copies(step - 1, (step + 1) % 2):
-            cp.wait()
-        for cp in copies(step, step % 2):
-            cp.wait()
-
-
-def transform_into_slots(three_center, coefficients, buffer_slot, empty_slot, slot_count):
+        each_copy(step - 1, (step + 1) % 2, wait)
+        each_copy(step, step % 2, wait)
+
+
+def transform_into_slots(three_center, coefficients, buffer_slot, empty_slot, slot_count, chunks):
     pair_count, rows, width = three_center.shape
     tile = coefficients.shape[1]
     empty_count = empty_slot.shape[0]
@@ -89,7 +95,7 @@
             pl.BlockSpec((per, rows, width), lambda i, s, e: (i, 0, 0)),
             pl.BlockSpec((per, 2 * tile, 2 * tile), lambda i, s, e: (i, 0, 0)),
         ],
-        out_specs=pl.BlockSpec(memory_space=pl.ANY),
+        out_specs=[pl.BlockSpec(memory_space=pl.ANY)] * chunks,
         scratch_shapes=[
             pltpu.VMEM((2, per, rows, width), three_center.dtype),
             pltpu.VMEM((rows, width), three_center.dtype),
@@ -97,10 +103,11 @@
         ],
     )
     block_bytes = rows * width * 2
+    chunk_shape = jax.ShapeDtypeStruct((slot_count // chunks, rows, width), three_center.dtype)
     return pl.pallas_call(
         _transform_kernel,
         grid_spec=grid_spec,
-        out_shape=jax.ShapeDtypeStruct((slot_count, rows, width), three_center.dtype),
+        out_shape=[chunk_shape] * chunks,
         compiler_params=pltpu.CompilerParams(dimension_semantics=("arbitrary",)),
         cost_estimate=pl.CostEstimate(
             flops=2 * pair_count * rows * width * 4 * tile,
@@ -168,22 +175,26 @@
     )
     pair_ids = jnp.arange(pair_count, dtype=jnp.int32)
     earlier = (target[:, None] == target[None, :]) & (pair_ids[:, None] > pair_ids[None, :])
-    buffer_slot = jnp.take(position, target) * CAP + jnp.sum(earlier.astype(jnp.int32), axis=1)
+    rank = jnp.sum(earlier.astype(jnp.int32), axis=1)
+    pos = jnp.take(position, target)
+    buffer_slot = ((pos % owned_tiles) * occ_count + pos // owned_tiles) * CAP + rank
     labels = jnp.full((slot_count,), -1, jnp.int32).at[buffer_slot].set(domain_slot)
     empty_count = slot_count - pair_count
     empty_slot = jnp.nonzero(labels < 0, size=empty_count, fill_value=0)[0].astype(jnp.int32)
-    labels = labels.reshape(occ_count, owned_tiles * CAP)
-
-    buffer = transform_into_slots(three_center, coefficients, buffer_slot, empty_slot, slot_count)
-    buffer = buffer.reshape(occ_count, owned_tiles * CAP * tile_width, col_width)
-    received = lax.all_to_all(buffer, "occ", split_axis=0, concat_axis=0, tiled=True)
+    labels = labels.reshape(owned_tiles, occ_count, CAP).transpose(1, 0, 2)
     received_labels = lax.all_to_all(labels, "occ", split_axis=0, concat_axis=0, tiled=True)
-    received = received.reshape(occ_count, owned_tiles * CAP, tile_width, col_width)
-
-    partial_gram = domain_gram(received, received_labels, DOM)
-    domain_rows = partial_gram.shape[0]
-    summed = lax.psum_scatter(partial_gram, "aux", scatter_dimension=0, tiled=True)
-    return summed.reshape(summed.shape[0], owned_tiles, domain_rows)
+
+    buffers = transform_into_slots(
+        three_center, coefficients, buffer_slot, empty_slot, slot_count, owned_tiles
+    )
+    pieces = []
+    for k in range(owned_tiles):
+        buffer = buffers[k].reshape(occ_count, CAP * tile_width, col_width)
+        received = lax.all_to_all(buffer, "occ", split_axis=0, concat_axis=0, tiled=True)
+        received = received.reshape(occ_count, CAP, tile_width, col_width)
+        partial_gram = domain_gram(received, received_labels[:, k], DOM)
+        pieces.append(lax.psum_scatter(partial_gram, "aux", scatter_dimension=0, tiled=True))
+    return jnp.stack(pieces, axis=1)
 
 
 def solution(mesh):

time: 475 us -> 369 us (0.78)
  waiting for transfers between devices: 390 us -> 243 us
  starting transfers between devices: 15.3 us -> 39 us
  Pallas kernels: 34.5 us -> 49 us
    all_to_all x1 -> x4, waiting for transfers between devices: 290 us -> 205 us  [per_device(): lax.all_to_all(buffer, 'occ', split_axis=0, concat_axis=0, tiled=True)]
    reduce_scatter x1 -> x4, waiting for transfers between devices: 99.5 us -> 38 us  [per_device(): lax.psum_scatter(partial_gram, 'aux', scatter_dimension=0, tiled=True)]
    all_to_all x1 -> x4, starting transfers between devices: 7.32 us -> 30.8 us  [per_device(): lax.all_to_all(buffer, 'occ', split_axis=0, concat_axis=0, tiled=True)]
    pallas_call x1 -> x4, Pallas kernels: 18.8 us -> 32.7 us  [domain_gram(): pl.pallas_call(_gram_kernel, grid_spec=grid_spec, out_shape=jax.ShapeDtyp...]
    another operation x1 -> x6, local copies, waits for them, and re-layouts: 0.09 us -> 5.16 us  [the longest x1 2.67 us: per_device(): return jnp.stack(pieces, axis=1)]
  transfers between devices with their start and end apart: 3 -> 9, of which waited for: 2 -> 5; matrix products, arithmetic and copies ran while one was open for 2% -> 4% of each run, Pallas kernels for 3% -> 11%
where the time goes in v2:
time: 369 us; the launch traced here: 368 us
  waiting for transfers between devices  243 us (66%)
  Pallas kernels  49 us (13%)
  starting transfers between devices  39 us (11%)
  between operations  13.3 us (4%)
  local copies, waits for them, and re-layouts  13 us (4%)
  other arithmetic  11.1 us (3%)
    all_to_all x4, waiting for transfers between devices, per_device(): lax.all_to_all(buffer, 'occ', split_axis=0, concat_axis=0, tiled=True)  205 us
    reduce_scatter x4, waiting for transfers between devices, per_device(): lax.psum_scatter(partial_gram, 'aux', scatter_dimension=0, tiled=True)  38 us
    pallas_call x4, Pallas kernels, domain_gram(): pl.pallas_call(_gram_kernel, grid_spec=grid_spec, out_shape=jax.ShapeDtyp...  32.7 us
    all_to_all x4, starting transfers between devices, per_device(): lax.all_to_all(buffer, 'occ', split_axis=0, concat_axis=0, tiled=True)  30.8 us
    pallas_call x1, Pallas kernels, transform_into_slots(): pl.pallas_call(_transform_kernel, grid_spec=grid_spec, out_shape=[chunk_s...  16.3 us
    all_to_all x1, starting transfers between devices, per_device(): lax.all_to_all(labels, 'occ', split_axis=0, concat_axis=0, tiled=True)  7.99 us
  transfers between devices with their start and end apart: 9, of which 5 were waited for; matrix products, arithmetic and copies ran while one was open for 4% of the time, Pallas kernels for 11%

profile of v2, /device:TPU:0, one launch (start us, length us, event | category | flops | bytes accessed | tf_op | source)
XLA Modules:
  0.0 368.2 jit_solution(1931360842074282994)
XLA Ops:
  8.9 1.2 gather_fusion
  10.1 1.2 compare_select_fusion.1
  13.3 8.0 %all-to-all-start = ((s32[16,4,2]{1,2,0:T(2,128)}), s32[16,4,2]{1,2,0:T(2,128)S(1)}, u32[]{:S(2)}, u32[]{:S(2)}) async-start(s32[16,4,2]{1,2,0:T(2,128)} %copy.22), calls=%async_computation | async-start | bytes 32768 | tf_op jit(solution)/shard_map/all_to_all | solution.py:185
  22.4 1.4 scatter_custom_fusion.1
  24.1 3.3 copy.25
  27.4 2.2 fusion.2.w_ref
  29.6 1.2 compare_select_fusion.5.empty_ref
  30.7 16.3 %shard_map.55 = (bf16[32,64,1024]{2,1,0:T(8,128)(2,1)}, bf16[32,64,1024]{2,1,0:T(8,128)(2,1)}, bf16[32,64,1024]{2,1,0:T(8,128)(2,1)}, bf16[32,64,1024]{2,1,0:T(8,128)(2,1)}) custom-call(s32[96]{0:T(128)} %get-tuple-element.18.slot_ref, s32[32]{0:T(128)} %compare_select_fusion.5.empty_ref, bf16[96,64,1024]{2,1,0:T(8,128)(2,1)} %tc_ref.1, ...), custom_call_target="tpu_custom_call" | custom-call | flops 3221225472 | bytes 29360128 | tf_op jit(solution)/shard_map/pallas_call | solution.py:107
  47.1 7.3 %all-to-all-start.2 = ((bf16[16,128,1024]{2,1,0:T(8,128)(2,1)}), bf16[16,128,1024]{2,1,0:T(8,128)(2,1)}, u32[]{:S(2)}, u32[]{:S(2)}) async-start(bf16[16,128,1024]{2,1,0:T(8,128)(2,1)} %bitcast.20), calls=%async_computation.3 | async-start | bytes 8388608 | tf_op jit(solution)/shard_map/all_to_all | solution.py:193
  54.4 1.2 slice_reduce_fusion.3
  56.3 52.5 %all-to-all-done.2 = bf16[16,128,1024]{2,1,0:T(8,128)(2,1)} async-done(((bf16[16,128,1024]{2,1,0:T(8,128)(2,1)}), bf16[16,128,1024]{2,1,0:T(8,128)(2,1)}, u32[]{:S(2)}, u32[]{:S(2)}) %all-to-all-start.2) | async-done | bytes 4194336 | tf_op jit(solution)/shard_map/all_to_all | solution.py:193
  108.8 8.0 %shard_map.57 = f32[1024,1024]{1,0:T(8,128)} custom-call(s32[32]{0:T(128)} %reshape_squeeze.13.lab_ref, bf16[16,2,64,1024]{3,2,1,0:T(8,128)(2,1)} %bitcast.7.x_ref), custom_call_target="tpu_custom_call" | custom-call | flops 2147483648 | bytes 8388608 | tf_op jit(solution)/shard_map/pallas_call | solution.py:151
  116.8 11.6 %all-to-all-start.1 = ((bf16[16,128,1024]{2,1,0:T(8,128)(2,1)}), bf16[16,128,1024]{2,1,0:T(8,128)(2,1)}, u32[]{:S(2)}, u32[]{:S(2)}) async-start(bf16[16,128,1024]{2,1,0:T(8,128)(2,1)} %bitcast.19), calls=%async_computation.1 | async-start | bytes 8388608 | tf_op jit(solution)/shard_map/all_to_all | solution.py:193
  129.0 52.7 %all-to-all-done.1 = bf16[16,128,1024]{2,1,0:T(8,128)(2,1)} async-done(((bf16[16,128,1024]{2,1,0:T(8,128)(2,1)}), bf16[16,128,1024]{2,1,0:T(8,128)(2,1)}, u32[]{:S(2)}, u32[]{:S(2)}) %all-to-all-start.1) | async-done | bytes 4194336 | tf_op jit(solution)/shard_map/all_to_all | solution.py:193
  181.8 8.4 %shard_map.56 = f32[1024,1024]{1,0:T(8,128)} custom-call(s32[32]{0:T(128)} %reshape_squeeze.12.lab_ref, bf16[16,2,64,1024]{3,2,1,0:T(8,128)(2,1)} %bitcast.4.x_ref), custom_call_target="tpu_custom_call" | custom-call | flops 2147483648 | bytes 8388608 | tf_op jit(solution)/shard_map/pallas_call | solution.py:151
  190.2 4.5 %all-to-all-start.3 = ((bf16[16,128,1024]{2,1,0:T(8,128)(2,1)}), bf16[16,128,1024]{2,1,0:T(8,128)(2,1)}, u32[]{:S(2)}, u32[]{:S(2)}) async-start(bf16[16,128,1024]{2,1,0:T(8,128)(2,1)} %bitcast.18), calls=%async_computation.5 | async-start | bytes 8388608 | tf_op jit(solution)/shard_map/all_to_all | solution.py:193
  195.4 48.8 %all-to-all-done.3 = bf16[16,128,1024]{2,1,0:T(8,128)(2,1)} async-done(((bf16[16,128,1024]{2,1,0:T(8,128)(2,1)}), bf16[16,128,1024]{2,1,0:T(8,128)(2,1)}, u32[]{:S(2)}, u32[]{:S(2)}) %all-to-all-start.3) | async-done | bytes 4194336 | tf_op jit(solution)/shard_map/all_to_all | solution.py:193
  244.1 8.1 %shard_map.58 = f32[1024,1024]{1,0:T(8,128)} custom-call(s32[32]{0:T(128)} %reshape_squeeze.14.lab_ref, bf16[16,2,64,1024]{3,2,1,0:T(8,128)(2,1)} %bitcast.10.x_ref), custom_call_target="tpu_custom_call" | custom-call | flops 2147483648 | bytes 8388608 | tf_op jit(solution)/shard_map/pallas_call | solution.py:151
  252.3 7.4 %all-to-all-start.4 = ((bf16[16,128,1024]{2,1,0:T(8,128)(2,1)}), bf16[16,128,1024]{2,1,0:T(8,128)(2,1)}, u32[]{:S(2)}, u32[]{:S(2)}) async-start(bf16[16,128,1024]{2,1,0:T(8,128)(2,1)} %bitcast.17), calls=%async_computation.7 | async-start | bytes 8388608 | tf_op jit(solution)/shard_map/all_to_all | solution.py:193
  260.4 50.7 %all-to-all-done.4 = bf16[16,128,1024]{2,1,0:T(8,128)(2,1)} async-done(((bf16[16,128,1024]{2,1,0:T(8,128)(2,1)}), bf16[16,128,1024]{2,1,0:T(8,128)(2,1)}, u32[]{:S(2)}, u32[]{:S(2)}) %all-to-all-start.4) | async-done | bytes 4194336 | tf_op jit(solution)/shard_map/all_to_all | solution.py:193
  311.1 8.2 %shard_map.59 = f32[1024,1024]{1,0:T(8,128)} custom-call(s32[32]{0:T(128)} %reshape_squeeze.15.lab_ref, bf16[16,2,64,1024]{3,2,1,0:T(8,128)(2,1)} %bitcast.13.x_ref), custom_call_target="tpu_custom_call" | custom-call | flops 2147483648 | bytes 8388608 | tf_op jit(solution)/shard_map/pallas_call | solution.py:151
  319.4 37.9 %reduce-scatter.11.cloned.1.call-done = f32[128,1024]{1,0:T(8,128)} async-done(((f32[1024,1024]{1,0:T(8,128)}), f32[128,1024]{1,0:T(8,128)}) %reduce-scatter.11.cloned.1.call-update) | async-done | bytes 524304 | tf_op jit(solution)/shard_map/reduce_scatter | solution.py:196
  357.4 1.7 pad_maximum_fusion
  359.0 2.7 copy.27
  (32 shorter events, 8.3 us)
Async XLA Ops:
  13.3 33.8 %all-to-all-start = ((s32[16,4,2]{1,2,0:T(2,128)}), s32[16,4,2]{1,2,0:T(2,128)S(1)}, u32[]{:S(2)}, u32[]{:S(2)}) async-start(s32[16,4,2]{1,2,0:T(2,128)} %copy.22), calls=%async_computation | async-start | bytes 32768 | tf_op jit(solution)/shard_map/all_to_all | solution.py:185
  47.1 61.7 %all-to-all-start.2 = ((bf16[16,128,1024]{2,1,0:T(8,128)(2,1)}), bf16[16,128,1024]{2,1,0:T(8,128)(2,1)}, u32[]{:S(2)}, u32[]{:S(2)}) async-start(bf16[16,128,1024]{2,1,0:T(8,128)(2,1)} %bitcast.20), calls=%async_computation.3 | async-start | bytes 8388608 | tf_op jit(solution)/shard_map/all_to_all | solution.py:193
  54.4 265.0 %reduce-scatter.7.cloned.1.call-start = ((), (), s32[]{:S(2)}) async-start(), calls=%async_computation.10 | async-start | bytes 4718592 | tf_op jit(solution)/shard_map/reduce_scatter | solution.py:196
  116.8 64.9 %all-to-all-start.1 = ((bf16[16,128,1024]{2,1,0:T(8,128)(2,1)}), bf16[16,128,1024]{2,1,0:T(8,128)(2,1)}, u32[]{:S(2)}, u32[]{:S(2)}) async-start(bf16[16,128,1024]{2,1,0:T(8,128)(2,1)} %bitcast.19), calls=%async_computation.1 | async-start | bytes 8388608 | tf_op jit(solution)/shard_map/all_to_all | solution.py:193
  128.4 191.0 %reduce-scatter.5.cloned.1.call-start = ((), (), s32[]{:S(2)}) async-start(), calls=%async_computation.9 | async-start | bytes 4718592 | tf_op jit(solution)/shard_map/reduce_scatter | solution.py:196
  190.2 54.0 %all-to-all-start.3 = ((bf16[16,128,1024]{2,1,0:T(8,128)(2,1)}), bf16[16,128,1024]{2,1,0:T(8,128)(2,1)}, u32[]{:S(2)}, u32[]{:S(2)}) async-start(bf16[16,128,1024]{2,1,0:T(8,128)(2,1)} %bitcast.18), calls=%async_computation.5 | async-start | bytes 8388608 | tf_op jit(solution)/shard_map/all_to_all | solution.py:193
  194.7 124.7 %reduce-scatter.9.cloned.1.call-start = ((), (), s32[]{:S(2)}) async-start(), calls=%async_computation.11 | async-start | bytes 4718592 | tf_op jit(solution)/shard_map/reduce_scatter | solution.py:196
  252.3 58.8 %all-to-all-start.4 = ((bf16[16,128,1024]{2,1,0:T(8,128)(2,1)}), bf16[16,128,1024]{2,1,0:T(8,128)(2,1)}, u32[]{:S(2)}, u32[]{:S(2)}) async-start(bf16[16,128,1024]{2,1,0:T(8,128)(2,1)} %bitcast.17), calls=%async_computation.7 | async-start | bytes 8388608 | tf_op jit(solution)/shard_map/all_to_all | solution.py:193
  259.7 97.6 %reduce-scatter.11.cloned.1.call-start = ((), (), s32[]{:S(2)}) async-start(), calls=%async_computation.12 | async-start | bytes 4718592 | tf_op jit(solution)/shard_map/reduce_scatter | solution.py:196
Sparse Core Ops, SparseCore 0:
  116.9 44.9 reduce-scatter.6
  190.3 37.5 reduce-scatter.4
  252.4 40.7 reduce-scatter.8
  319.5 37.8 reduce-scatter.10

commit v3 on v2

v3 whole, which is shorter than its diff:
```python
import math

import jax
import jax.numpy as jnp
from jax import lax
from jax.experimental import pallas as pl
from jax.experimental.pallas import tpu as pltpu
from jax.sharding import PartitionSpec as P

DOM = 16
CAP = 2
LANES = 256


def _transform_kernel(out_ref, slot_ref, tc_ref, w_ref, *rest):
    chunks = len(rest) - 2
    outs, (buf, sems) = rest[:chunks], rest[chunks:]
    step = pl.program_id(0)
    steps = pl.num_programs(0)
    per = tc_ref.shape[0]
    rows, width = tc_ref.shape[1], tc_ref.shape[2]
    groups = width // LANES
    half = w_ref.shape[1]
    side = buf.at[step % 2]

    def each_copy(at, parity, act):
        held = buf.at[parity]
        for j in range(per):
            chunk, local = out_ref[at * per + j], slot_ref[at * per + j]
            for kk in range(chunks):
                @pl.when(chunk == kk)
                def _():
                    act(pltpu.make_async_copy(held.at[j], outs[kk].at[local], sems.at[parity, j]))

    def start(cp):
        cp.start()

    def wait(cp):
        cp.wait()

    @pl.when(step >= 2)
    def _():
        each_copy(step - 2, step % 2, wait)

    pad = jnp.zeros((half, half), w_ref.dtype)
    for j in range(per):
        w2 = w_ref[j]
        w4 = jnp.concatenate(
            [jnp.concatenate([w2, pad], axis=1), jnp.concatenate([pad, w2], axis=1)], axis=0
        )
        x = tc_ref[j]
        stacked = jnp.concatenate([x[:, g * LANES:(g + 1) * LANES] for g in range(groups)], axis=0)
        y = jnp.dot(stacked, w4, preferred_element_type=jnp.float32).astype(buf.dtype)
        for g in range(groups):
            side[j, :, g * LANES:(g + 1) * LANES] = y[g * rows:(g + 1) * rows]

    each_copy(step, step % 2, start)

    @pl.when(step == steps - 1)
    def _():
        each_copy(step - 1, (step + 1) % 2, wait)
        each_copy(step, step % 2, wait)


def transform_into_slots(three_center, coefficients, out_index, slot_index, group_slots):
    pair_count, rows, width = three_center.shape
    tile = coefficients.shape[1]
    steps = 8 if pair_count % 8 == 0 else 1
    per = pair_count // steps
    zeros = jnp.zeros_like(coefficients)
    w2 = jnp.concatenate(
        [
            jnp.concatenate([coefficients, zeros], axis=2),
            jnp.concatenate([zeros, coefficients], axis=2),
        ],
        axis=1,
    )
    grid_spec = pltpu.PrefetchScalarGridSpec(
        num_scalar_prefetch=2,
        grid=(steps,),
        in_specs=[
            pl.BlockSpec((per, rows, width), lambda i, o, s: (i, 0, 0)),
            pl.BlockSpec((per, 2 * tile, 2 * tile), lambda i, o, s: (i, 0, 0)),
        ],
        out_specs=[pl.BlockSpec(memory_space=pl.ANY)] * len(group_slots),
        scratch_shapes=[
            pltpu.VMEM((2, per, rows, width), three_center.dtype),
            pltpu.SemaphoreType.DMA((2, per)),
        ],
    )
    block_bytes = rows * width * 2
    return pl.pallas_call(
        _transform_kernel,
        grid_spec=grid_spec,
        out_shape=[jax.ShapeDtypeStruct((n, rows, width), three_center.dtype) for n in group_slots],
        compiler_params=pltpu.CompilerParams(dimension_semantics=("arbitrary",)),
        cost_estimate=pl.CostEstimate(
            flops=2 * pair_count * rows * width * 4 * tile,
            transcendentals=0,
            bytes_accessed=2 * pair_count * block_bytes,
        ),
    )(out_index, slot_index, three_center, w2)


def _gram_kernel(lab_ref, x_ref, o_ref, acc, fitted_t):
    step = pl.program_id(0)
    sources, cap = x_ref.shape[0], x_ref.shape[1]
    dom, rows, width = acc.shape
    block = o_ref.shape[0]

    @pl.when(step == 0)
    def _():
        acc[...] = jnp.zeros_like(acc)
        for s in range(sources):
            for c in range(cap):
                e = lab_ref[s * cap + c]

                @pl.when(e >= 0)
                def _():
                    acc[e] += x_ref[s, c].astype(jnp.float32)

        fitted = acc[...].astype(x_ref.dtype).reshape(dom * rows, width)
        fitted_t[...] = fitted.T

    start = pl.multiple_of(step * block, block)
    lhs = acc[pl.ds(pl.multiple_of(step * (block // rows), block // rows), block // rows)]
    lhs = lhs.astype(x_ref.dtype).reshape(block, width)
    o_ref[...] = jnp.dot(lhs, fitted_t[...], preferred_element_type=jnp.float32)


def domain_gram(received, which, labels, dom, row_steps=4):
    sources, slots, rows, width = received.shape
    cap = CAP
    domain_rows = dom * rows
    block = domain_rows // row_steps
    grid_spec = pltpu.PrefetchScalarGridSpec(
        num_scalar_prefetch=1,
        grid=(row_steps,),
        in_specs=[pl.BlockSpec((sources, cap, rows, width), lambda i, lab: (0, which, 0, 0))],
        out_specs=pl.BlockSpec((block, domain_rows), lambda i, lab: (i, 0)),
        scratch_shapes=[
            pltpu.VMEM((dom, rows, width), jnp.float32),
            pltpu.VMEM((width, domain_rows), received.dtype),
        ],
    )
    return pl.pallas_call(
        _gram_kernel,
        grid_spec=grid_spec,
        out_shape=jax.ShapeDtypeStruct((domain_rows, domain_rows), jnp.float32),
        compiler_params=pltpu.CompilerParams(
            dimension_semantics=("arbitrary",), vmem_limit_bytes=60 * 1024 * 1024
        ),
        cost_estimate=pl.CostEstimate(
            flops=2 * domain_rows * domain_rows * width,
            transcendentals=0,
            bytes_accessed=sources * cap * rows * width * 2 + domain_rows * domain_rows * 4,
        ),
    )(labels.reshape(-1), received)


def per_device(three_center, coefficients, target, domain_slot, owner_order):
    pair_count, tile_width, col_width = three_center.shape
    occ_count = lax.axis_size("occ")
    tile_count = owner_order.shape[0]
    owned_tiles = tile_count // occ_count
    slot_count = tile_count * CAP
    tile_ids = jnp.arange(tile_count, dtype=jnp.int32)
    position = jnp.sum(
        jnp.where(owner_order[None, :] == tile_ids[:, None], tile_ids[None, :], 0), axis=1
    )
    pair_ids = jnp.arange(pair_count, dtype=jnp.int32)
    earlier = (target[:, None] == target[None, :]) & (pair_ids[:, None] > pair_ids[None, :])
    rank = jnp.sum(earlier.astype(jnp.int32), axis=1)
    pos = jnp.take(position, target)
    groups = [[0, 1]] + [[k] for k in range(2, owned_tiles)] if owned_tiles > 2 else [[k] for k in range(owned_tiles)]
    group_of = [g for g, group in enumerate(groups) for k in group]
    place_of = [i for group in groups for i, k in enumerate(group)]
    size_of = [len(groups[g]) for g in group_of]
    k_local = pos % owned_tiles
    out_index = jnp.take(jnp.array(group_of, jnp.int32), k_local)
    slot_index = ((pos // owned_tiles) * jnp.take(jnp.array(size_of, jnp.int32), k_local)
                  + jnp.take(jnp.array(place_of, jnp.int32), k_local)) * CAP + rank
    tile_slot = (k_local * occ_count + pos // owned_tiles) * CAP + rank
    labels = jnp.full((slot_count,), -1, jnp.int32).at[tile_slot].set(domain_slot)
    labels = labels.reshape(owned_tiles, occ_count, CAP).transpose(1, 0, 2)
    received_labels = lax.all_to_all(labels, "occ", split_axis=0, concat_axis=0, tiled=True)

    buffers = transform_into_slots(
        three_center, coefficients, out_index, slot_index,
        [occ_count * len(group) * CAP for group in groups],
    )
    pieces = []
    held = ()
    for g, group in enumerate(groups):
        buffer = buffers[g].reshape(occ_count, len(group) * CAP * tile_width, col_width)
        buffer, held = lax.optimization_barrier((buffer, held))
        received = lax.all_to_all(buffer, "occ", split_axis=0, concat_axis=0, tiled=True)
        received = received.reshape(occ_count, len(group) * CAP, tile_width, col_width)
        grams = [domain_gram(received, i, received_labels[:, k], DOM) for i, k in enumerate(group)]
        pieces += [lax.psum_scatter(gm, "aux", scatter_dimension=0, tiled=True) for gm in grams]
        held = tuple(grams)
    return jnp.stack(pieces, axis=1)


def solution(mesh):
    in_specs = (P("occ", None, "aux"), P("occ", None, None), P("occ"), P("occ"), P())
    out_specs = P("aux", "occ", None)
    return jax.shard_map(
        per_device, mesh=mesh, in_specs=in_specs, out_specs=out_specs, check_vma=False
    )
```

time: 369 us -> 393 us (1.065)
  waiting for transfers between devices: 243 us -> 278 us
  starting transfers between devices: 39 us -> 31.4 us
    all_to_all x4 -> x3, waiting for transfers between devices: 205 us -> 240 us  [per_device(): lax.all_to_all(buffer, 'occ', split_axis=0, concat_axis=0, tiled=True)]
    all_to_all x4 -> x3, starting transfers between devices: 30.8 us -> 23.1 us  [per_device(): lax.all_to_all(buffer, 'occ', split_axis=0, concat_axis=0, tiled=True)]
  transfers between devices with their start and end apart: 9 -> 8, of which waited for: 5 -> 4; matrix products, arithmetic and copies ran while one was open for 4% -> 2% of each run, Pallas kernels for 11% -> 10%
where the time goes in v3:
time: 393 us; the launch traced here: 392 us
  waiting for transfers between devices  278 us (71%)
  Pallas kernels  49.1 us (12%)
  starting transfers between devices  31.4 us (8%)
  between operations  13.3 us (3%)
  local copies, waits for them, and re-layouts  12.8 us (3%)
  other arithmetic  8.06 us (2%)
    all_to_all x3, waiting for transfers between devices, per_device(): lax.all_to_all(buffer, 'occ', split_axis=0, concat_axis=0, tiled=True)  240 us
    reduce_scatter x4, waiting for transfers between devices, per_device(): lax.psum_scatter(gm, 'aux', scatter_dimension=0, tiled=True)  37.9 us
    pallas_call x4, Pallas kernels, domain_gram(): pl.pallas_call(_gram_kernel, grid_spec=grid_spec, out_shape=jax.ShapeDtyp...  34.6 us
    all_to_all x3, starting transfers between devices, per_device(): lax.all_to_all(buffer, 'occ', split_axis=0, concat_axis=0, tiled=True)  23.1 us
    pallas_call x1, Pallas kernels, transform_into_slots(): pl.pallas_call(_transform_kernel, grid_spec=grid_spec, out_shape=[jax.Sha...  14.5 us
    all_to_all x1, starting transfers between devices, per_device(): lax.all_to_all(labels, 'occ', split_axis=0, concat_axis=0, tiled=True)  7.99 us
  transfers between devices with their start and end apart: 8, of which 4 were waited for; matrix products, arithmetic and copies ran while one was open for 2% of the time, Pallas kernels for 10%

profile of v3, /device:TPU:0, one launch (start us, length us, event | category | flops | bytes accessed | tf_op | source)
XLA Modules:
  0.0 392.4 jit_solution(6127847270032630393)
XLA Ops:
  6.5 0.9 convert_reduce_fusion
  8.1 0.8 select_reduce_fusion
  8.9 1.2 gather_fusion
  10.1 1.2 fusion.7
  11.9 1.0 scatter_custom_fusion
  13.1 0.8 copy.19
  13.9 8.0 %all-to-all-start = ((s32[16,4,2]{1,2,0:T(2,128)}), s32[16,4,2]{1,2,0:T(2,128)S(1)}, u32[]{:S(2)}, u32[]{:S(2)}) async-start(s32[16,4,2]{1,2,0:T(2,128)} %copy.19), calls=%async_computation | async-start | bytes 32768 | tf_op jit(solution)/shard_map/all_to_all | solution.py:186
  21.9 3.3 copy.20
  25.2 2.3 fusion.2.w_ref
  27.5 14.5 %shard_map.82 = (bf16[64,64,1024]{2,1,0:T(8,128)(2,1)}, bf16[32,64,1024]{2,1,0:T(8,128)(2,1)}, bf16[32,64,1024]{2,1,0:T(8,128)(2,1)}) custom-call(s32[96]{0:T(128)} %get-tuple-element.23.out_ref, s32[96]{0:T(128)} %get-tuple-element.20.slot_ref, bf16[96,64,1024]{2,1,0:T(8,128)(2,1)} %tc_ref.1, bf16[96,128,128]{2,1,0:T(8,128)(2,1)} %fusion.2.w_ref), custom_call_target="tpu_custom_call" | custom-call | flops 3221225472 | bytes 25165824 | tf_op jit(solution)/shard_map/pallas_call | solution.py:92
  41.9 7.3 %all-to-all-start.1 = ((bf16[16,256,1024]{2,1,0:T(8,128)(2,1)}), bf16[16,256,1024]{2,1,0:T(8,128)(2,1)}, u32[]{:S(2)}, u32[]{:S(2)}) async-start(bf16[16,256,1024]{2,1,0:T(8,128)(2,1)} %bitcast.12), calls=%async_computation.1 | async-start | bytes 16777216 | tf_op jit(solution)/shard_map/all_to_all | solution.py:197
  49.3 1.2 slice_reduce_fusion.2
  51.1 138.7 %all-to-all-done.1 = bf16[16,256,1024]{2,1,0:T(8,128)(2,1)} async-done(((bf16[16,256,1024]{2,1,0:T(8,128)(2,1)}), bf16[16,256,1024]{2,1,0:T(8,128)(2,1)}, u32[]{:S(2)}, u32[]{:S(2)}) %all-to-all-start.1) | async-done | bytes 8388640 | tf_op jit(solution)/shard_map/all_to_all | solution.py:197
  189.8 8.7 %shard_map.83 = f32[1024,1024]{1,0:T(8,128)} custom-call(s32[32]{0:T(128)} %reshape_squeeze.12.lab_ref, bf16[16,4,64,1024]{3,2,1,0:T(8,128)(2,1)} %bitcast.2.x_ref), custom_call_target="tpu_custom_call" | custom-call | flops 2147483648 | bytes 8388608 | tf_op jit(solution)/shard_map/pallas_call | solution.py:146
  199.2 8.6 %shard_map.84 = f32[1024,1024]{1,0:T(8,128)} custom-call(s32[32]{0:T(128)} %reshape_squeeze.13.lab_ref, bf16[16,4,64,1024]{3,2,1,0:T(8,128)(2,1)} %bitcast.2.x_ref), custom_call_target="tpu_custom_call" | custom-call | flops 2147483648 | bytes 8388608 | tf_op jit(solution)/shard_map/pallas_call | solution.py:146
  207.8 10.1 %all-to-all-start.2 = ((bf16[16,128,1024]{2,1,0:T(8,128)(2,1)}), bf16[16,128,1024]{2,1,0:T(8,128)(2,1)}, u32[]{:S(2)}, u32[]{:S(2)}) async-start(bf16[16,128,1024]{2,1,0:T(8,128)(2,1)} %bitcast.14), calls=%async_computation.4 | async-start | bytes 8388608 | tf_op jit(solution)/shard_map/all_to_all | solution.py:197
  218.6 50.2 %all-to-all-done.2 = bf16[16,128,1024]{2,1,0:T(8,128)(2,1)} async-done(((bf16[16,128,1024]{2,1,0:T(8,128)(2,1)}), bf16[16,128,1024]{2,1,0:T(8,128)(2,1)}, u32[]{:S(2)}, u32[]{:S(2)}) %all-to-all-start.2) | async-done | bytes 4194336 | tf_op jit(solution)/shard_map/all_to_all | solution.py:197
  268.8 8.6 %shard_map.85 = f32[1024,1024]{1,0:T(8,128)} custom-call(s32[32]{0:T(128)} %reshape_squeeze.14.lab_ref, bf16[16,2,64,1024]{3,2,1,0:T(8,128)(2,1)} %bitcast.6.x_ref), custom_call_target="tpu_custom_call" | custom-call | flops 2147483648 | bytes 8388608 | tf_op jit(solution)/shard_map/pallas_call | solution.py:146
  277.5 5.7 %all-to-all-start.3 = ((bf16[16,128,1024]{2,1,0:T(8,128)(2,1)}), bf16[16,128,1024]{2,1,0:T(8,128)(2,1)}, u32[]{:S(2)}, u32[]{:S(2)}) async-start(bf16[16,128,1024]{2,1,0:T(8,128)(2,1)} %bitcast.13), calls=%async_computation.6 | async-start | bytes 8388608 | tf_op jit(solution)/shard_map/all_to_all | solution.py:197
  284.0 51.0 %all-to-all-done.3 = bf16[16,128,1024]{2,1,0:T(8,128)(2,1)} async-done(((bf16[16,128,1024]{2,1,0:T(8,128)(2,1)}), bf16[16,128,1024]{2,1,0:T(8,128)(2,1)}, u32[]{:S(2)}, u32[]{:S(2)}) %all-to-all-start.3) | async-done | bytes 4194336 | tf_op jit(solution)/shard_map/all_to_all | solution.py:197
  335.0 8.6 %shard_map.86 = f32[1024,1024]{1,0:T(8,128)} custom-call(s32[32]{0:T(128)} %reshape_squeeze.15.lab_ref, bf16[16,2,64,1024]{3,2,1,0:T(8,128)(2,1)} %bitcast.9.x_ref), custom_call_target="tpu_custom_call" | custom-call | flops 2147483648 | bytes 8388608 | tf_op jit(solution)/shard_map/pallas_call | solution.py:146
  343.8 37.8 %reduce-scatter.11.cloned.1.call-done = f32[128,1024]{1,0:T(8,128)} async-done(((f32[1024,1024]{1,0:T(8,128)}), f32[128,1024]{1,0:T(8,128)}) %reduce-scatter.11.cloned.1.call-update) | async-done | bytes 524304 | tf_op jit(solution)/shard_map/reduce_scatter | solution.py:200
  381.6 1.7 pad_maximum_fusion
  383.2 2.7 copy.22
  (20 shorter events, 4.3 us)
Async XLA Ops:
  13.9 28.1 %all-to-all-start = ((s32[16,4,2]{1,2,0:T(2,128)}), s32[16,4,2]{1,2,0:T(2,128)S(1)}, u32[]{:S(2)}, u32[]{:S(2)}) async-start(s32[16,4,2]{1,2,0:T(2,128)} %copy.19), calls=%async_computation | async-start | bytes 32768 | tf_op jit(solution)/shard_map/all_to_all | solution.py:186
  41.9 147.8 %all-to-all-start.1 = ((bf16[16,256,1024]{2,1,0:T(8,128)(2,1)}), bf16[16,256,1024]{2,1,0:T(8,128)(2,1)}, u32[]{:S(2)}, u32[]{:S(2)}) async-start(bf16[16,256,1024]{2,1,0:T(8,128)(2,1)} %bitcast.12), calls=%async_computation.1 | async-start | bytes 16777216 | tf_op jit(solution)/shard_map/all_to_all | solution.py:197
  49.2 294.5 %reduce-scatter.5.cloned.1.call-start = ((), (), s32[]{:S(2)}) async-start(), calls=%async_computation.8 | async-start | bytes 4718592 | tf_op jit(solution)/shard_map/reduce_scatter | solution.py:200
  198.5 145.2 %reduce-scatter.7.cloned.1.call-start = ((), (), s32[]{:S(2)}) async-start(), calls=%async_computation.9 | async-start | bytes 4718592 | tf_op jit(solution)/shard_map/reduce_scatter | solution.py:200
  207.8 61.0 %all-to-all-start.2 = ((bf16[16,128,1024]{2,1,0:T(8,128)(2,1)}), bf16[16,128,1024]{2,1,0:T(8,128)(2,1)}, u32[]{:S(2)}, u32[]{:S(2)}) async-start(bf16[16,128,1024]{2,1,0:T(8,128)(2,1)} %bitcast.14), calls=%async_computation.4 | async-start | bytes 8388608 | tf_op jit(solution)/shard_map/all_to_all | solution.py:197
  217.9 125.8 %reduce-scatter.9.cloned.1.call-start = ((), (), s32[]{:S(2)}) async-start(), calls=%async_computation.10 | async-start | bytes 4718592 | tf_op jit(solution)/shard_map/reduce_scatter | solution.py:200
  277.5 57.5 %all-to-all-start.3 = ((bf16[16,128,1024]{2,1,0:T(8,128)(2,1)}), bf16[16,128,1024]{2,1,0:T(8,128)(2,1)}, u32[]{:S(2)}, u32[]{:S(2)}) async-start(bf16[16,128,1024]{2,1,0:T(8,128)(2,1)} %bitcast.13), calls=%async_computation.6 | async-start | bytes 8388608 | tf_op jit(solution)/shard_map/all_to_all | solution.py:197
  283.2 98.4 %reduce-scatter.11.cloned.1.call-start = ((), (), s32[]{:S(2)}) async-start(), calls=%async_computation.11 | async-start | bytes 4718592 | tf_op jit(solution)/shard_map/reduce_scatter | solution.py:200
Sparse Core Ops, SparseCore 0:
  198.6 43.0 reduce-scatter.4
  244.2 37.4 reduce-scatter.6
  284.1 37.5 reduce-scatter.8
  343.8 37.7 reduce-scatter.10

commit v4 on v3

--- a/solution.py
+++ b/solution.py
@@ -1,3 +1,4 @@
+import functools
 import math
 
 import jax
@@ -102,65 +103,82 @@
     )(out_index, slot_index, three_center, w2)
 
 
-def _gram_kernel(lab_ref, x_ref, o_ref, acc, fitted_t):
-    step = pl.program_id(0)
+def _gram_kernel(lab_ref, x_ref, o_ref, acc, fs, ft2, *, row_blk):
     sources, cap = x_ref.shape[0], x_ref.shape[1]
     dom, rows, width = acc.shape
-    block = o_ref.shape[0]
-
-    @pl.when(step == 0)
-    def _():
-        acc[...] = jnp.zeros_like(acc)
-        for s in range(sources):
-            for c in range(cap):
-                e = lab_ref[s * cap + c]
-
-                @pl.when(e >= 0)
-                def _():
-                    acc[e] += x_ref[s, c].astype(jnp.float32)
-
-        fitted = acc[...].astype(x_ref.dtype).reshape(dom * rows, width)
-        fitted_t[...] = fitted.T
-
-    start = pl.multiple_of(step * block, block)
-    lhs = acc[pl.ds(pl.multiple_of(step * (block // rows), block // rows), block // rows)]
-    lhs = lhs.astype(x_ref.dtype).reshape(block, width)
-    o_ref[...] = jnp.dot(lhs, fitted_t[...], preferred_element_type=jnp.float32)
-
-
-def domain_gram(received, which, labels, dom, row_steps=4):
-    sources, slots, rows, width = received.shape
-    cap = CAP
-    domain_rows = dom * rows
-    block = domain_rows // row_steps
+    n = dom * rows
+    cols = o_ref.shape[1]
+    wrap = ft2.shape[1] - n
+    acc[...] = jnp.zeros_like(acc)
+    for s in range(sources):
+        for c in range(cap):
+            e = lab_ref[s * cap + c]
+
+            @pl.when(e >= 0)
+            def _():
+                acc[e] += x_ref[s, c].astype(jnp.float32)
+
+    fs[...] = acc[...].astype(fs.dtype).reshape(n, width)
+    ft = fs[...].T
+    ft2[:, :n] = ft
+    ft2[:, n:] = ft[:, :wrap]
+    for a in range(n // row_blk):
+        lhs = fs[a * row_blk:(a + 1) * row_blk, :]
+        o_ref[a * row_blk:(a + 1) * row_blk, :] = jnp.dot(
+            lhs, ft2[:, a * row_blk:a * row_blk + cols], preferred_element_type=jnp.float32
+        )
+
+
+def packed_gram(received, labels, dom, parts):
+    sources, cap, rows, width = received.shape
+    n = dom * rows
+    row_blk = n // parts
+    keep = parts // 2 + 1
+    cols = keep * row_blk
     grid_spec = pltpu.PrefetchScalarGridSpec(
         num_scalar_prefetch=1,
-        grid=(row_steps,),
-        in_specs=[pl.BlockSpec((sources, cap, rows, width), lambda i, lab: (0, which, 0, 0))],
-        out_specs=pl.BlockSpec((block, domain_rows), lambda i, lab: (i, 0)),
+        grid=(1,),
+        in_specs=[pl.BlockSpec((sources, cap, rows, width), lambda i, lab: (0, 0, 0, 0))],
+        out_specs=pl.BlockSpec((n, cols), lambda i, lab: (0, 0)),
         scratch_shapes=[
             pltpu.VMEM((dom, rows, width), jnp.float32),
-            pltpu.VMEM((width, domain_rows), received.dtype),
+            pltpu.VMEM((n, width), received.dtype),
+            pltpu.VMEM((width, n + cols - row_blk), received.dtype),
         ],
     )
     return pl.pallas_call(
-        _gram_kernel,
+        functools.partial(_gram_kernel, row_blk=row_blk),
         grid_spec=grid_spec,
-        out_shape=jax.ShapeDtypeStruct((domain_rows, domain_rows), jnp.float32),
+        out_shape=jax.ShapeDtypeStruct((n, cols), jnp.float32),
         compiler_params=pltpu.CompilerParams(
             dimension_semantics=("arbitrary",), vmem_limit_bytes=60 * 1024 * 1024
         ),
         cost_estimate=pl.CostEstimate(
-            flops=2 * domain_rows * domain_rows * width,
+            flops=2 * n * cols * width,
             transcendentals=0,
-            bytes_accessed=sources * cap * rows * width * 2 + domain_rows * domain_rows * 4,
+            bytes_accessed=sources * cap * rows * width * 2 + n * cols * 4,
         ),
     )(labels.reshape(-1), received)
+
+
+def unpack_rows(reduced, parts):
+    rows, cols = reduced.shape
+    blk = rows
+    keep = cols // blk
+    blocks = [reduced[:, j * blk:(j + 1) * blk] for j in range(keep)]
+    for p in range(keep, parts):
+        shift = parts - p
+        sent = reduced[:, shift * blk:(shift + 1) * blk]
+        got = lax.ppermute(sent, "aux", perm=[(i, (i + shift) % parts) for i in range(parts)])
+        blocks.append(got.T)
+    rotated = jnp.concatenate(blocks, axis=1)
+    return jnp.roll(rotated, lax.axis_index("aux") * blk, axis=1)
 
 
 def per_device(three_center, coefficients, target, domain_slot, owner_order):
     pair_count, tile_width, col_width = three_center.shape
     occ_count = lax.axis_size("occ")
+    aux_count = lax.axis_size("aux")
     tile_count = owner_order.shape[0]
     owned_tiles = tile_count // occ_count
     slot_count = tile_count * CAP
@@ -172,33 +190,23 @@
     earlier = (target[:, None] == target[None, :]) & (pair_ids[:, None] > pair_ids[None, :])
     rank = jnp.sum(earlier.astype(jnp.int32), axis=1)
     pos = jnp.take(position, target)
-    groups = [[0, 1]] + [[k] for k in range(2, owned_tiles)] if owned_tiles > 2 else [[k] for k in range(owned_tiles)]
-    group_of = [g for g, group in enumerate(groups) for k in group]
-    place_of = [i for group in groups for i, k in enumerate(group)]
-    size_of = [len(groups[g]) for g in group_of]
-    k_local = pos % owned_tiles
-    out_index = jnp.take(jnp.array(group_of, jnp.int32), k_local)
-    slot_index = ((pos // owned_tiles) * jnp.take(jnp.array(size_of, jnp.int32), k_local)
-                  + jnp.take(jnp.array(place_of, jnp.int32), k_local)) * CAP + rank
-    tile_slot = (k_local * occ_count + pos // owned_tiles) * CAP + rank
-    labels = jnp.full((slot_count,), -1, jnp.int32).at[tile_slot].set(domain_slot)
+    out_index = pos % owned_tiles
+    slot_index = (pos // owned_tiles) * CAP + rank
+    labels = jnp.full((slot_count,), -1, jnp.int32).at[out_index * occ_count * CAP + slot_index].set(domain_slot)
     labels = labels.reshape(owned_tiles, occ_count, CAP).transpose(1, 0, 2)
     received_labels = lax.all_to_all(labels, "occ", split_axis=0, concat_axis=0, tiled=True)
 
     buffers = transform_into_slots(
-        three_center, coefficients, out_index, slot_index,
-        [occ_count * len(group) * CAP for group in groups],
+        three_center, coefficients, out_index, slot_index, [occ_count * CAP] * owned_tiles
     )
     pieces = []
-    held = ()
-    for g, group in enumerate(groups):
-        buffer = buffers[g].reshape(occ_count, len(group) * CAP * tile_width, col_width)
-        buffer, held = lax.optimization_barrier((buffer, held))
+    for k in range(owned_tiles):
+        buffer = buffers[k].reshape(occ_count, CAP * tile_width, col_width)
         received = lax.all_to_all(buffer, "occ", split_axis=0, concat_axis=0, tiled=True)
-        received = received.reshape(occ_count, len(group) * CAP, tile_width, col_width)
-        grams = [domain_gram(received, i, received_labels[:, k], DOM) for i, k in enumerate(group)]
-        pieces += [lax.psum_scatter(gm, "aux", scatter_dimension=0, tiled=True) for gm in grams]
-        held = tuple(grams)
+        received = received.reshape(occ_count, CAP, tile_width, col_width)
+        packed = packed_gram(received, received_labels[:, k], DOM, aux_count)
+        reduced = lax.psum_scatter(packed, "aux", scatter_dimension=0, tiled=True)
+        pieces.append(unpack_rows(reduced, aux_count))
     return jnp.stack(pieces, axis=1)
 
 

time: 393 us -> 371 us (0.944)
  waiting for transfers between devices: 278 us -> 240 us
  starting transfers between devices: 31.4 us -> 46.9 us
  local copies, waits for them, and re-layouts: 12.8 us -> 17.7 us
  Pallas kernels: 49.1 us -> 44.6 us
    all_to_all x3 -> x4, waiting for transfers between devices: 240 us -> 205 us  [per_device(): lax.all_to_all(buffer, 'occ', split_axis=0, concat_axis=0, tiled=True)]
    reduce_scatter x4, waiting for transfers between devices: 37.9 us -> 27.6 us  [per_device(): reduced = lax.psum_scatter(packed, 'aux', scatter_dimension=0, tiled=True)]
    ppermute x0 -> x12, waiting for transfers between devices: none -> 7.84 us  [unpack_rows(): lax.ppermute(sent, 'aux', perm=[(i, (i + shift) % parts) for i in range(p...]
    all_to_all x3 -> x4, starting transfers between devices: 23.1 us -> 30.9 us  [per_device(): lax.all_to_all(buffer, 'occ', split_axis=0, concat_axis=0, tiled=True)]
    ppermute x0 -> x12, starting transfers between devices: none -> 7.81 us  [unpack_rows(): lax.ppermute(sent, 'aux', perm=[(i, (i + shift) % parts) for i in range(p...]
    pallas_call x4, Pallas kernels: 34.6 us -> 30.1 us  [packed_gram(): pl.pallas_call(functools.partial(_gram_kernel, row_blk=row_blk), grid_spe...]
  transfers between devices with their start and end apart: 8 -> 21, of which waited for: 4 -> 11; matrix products, arithmetic and copies ran while one was open for 2% -> 4% of each run, Pallas kernels for 10% -> 10%
where the time goes in v4:
time: 371 us; the launch traced here: 370 us
  waiting for transfers between devices  240 us (65%)
  starting transfers between devices  46.9 us (13%)
  Pallas kernels  44.6 us (12%)
  local copies, waits for them, and re-layouts  17.7 us (5%)
  between operations  13.5 us (4%)
  other arithmetic  7.12 us (2%)
    all_to_all x4, waiting for transfers between devices, per_device(): lax.all_to_all(buffer, 'occ', split_axis=0, concat_axis=0, tiled=True)  205 us
    all_to_all x4, starting transfers between devices, per_device(): lax.all_to_all(buffer, 'occ', split_axis=0, concat_axis=0, tiled=True)  30.9 us
    pallas_call x4, Pallas kernels, packed_gram(): pl.pallas_call(functools.partial(_gram_kernel, row_blk=row_blk), grid_spe...  30.1 us
    reduce_scatter x4, waiting for transfers between devices, per_device(): reduced = lax.psum_scatter(packed, 'aux', scatter_dimension=0, tiled=True)  27.6 us
    pallas_call x1, Pallas kernels, transform_into_slots(): pl.pallas_call(_transform_kernel, grid_spec=grid_spec, out_shape=[jax.Sha...  14.5 us
    all_to_all x1, starting transfers between devices, per_device(): lax.all_to_all(labels, 'occ', split_axis=0, concat_axis=0, tiled=True)  7.99 us
    ppermute x12, waiting for transfers between devices, unpack_rows(): lax.ppermute(sent, 'aux', perm=[(i, (i + shift) % parts) for i in range(p...  7.84 us
    ppermute x12, starting transfers between devices, unpack_rows(): lax.ppermute(sent, 'aux', perm=[(i, (i + shift) % parts) for i in range(p...  7.81 us
  transfers between devices with their start and end apart: 21, of which 11 were waited for; matrix products, arithmetic and copies ran while one was open for 4% of the time, Pallas kernels for 10%

profile of v4, /device:TPU:0, one launch (start us, length us, event | category | flops | bytes accessed | tf_op | source)
XLA Modules:
  0.0 370.3 jit_solution(6801649540924377511)
XLA Ops:
  13.3 8.0 %all-to-all-start = ((s32[16,4,2]{1,2,0:T(2,128)}), s32[16,4,2]{1,2,0:T(2,128)S(1)}, u32[]{:S(2)}, u32[]{:S(2)}) async-start(s32[16,4,2]{1,2,0:T(2,128)} %copy.51), calls=%async_computation | async-start | bytes 32768 | tf_op jit(solution)/shard_map/all_to_all | solution.py:197
  21.3 3.3 copy.52
  24.6 2.1 fusion.2.w_ref
  26.8 14.5 %shard_map.55 = (bf16[32,64,1024]{2,1,0:T(8,128)(2,1)}, bf16[32,64,1024]{2,1,0:T(8,128)(2,1)}, bf16[32,64,1024]{2,1,0:T(8,128)(2,1)}, bf16[32,64,1024]{2,1,0:T(8,128)(2,1)}) custom-call(s32[96]{0:T(128)} %get-tuple-element.19.out_ref, s32[96]{0:T(128)} %get-tuple-element.20.slot_ref, bf16[96,64,1024]{2,1,0:T(8,128)(2,1)} %tc_ref.1, ...), custom_call_target="tpu_custom_call" | custom-call | flops 3221225472 | bytes 25165824 | tf_op jit(solution)/shard_map/pallas_call | solution.py:93
  41.3 7.3 %all-to-all-start.1 = ((bf16[16,128,1024]{2,1,0:T(8,128)(2,1)}), bf16[16,128,1024]{2,1,0:T(8,128)(2,1)}, u32[]{:S(2)}, u32[]{:S(2)}) async-start(bf16[16,128,1024]{2,1,0:T(8,128)(2,1)} %bitcast.32), calls=%async_computation.1 | async-start | bytes 8388608 | tf_op jit(solution)/shard_map/all_to_all | solution.py:205
  50.5 52.5 %all-to-all-done.1 = bf16[16,128,1024]{2,1,0:T(8,128)(2,1)} async-done(((bf16[16,128,1024]{2,1,0:T(8,128)(2,1)}), bf16[16,128,1024]{2,1,0:T(8,128)(2,1)}, u32[]{:S(2)}, u32[]{:S(2)}) %all-to-all-start.1) | async-done | bytes 4194336 | tf_op jit(solution)/shard_map/all_to_all | solution.py:205
  103.0 7.7 %shard_map.56 = f32[1024,640]{1,0:T(8,128)} custom-call(s32[32]{0:T(128)} %reshape_squeeze.12.lab_ref, bf16[16,2,64,1024]{3,2,1,0:T(8,128)(2,1)} %bitcast.2.x_ref), custom_call_target="tpu_custom_call" | custom-call | flops 1342177280 | bytes 6815744 | tf_op jit(solution)/shard_map/pallas_call | solution.py:149
  110.7 11.3 %all-to-all-start.2 = ((bf16[16,128,1024]{2,1,0:T(8,128)(2,1)}), bf16[16,128,1024]{2,1,0:T(8,128)(2,1)}, u32[]{:S(2)}, u32[]{:S(2)}) async-start(bf16[16,128,1024]{2,1,0:T(8,128)(2,1)} %bitcast.31), calls=%async_computation.3 | async-start | bytes 8388608 | tf_op jit(solution)/shard_map/all_to_all | solution.py:205
  122.7 52.7 %all-to-all-done.2 = bf16[16,128,1024]{2,1,0:T(8,128)(2,1)} async-done(((bf16[16,128,1024]{2,1,0:T(8,128)(2,1)}), bf16[16,128,1024]{2,1,0:T(8,128)(2,1)}, u32[]{:S(2)}, u32[]{:S(2)}) %all-to-all-start.2) | async-done | bytes 4194336 | tf_op jit(solution)/shard_map/all_to_all | solution.py:205
  175.4 7.6 %shard_map.57 = f32[1024,640]{1,0:T(8,128)} custom-call(s32[32]{0:T(128)} %reshape_squeeze.13.lab_ref, bf16[16,2,64,1024]{3,2,1,0:T(8,128)(2,1)} %bitcast.8.x_ref), custom_call_target="tpu_custom_call" | custom-call | flops 1342177280 | bytes 6815744 | tf_op jit(solution)/shard_map/pallas_call | solution.py:149
  183.1 4.8 %all-to-all-start.3 = ((bf16[16,128,1024]{2,1,0:T(8,128)(2,1)}), bf16[16,128,1024]{2,1,0:T(8,128)(2,1)}, u32[]{:S(2)}, u32[]{:S(2)}) async-start(bf16[16,128,1024]{2,1,0:T(8,128)(2,1)} %bitcast.30), calls=%async_computation.5 | async-start | bytes 8388608 | tf_op jit(solution)/shard_map/all_to_all | solution.py:205
  188.5 48.4 %all-to-all-done.3 = bf16[16,128,1024]{2,1,0:T(8,128)(2,1)} async-done(((bf16[16,128,1024]{2,1,0:T(8,128)(2,1)}), bf16[16,128,1024]{2,1,0:T(8,128)(2,1)}, u32[]{:S(2)}, u32[]{:S(2)}) %all-to-all-start.3) | async-done | bytes 4194336 | tf_op jit(solution)/shard_map/all_to_all | solution.py:205
  236.8 7.3 %shard_map.58 = f32[1024,640]{1,0:T(8,128)} custom-call(s32[32]{0:T(128)} %reshape_squeeze.14.lab_ref, bf16[16,2,64,1024]{3,2,1,0:T(8,128)(2,1)} %bitcast.14.x_ref), custom_call_target="tpu_custom_call" | custom-call | flops 1342177280 | bytes 6815744 | tf_op jit(solution)/shard_map/pallas_call | solution.py:149
  244.2 7.5 %all-to-all-start.4 = ((bf16[16,128,1024]{2,1,0:T(8,128)(2,1)}), bf16[16,128,1024]{2,1,0:T(8,128)(2,1)}, u32[]{:S(2)}, u32[]{:S(2)}) async-start(bf16[16,128,1024]{2,1,0:T(8,128)(2,1)} %bitcast.29), calls=%async_computation.7 | async-start | bytes 8388608 | tf_op jit(solution)/shard_map/all_to_all | solution.py:205
  252.4 51.4 %all-to-all-done.4 = bf16[16,128,1024]{2,1,0:T(8,128)(2,1)} async-done(((bf16[16,128,1024]{2,1,0:T(8,128)(2,1)}), bf16[16,128,1024]{2,1,0:T(8,128)(2,1)}, u32[]{:S(2)}, u32[]{:S(2)}) %all-to-all-start.4) | async-done | bytes 4194336 | tf_op jit(solution)/shard_map/all_to_all | solution.py:205
  303.8 7.4 %shard_map.59 = f32[1024,640]{1,0:T(8,128)} custom-call(s32[32]{0:T(128)} %reshape_squeeze.15.lab_ref, bf16[16,2,64,1024]{3,2,1,0:T(8,128)(2,1)} %bitcast.20.x_ref), custom_call_target="tpu_custom_call" | custom-call | flops 1342177280 | bytes 6815744 | tf_op jit(solution)/shard_map/pallas_call | solution.py:149
  312.5 1.6 collective-permute-start.1
  314.3 2.1 collective-permute-start.2
  319.1 27.6 %reduce-scatter.11.cloned.1.call-done = f32[128,640]{1,0:T(8,128)} async-done(((f32[1024,640]{1,0:T(8,128)}), f32[128,640]{1,0:T(8,128)}) %reduce-scatter.11.cloned.1.call-update) | async-done | bytes 327696 | tf_op jit(solution)/shard_map/reduce_scatter | solution.py:208
  348.6 3.1 collective-permute-start.7
  352.1 2.3 collective-permute-done.3
  355.8 2.2 collective-permute-done.8
  358.3 2.1 collective-permute-done.10
  361.1 2.7 copy.66
  (73 shorter events, 19.2 us)
Async XLA Ops:
  13.3 28.0 %all-to-all-start = ((s32[16,4,2]{1,2,0:T(2,128)}), s32[16,4,2]{1,2,0:T(2,128)S(1)}, u32[]{:S(2)}, u32[]{:S(2)}) async-start(s32[16,4,2]{1,2,0:T(2,128)} %copy.51), calls=%async_computation | async-start | bytes 32768 | tf_op jit(solution)/shard_map/all_to_all | solution.py:197
  41.3 61.7 %all-to-all-start.1 = ((bf16[16,128,1024]{2,1,0:T(8,128)(2,1)}), bf16[16,128,1024]{2,1,0:T(8,128)(2,1)}, u32[]{:S(2)}, u32[]{:S(2)}) async-start(bf16[16,128,1024]{2,1,0:T(8,128)(2,1)} %bitcast.32), calls=%async_computation.1 | async-start | bytes 8388608 | tf_op jit(solution)/shard_map/all_to_all | solution.py:205
  48.6 262.7 %reduce-scatter.5.cloned.1.call-start = ((), (), s32[]{:S(2)}) async-start(), calls=%async_computation.9 | async-start | bytes 2949120 | tf_op jit(solution)/shard_map/reduce_scatter | solution.py:208
  110.7 64.7 %all-to-all-start.2 = ((bf16[16,128,1024]{2,1,0:T(8,128)(2,1)}), bf16[16,128,1024]{2,1,0:T(8,128)(2,1)}, u32[]{:S(2)}, u32[]{:S(2)}) async-start(bf16[16,128,1024]{2,1,0:T(8,128)(2,1)} %bitcast.31), calls=%async_computation.3 | async-start | bytes 8388608 | tf_op jit(solution)/shard_map/all_to_all | solution.py:205
  122.0 194.3 %reduce-scatter.7.cloned.1.call-start = ((), (), s32[]{:S(2)}) async-start(), calls=%async_computation.10 | async-start | bytes 2949120 | tf_op jit(solution)/shard_map/reduce_scatter | solution.py:208
  183.1 53.8 %all-to-all-start.3 = ((bf16[16,128,1024]{2,1,0:T(8,128)(2,1)}), bf16[16,128,1024]{2,1,0:T(8,128)(2,1)}, u32[]{:S(2)}, u32[]{:S(2)}) async-start(bf16[16,128,1024]{2,1,0:T(8,128)(2,1)} %bitcast.30), calls=%async_computation.5 | async-start | bytes 8388608 | tf_op jit(solution)/shard_map/all_to_all | solution.py:205
  187.8 130.3 %reduce-scatter.9.cloned.1.call-start = ((), (), s32[]{:S(2)}) async-start(), calls=%async_computation.11 | async-start | bytes 2949120 | tf_op jit(solution)/shard_map/reduce_scatter | solution.py:208
  244.2 59.6 %all-to-all-start.4 = ((bf16[16,128,1024]{2,1,0:T(8,128)(2,1)}), bf16[16,128,1024]{2,1,0:T(8,128)(2,1)}, u32[]{:S(2)}, u32[]{:S(2)}) async-start(bf16[16,128,1024]{2,1,0:T(8,128)(2,1)} %bitcast.29), calls=%async_computation.7 | async-start | bytes 8388608 | tf_op jit(solution)/shard_map/all_to_all | solution.py:205
  251.8 95.0 %reduce-scatter.11.cloned.1.call-start = ((), (), s32[]{:S(2)}) async-start(), calls=%async_computation.12 | async-start | bytes 2949120 | tf_op jit(solution)/shard_map/reduce_scatter | solution.py:208
  311.3 40.4 %copy-start.1 = (f32[128,640]{1,0:T(8,128)S(1)}, f32[128,640]{1,0:T(8,128)}, u32[]{:S(2)}) copy-start(f32[128,640]{1,0:T(8,128)} %reduce-scatter.5.cloned.1.call-done) | copy-start | bytes 983044
  312.3 36.0 %collective-permute-start = (f32[128,128]{0,1:T(8,128)S(1)}, f32[128,128]{0,1:T(8,128)S(1)}, u32[]{:S(2)}, u32[]{:S(2)}) collective-permute-start(f32[128,128]{0,1:T(8,128)S(1)} %copy.67), channel_id=1, source_target_pairs={{0,48},{16,64},{32,80},{48,96},{64,112},{80,0},{96,16},{112,32},{1... | collective-permute-start | bytes 196616 | tf_op jit(solution)/shard_map/ppermute | solution.py:172
  312.5 36.0 %collective-permute-start.1 = (f32[128,128]{0,1:T(8,128)S(1)}, f32[128,128]{0,1:T(8,128)S(1)}, u32[]{:S(2)}, u32[]{:S(2)}) collective-permute-start(f32[128,128]{0,1:T(8,128)S(1)} %copy.68), channel_id=1, source_target_pairs={{0,32},{16,48},{32,64},{48,80},{64,96},{80,112},{96,0},{112,16},{1... | collective-permute-start | bytes 196616 | tf_op jit(solution)/shard_map/ppermute | solution.py:172
  314.3 34.3 %collective-permute-start.2 = (f32[128,128]{0,1:T(8,128)S(1)}, f32[128,128]{0,1:T(8,128)S(1)}, u32[]{:S(2)}, u32[]{:S(2)}) collective-permute-start(f32[128,128]{0,1:T(8,128)S(1)} %copy.69), channel_id=1, source_target_pairs={{0,16},{16,32},{32,48},{48,64},{64,80},{80,96},{96,112},{112,0},{1... | collective-permute-start | bytes 196616 | tf_op jit(solution)/shard_map/ppermute | solution.py:172
  316.3 38.0 %copy-start = (f32[128,640]{1,0:T(8,128)S(1)}, f32[128,640]{1,0:T(8,128)}, u32[]{:S(2)}) copy-start(f32[128,640]{1,0:T(8,128)} %reduce-scatter.7.cloned.1.call-done) | copy-start | bytes 983044
  317.4 34.6 %collective-permute-start.4 = (f32[128,128]{0,1:T(8,128)S(1)}, f32[128,128]{0,1:T(8,128)S(1)}, u32[]{:S(2)}, u32[]{:S(2)}) collective-permute-start(f32[128,128]{0,1:T(8,128)S(1)} %copy.71), channel_id=1, source_target_pairs={{0,32},{16,48},{32,64},{48,80},{64,96},{80,112},{96,0},{112,16},{1... | collective-permute-start | bytes 196616 | tf_op jit(solution)/shard_map/ppermute | solution.py:172
  317.9 34.1 %collective-permute-start.5 = (f32[128,128]{0,1:T(8,128)S(1)}, f32[128,128]{0,1:T(8,128)S(1)}, u32[]{:S(2)}, u32[]{:S(2)}) collective-permute-start(f32[128,128]{0,1:T(8,128)S(1)} %copy.72), channel_id=1, source_target_pairs={{0,16},{16,32},{32,48},{48,64},{64,80},{80,96},{96,112},{112,0},{1... | collective-permute-start | bytes 196616 | tf_op jit(solution)/shard_map/ppermute | solution.py:172
  318.2 39.8 %copy-start.2 = (f32[128,640]{1,0:T(8,128)S(1)}, f32[128,640]{1,0:T(8,128)}, u32[]{:S(2)}) copy-start(f32[128,640]{1,0:T(8,128)} %reduce-scatter.9.cloned.1.call-done) | copy-start | bytes 983044
  348.4 6.0 %collective-permute-start.3 = (f32[128,128]{0,1:T(8,128)S(1)}, f32[128,128]{0,1:T(8,128)S(1)}, u32[]{:S(2)}, u32[]{:S(2)}) collective-permute-start(f32[128,128]{0,1:T(8,128)S(1)} %copy.70), channel_id=1, source_target_pairs={{0,48},{16,64},{32,80},{48,96},{64,112},{80,0},{96,16},{112,32},{1... | collective-permute-start | bytes 196616 | tf_op jit(solution)/shard_map/ppermute | solution.py:172
  348.5 6.6 %collective-permute-start.6 = (f32[128,128]{0,1:T(8,128)S(1)}, f32[128,128]{0,1:T(8,128)S(1)}, u32[]{:S(2)}, u32[]{:S(2)}) collective-permute-start(f32[128,128]{0,1:T(8,128)S(1)} %copy.73), channel_id=1, source_target_pairs={{0,48},{16,64},{32,80},{48,96},{64,112},{80,0},{96,16},{112,32},{1... | collective-permute-start | bytes 196616 | tf_op jit(solution)/shard_map/ppermute | solution.py:172
  348.6 7.2 %collective-permute-start.7 = (f32[128,128]{0,1:T(8,128)S(1)}, f32[128,128]{0,1:T(8,128)S(1)}, u32[]{:S(2)}, u32[]{:S(2)}) collective-permute-start(f32[128,128]{0,1:T(8,128)S(1)} %copy.74), channel_id=1, source_target_pairs={{0,32},{16,48},{32,64},{48,80},{64,96},{80,112},{96,0},{112,16},{1... | collective-permute-start | bytes 196616 | tf_op jit(solution)/shard_map/ppermute | solution.py:172
  352.0 6.0 %collective-permute-start.8 = (f32[128,128]{0,1:T(8,128)S(1)}, f32[128,128]{0,1:T(8,128)S(1)}, u32[]{:S(2)}, u32[]{:S(2)}) collective-permute-start(f32[128,128]{0,1:T(8,128)S(1)} %copy.75), channel_id=1, source_target_pairs={{0,16},{16,32},{32,48},{48,64},{64,80},{80,96},{96,112},{112,0},{1... | collective-permute-start | bytes 196616 | tf_op jit(solution)/shard_map/ppermute | solution.py:172
  352.0 6.3 %collective-permute-start.9 = (f32[128,128]{0,1:T(8,128)S(1)}, f32[128,128]{0,1:T(8,128)S(1)}, u32[]{:S(2)}, u32[]{:S(2)}) collective-permute-start(f32[128,128]{0,1:T(8,128)S(1)} %copy.76), channel_id=1, source_target_pairs={{0,48},{16,64},{32,80},{48,96},{64,112},{80,0},{96,16},{112,32},{1... | collective-permute-start | bytes 196616 | tf_op jit(solution)/shard_map/ppermute | solution.py:172
  354.4 6.0 %collective-permute-start.10 = (f32[128,128]{0,1:T(8,128)S(1)}, f32[128,128]{0,1:T(8,128)S(1)}, u32[]{:S(2)}, u32[]{:S(2)}) collective-permute-start(f32[128,128]{0,1:T(8,128)S(1)} %copy.77), channel_id=1, source_target_pairs={{0,32},{16,48},{32,64},{48,80},{64,96},{80,112},{96,0},{112,16},{1... | collective-permute-start | bytes 196616 | tf_op jit(solution)/shard_map/ppermute | solution.py:172
  355.1 5.5 %collective-permute-start.11 = (f32[128,128]{0,1:T(8,128)S(1)}, f32[128,128]{0,1:T(8,128)S(1)}, u32[]{:S(2)}, u32[]{:S(2)}) collective-permute-start(f32[128,128]{0,1:T(8,128)S(1)} %copy.78), channel_id=1, source_target_pairs={{0,16},{16,32},{32,48},{48,64},{64,80},{80,96},{96,112},{112,0},{1... | collective-permute-start | bytes 196616 | tf_op jit(solution)/shard_map/ppermute | solution.py:172
  (1 other events, 13.8 us)
Sparse Core Ops, SparseCore 0:
  110.8 41.5 reduce-scatter.4
  183.2 34.3 reduce-scatter.6
  244.3 37.7 reduce-scatter.8
  311.3 35.3 reduce-scatter.10

commit v5 on v4

--- a/solution.py
+++ b/solution.py
@@ -202,7 +202,11 @@
     pieces = []
     for k in range(owned_tiles):
         buffer = buffers[k].reshape(occ_count, CAP * tile_width, col_width)
+        if k == 2:
+            buffer, pieces[0] = lax.optimization_barrier((buffer, pieces[0]))
         received = lax.all_to_all(buffer, "occ", split_axis=0, concat_axis=0, tiled=True)
+        if k == 3:
+            received, pieces[1] = lax.optimization_barrier((received, pieces[1]))
         received = received.reshape(occ_count, CAP, tile_width, col_width)
         packed = packed_gram(received, received_labels[:, k], DOM, aux_count)
         reduced = lax.psum_scatter(packed, "aux", scatter_dimension=0, tiled=True)

time: 371 us -> 388 us (1.046)
  waiting for transfers between devices: 240 us -> 246 us
  local copies, waits for them, and re-layouts: 17.7 us -> 21.7 us
    all_to_all x4, waiting for transfers between devices: 205 us -> 196 us  [per_device(): lax.all_to_all(buffer, 'occ', split_axis=0, concat_axis=0, tiled=True)]
    reduce_scatter x4, waiting for transfers between devices: 27.6 us -> 35.6 us  [per_device(): reduced = lax.psum_scatter(packed, 'aux', scatter_dimension=0, tiled=True)]
    ppermute x12, waiting for transfers between devices: 7.84 us -> 14.5 us  [unpack_rows(): lax.ppermute(sent, 'aux', perm=[(i, (i + shift) % parts) for i in range(p...]
    ppermute x12, starting transfers between devices: 7.81 us -> 13 us  [unpack_rows(): lax.ppermute(sent, 'aux', perm=[(i, (i + shift) % parts) for i in range(p...]
  transfers between devices with their start and end apart: 21 -> 21, of which waited for: 11 -> 13; matrix products, arithmetic and copies ran while one was open for 4% -> 5% of each run, Pallas kernels for 10% -> 10%
where the time goes in v5:
time: 388 us; the launch traced here: 387 us
  waiting for transfers between devices  246 us (63%)
  starting transfers between devices  50.6 us (13%)
  Pallas kernels  44.7 us (12%)
  local copies, waits for them, and re-layouts  21.7 us (6%)
  between operations  13.4 us (3%)
  other arithmetic  9.96 us (3%)
    all_to_all x4, waiting for transfers between devices, per_device(): lax.all_to_all(buffer, 'occ', split_axis=0, concat_axis=0, tiled=True)  196 us
    reduce_scatter x4, waiting for transfers between devices, per_device(): reduced = lax.psum_scatter(packed, 'aux', scatter_dimension=0, tiled=True)  35.6 us
    pallas_call x4, Pallas kernels, packed_gram(): pl.pallas_call(functools.partial(_gram_kernel, row_blk=row_blk), grid_spe...  30.2 us
    all_to_all x4, starting transfers between devices, per_device(): lax.all_to_all(buffer, 'occ', split_axis=0, concat_axis=0, tiled=True)  29.5 us
    pallas_call x1, Pallas kernels, transform_into_slots(): pl.pallas_call(_transform_kernel, grid_spec=grid_spec, out_shape=[jax.Sha...  14.5 us
    ppermute x12, waiting for transfers between devices, unpack_rows(): lax.ppermute(sent, 'aux', perm=[(i, (i + shift) % parts) for i in range(p...  14.5 us
    ppermute x12, starting transfers between devices, unpack_rows(): lax.ppermute(sent, 'aux', perm=[(i, (i + shift) % parts) for i in range(p...  13 us
    all_to_all x1, starting transfers between devices, per_device(): lax.all_to_all(labels, 'occ', split_axis=0, concat_axis=0, tiled=True)  7.99 us
  transfers between devices with their start and end apart: 21, of which 13 were waited for; matrix products, arithmetic and copies ran while one was open for 5% of the time, Pallas kernels for 10%

profile of v5, /device:TPU:0, one launch (start us, length us, event | category | flops | bytes accessed | tf_op | source)
XLA Modules:
  0.0 386.6 jit_solution(9425633299874769567)
XLA Ops:
  13.3 8.0 %all-to-all-start = ((s32[16,4,2]{1,2,0:T(2,128)}), s32[16,4,2]{1,2,0:T(2,128)S(1)}, u32[]{:S(2)}, u32[]{:S(2)}) async-start(s32[16,4,2]{1,2,0:T(2,128)} %copy.51), calls=%async_computation | async-start | bytes 32768 | tf_op jit(solution)/shard_map/all_to_all | solution.py:197
  21.3 3.3 copy.49
  24.6 2.1 fusion.2.w_ref
  26.8 14.5 %shard_map.55 = (bf16[32,64,1024]{2,1,0:T(8,128)(2,1)}, bf16[32,64,1024]{2,1,0:T(8,128)(2,1)}, bf16[32,64,1024]{2,1,0:T(8,128)(2,1)}, bf16[32,64,1024]{2,1,0:T(8,128)(2,1)}) custom-call(s32[96]{0:T(128)} %get-tuple-element.27.out_ref, s32[96]{0:T(128)} %get-tuple-element.28.slot_ref, bf16[96,64,1024]{2,1,0:T(8,128)(2,1)} %tc_ref.1, ...), custom_call_target="tpu_custom_call" | custom-call | flops 3221225472 | bytes 25165824 | tf_op jit(solution)/shard_map/pallas_call | solution.py:93
  41.3 7.3 %all-to-all-start.3 = ((bf16[16,128,1024]{2,1,0:T(8,128)(2,1)}), bf16[16,128,1024]{2,1,0:T(8,128)(2,1)}, u32[]{:S(2)}, u32[]{:S(2)}) async-start(bf16[16,128,1024]{2,1,0:T(8,128)(2,1)} %bitcast.30), calls=%async_computation.4 | async-start | bytes 8388608 | tf_op jit(solution)/shard_map/all_to_all | solution.py:207
  50.5 52.5 %all-to-all-done.3 = bf16[16,128,1024]{2,1,0:T(8,128)(2,1)} async-done(((bf16[16,128,1024]{2,1,0:T(8,128)(2,1)}), bf16[16,128,1024]{2,1,0:T(8,128)(2,1)}, u32[]{:S(2)}, u32[]{:S(2)}) %all-to-all-start.3) | async-done | bytes 4194336 | tf_op jit(solution)/shard_map/all_to_all | solution.py:207
  103.0 7.6 %shard_map.57 = f32[1024,640]{1,0:T(8,128)} custom-call(s32[32]{0:T(128)} %reshape_squeeze.13.lab_ref, bf16[16,2,64,1024]{3,2,1,0:T(8,128)(2,1)} %bitcast.10.x_ref), custom_call_target="tpu_custom_call" | custom-call | flops 1342177280 | bytes 6815744 | tf_op jit(solution)/shard_map/pallas_call | solution.py:149
  110.7 11.3 %all-to-all-start.1 = ((bf16[16,128,1024]{2,1,0:T(8,128)(2,1)}), bf16[16,128,1024]{2,1,0:T(8,128)(2,1)}, u32[]{:S(2)}, u32[]{:S(2)}) async-start(bf16[16,128,1024]{2,1,0:T(8,128)(2,1)} %bitcast.29), calls=%async_computation.1 | async-start | bytes 8388608 | tf_op jit(solution)/shard_map/all_to_all | solution.py:207
  122.6 52.7 %all-to-all-done.1 = bf16[16,128,1024]{2,1,0:T(8,128)(2,1)} async-done(((bf16[16,128,1024]{2,1,0:T(8,128)(2,1)}), bf16[16,128,1024]{2,1,0:T(8,128)(2,1)}, u32[]{:S(2)}, u32[]{:S(2)}) %all-to-all-start.1) | async-done | bytes 4194336 | tf_op jit(solution)/shard_map/all_to_all | solution.py:207
  175.3 7.6 %shard_map.56 = f32[1024,640]{1,0:T(8,128)} custom-call(s32[32]{0:T(128)} %reshape_squeeze.12.lab_ref, bf16[16,2,64,1024]{3,2,1,0:T(8,128)(2,1)} %bitcast.3.x_ref), custom_call_target="tpu_custom_call" | custom-call | flops 1342177280 | bytes 6815744 | tf_op jit(solution)/shard_map/pallas_call | solution.py:149
  183.0 3.3 copy.52
  186.3 4.6 %all-to-all-start.2 = ((bf16[16,128,1024]{2,1,0:T(8,128)(2,1)}), bf16[16,128,1024]{2,1,0:T(8,128)(2,1)}, u32[]{:S(2)}, u32[]{:S(2)}) async-start(bf16[16,128,1024]{2,1,0:T(8,128)(2,1)} %bitcast.28), calls=%async_computation.3 | async-start | bytes 8388608 | tf_op jit(solution)/shard_map/all_to_all | solution.py:207
  193.9 2.1 collective-permute-start.5
  198.1 2.3 collective-permute-done.4
  200.4 2.1 collective-permute-done.5
  203.7 37.1 %all-to-all-done.2 = bf16[16,128,1024]{2,1,0:T(8,128)(2,1)} async-done(((bf16[16,128,1024]{2,1,0:T(8,128)(2,1)}), bf16[16,128,1024]{2,1,0:T(8,128)(2,1)}, u32[]{:S(2)}, u32[]{:S(2)}) %all-to-all-start.2) | async-done | bytes 4194336 | tf_op jit(solution)/shard_map/all_to_all | solution.py:207
  240.9 7.5 %shard_map.59 = f32[1024,640]{1,0:T(8,128)} custom-call(s32[32]{0:T(128)} %reshape_squeeze.15.lab_ref, bf16[16,2,64,1024]{3,2,1,0:T(8,128)(2,1)} %bitcast.20.x_ref), custom_call_target="tpu_custom_call" | custom-call | flops 1342177280 | bytes 6815744 | tf_op jit(solution)/shard_map/pallas_call | solution.py:149
  258.2 6.3 %all-to-all-start.4 = ((bf16[16,128,1024]{2,1,0:T(8,128)(2,1)}), bf16[16,128,1024]{2,1,0:T(8,128)(2,1)}, u32[]{:S(2)}, u32[]{:S(2)}) async-start(bf16[16,128,1024]{2,1,0:T(8,128)(2,1)} %bitcast.27), calls=%async_computation.6 | async-start | bytes 8388608 | tf_op jit(solution)/shard_map/all_to_all | solution.py:207
  265.2 53.7 %all-to-all-done.4 = bf16[16,128,1024]{2,1,0:T(8,128)(2,1)} async-done(((bf16[16,128,1024]{2,1,0:T(8,128)(2,1)}), bf16[16,128,1024]{2,1,0:T(8,128)(2,1)}, u32[]{:S(2)}, u32[]{:S(2)}) %all-to-all-start.4) | async-done | bytes 4194336 | tf_op jit(solution)/shard_map/all_to_all | solution.py:207
  318.9 7.5 %shard_map.58 = f32[1024,640]{1,0:T(8,128)} custom-call(s32[32]{0:T(128)} %reshape_squeeze.14.lab_ref, bf16[16,2,64,1024]{3,2,1,0:T(8,128)(2,1)} %bitcast.15.x_ref), custom_call_target="tpu_custom_call" | custom-call | flops 1342177280 | bytes 6815744 | tf_op jit(solution)/shard_map/pallas_call | solution.py:149
  328.0 4.7 %collective-permute-start.11 = (f32[128,128]{0,1:T(8,128)S(1)}, f32[128,128]{0,1:T(8,128)S(1)}, u32[]{:S(2)}, u32[]{:S(2)}) collective-permute-start(f32[128,128]{0,1:T(8,128)S(1)} %copy.72), channel_id=1, source_target_pairs={{0,16},{16,32},{32,48},{48,64},{64,80},{80,96},{96,112},{112,0},{1... | collective-permute-start | bytes 196616 | tf_op jit(solution)/shard_map/ppermute | solution.py:172
  332.8 35.5 %reduce-scatter.9.cloned.1.call-done = f32[128,640]{1,0:T(8,128)} async-done(((f32[1024,640]{1,0:T(8,128)}), f32[128,640]{1,0:T(8,128)}) %reduce-scatter.9.cloned.1.call-update) | async-done | bytes 327696 | tf_op jit(solution)/shard_map/reduce_scatter | solution.py:212
  371.1 3.9 collective-permute-done.6
  377.4 2.7 copy.63
  (64 shorter events, 32.9 us)
Async XLA Ops:
  13.3 28.0 %all-to-all-start = ((s32[16,4,2]{1,2,0:T(2,128)}), s32[16,4,2]{1,2,0:T(2,128)S(1)}, u32[]{:S(2)}, u32[]{:S(2)}) async-start(s32[16,4,2]{1,2,0:T(2,128)} %copy.51), calls=%async_computation | async-start | bytes 32768 | tf_op jit(solution)/shard_map/all_to_all | solution.py:197
  41.3 61.7 %all-to-all-start.3 = ((bf16[16,128,1024]{2,1,0:T(8,128)(2,1)}), bf16[16,128,1024]{2,1,0:T(8,128)(2,1)}, u32[]{:S(2)}, u32[]{:S(2)}) async-start(bf16[16,128,1024]{2,1,0:T(8,128)(2,1)} %bitcast.30), calls=%async_computation.4 | async-start | bytes 8388608 | tf_op jit(solution)/shard_map/all_to_all | solution.py:207
  48.6 142.4 %reduce-scatter.7.cloned.1.call-start = ((), (), s32[]{:S(2)}) async-start(), calls=%async_computation.10 | async-start | bytes 2949120 | tf_op jit(solution)/shard_map/reduce_scatter | solution.py:212
  110.7 64.7 %all-to-all-start.1 = ((bf16[16,128,1024]{2,1,0:T(8,128)(2,1)}), bf16[16,128,1024]{2,1,0:T(8,128)(2,1)}, u32[]{:S(2)}, u32[]{:S(2)}) async-start(bf16[16,128,1024]{2,1,0:T(8,128)(2,1)} %bitcast.29), calls=%async_computation.1 | async-start | bytes 8388608 | tf_op jit(solution)/shard_map/all_to_all | solution.py:207
  122.0 126.4 %reduce-scatter.5.cloned.1.call-start = ((), (), s32[]{:S(2)}) async-start(), calls=%async_computation.9 | async-start | bytes 2949120 | tf_op jit(solution)/shard_map/reduce_scatter | solution.py:212
  186.3 54.5 %all-to-all-start.2 = ((bf16[16,128,1024]{2,1,0:T(8,128)(2,1)}), bf16[16,128,1024]{2,1,0:T(8,128)(2,1)}, u32[]{:S(2)}, u32[]{:S(2)}) async-start(bf16[16,128,1024]{2,1,0:T(8,128)(2,1)} %bitcast.28), calls=%async_computation.3 | async-start | bytes 8388608 | tf_op jit(solution)/shard_map/all_to_all | solution.py:207
  190.9 135.5 %reduce-scatter.11.cloned.1.call-start = ((), (), s32[]{:S(2)}) async-start(), calls=%async_computation.12 | async-start | bytes 2949120 | tf_op jit(solution)/shard_map/reduce_scatter | solution.py:212
  192.0 6.1 %collective-permute-start.3 = (f32[128,128]{0,1:T(8,128)S(1)}, f32[128,128]{0,1:T(8,128)S(1)}, u32[]{:S(2)}, u32[]{:S(2)}) collective-permute-start(f32[128,128]{0,1:T(8,128)S(1)} %copy.64), channel_id=1, source_target_pairs={{0,48},{16,64},{32,80},{48,96},{64,112},{80,0},{96,16},{112,32},{1... | collective-permute-start | bytes 196616 | tf_op jit(solution)/shard_map/ppermute | solution.py:172
  192.1 8.3 %collective-permute-start.4 = (f32[128,128]{0,1:T(8,128)S(1)}, f32[128,128]{0,1:T(8,128)S(1)}, u32[]{:S(2)}, u32[]{:S(2)}) collective-permute-start(f32[128,128]{0,1:T(8,128)S(1)} %copy.65), channel_id=1, source_target_pairs={{0,32},{16,48},{32,64},{48,80},{64,96},{80,112},{96,0},{112,16},{1... | collective-permute-start | bytes 196616 | tf_op jit(solution)/shard_map/ppermute | solution.py:172
  193.9 8.6 %collective-permute-start.5 = (f32[128,128]{0,1:T(8,128)S(1)}, f32[128,128]{0,1:T(8,128)S(1)}, u32[]{:S(2)}, u32[]{:S(2)}) collective-permute-start(f32[128,128]{0,1:T(8,128)S(1)} %copy.66), channel_id=1, source_target_pairs={{0,16},{16,32},{32,48},{48,64},{64,80},{80,96},{96,112},{112,0},{1... | collective-permute-start | bytes 196616 | tf_op jit(solution)/shard_map/ppermute | solution.py:172
  249.3 5.7 %collective-permute-start = (f32[128,128]{0,1:T(8,128)S(1)}, f32[128,128]{0,1:T(8,128)S(1)}, u32[]{:S(2)}, u32[]{:S(2)}) collective-permute-start(f32[128,128]{0,1:T(8,128)S(1)} %get-tuple-element.34), channel_id=1, source_target_pairs={{0,48},{16,64},{32,80},{48,96},{64,112},{80,0},{96,16},{112,32},{1... | collective-permute-start | bytes 196616 | tf_op jit(solution)/shard_map/ppermute | solution.py:172
  249.4 6.6 %collective-permute-start.1 = (f32[128,128]{0,1:T(8,128)S(1)}, f32[128,128]{0,1:T(8,128)S(1)}, u32[]{:S(2)}, u32[]{:S(2)}) collective-permute-start(f32[128,128]{0,1:T(8,128)S(1)} %get-tuple-element.33), channel_id=1, source_target_pairs={{0,32},{16,48},{32,64},{48,80},{64,96},{80,112},{96,0},{112,16},{1... | collective-permute-start | bytes 196616 | tf_op jit(solution)/shard_map/ppermute | solution.py:172
  251.0 6.9 %collective-permute-start.2 = (f32[128,128]{0,1:T(8,128)S(1)}, f32[128,128]{0,1:T(8,128)S(1)}, u32[]{:S(2)}, u32[]{:S(2)}) collective-permute-start(f32[128,128]{0,1:T(8,128)S(1)} %get-tuple-element.32), channel_id=1, source_target_pairs={{0,16},{16,32},{32,48},{48,64},{64,80},{80,96},{96,112},{112,0},{1... | collective-permute-start | bytes 196616 | tf_op jit(solution)/shard_map/ppermute | solution.py:172
  258.2 60.7 %all-to-all-start.4 = ((bf16[16,128,1024]{2,1,0:T(8,128)(2,1)}), bf16[16,128,1024]{2,1,0:T(8,128)(2,1)}, u32[]{:S(2)}, u32[]{:S(2)}) async-start(bf16[16,128,1024]{2,1,0:T(8,128)(2,1)} %bitcast.27), calls=%async_computation.6 | async-start | bytes 8388608 | tf_op jit(solution)/shard_map/all_to_all | solution.py:207
  264.5 103.8 %reduce-scatter.9.cloned.1.call-start = ((), (), s32[]{:S(2)}) async-start(), calls=%async_computation.11 | async-start | bytes 2949120 | tf_op jit(solution)/shard_map/reduce_scatter | solution.py:212
  327.4 42.2 %collective-permute-start.9 = (f32[128,128]{0,1:T(8,128)S(1)}, f32[128,128]{0,1:T(8,128)S(1)}, u32[]{:S(2)}, u32[]{:S(2)}) collective-permute-start(f32[128,128]{0,1:T(8,128)S(1)} %copy.70), channel_id=1, source_target_pairs={{0,48},{16,64},{32,80},{48,96},{64,112},{80,0},{96,16},{112,32},{1... | collective-permute-start | bytes 196616 | tf_op jit(solution)/shard_map/ppermute | solution.py:172
  327.8 42.0 %collective-permute-start.10 = (f32[128,128]{0,1:T(8,128)S(1)}, f32[128,128]{0,1:T(8,128)S(1)}, u32[]{:S(2)}, u32[]{:S(2)}) collective-permute-start(f32[128,128]{0,1:T(8,128)S(1)} %copy.71), channel_id=1, source_target_pairs={{0,32},{16,48},{32,64},{48,80},{64,96},{80,112},{96,0},{112,16},{1... | collective-permute-start | bytes 196616 | tf_op jit(solution)/shard_map/ppermute | solution.py:172
  328.0 41.8 %collective-permute-start.11 = (f32[128,128]{0,1:T(8,128)S(1)}, f32[128,128]{0,1:T(8,128)S(1)}, u32[]{:S(2)}, u32[]{:S(2)}) collective-permute-start(f32[128,128]{0,1:T(8,128)S(1)} %copy.72), channel_id=1, source_target_pairs={{0,16},{16,32},{32,48},{48,64},{64,80},{80,96},{96,112},{112,0},{1... | collective-permute-start | bytes 196616 | tf_op jit(solution)/shard_map/ppermute | solution.py:172
  369.3 5.6 %collective-permute-start.6 = (f32[128,128]{0,1:T(8,128)S(1)}, f32[128,128]{0,1:T(8,128)S(1)}, u32[]{:S(2)}, u32[]{:S(2)}) collective-permute-start(f32[128,128]{0,1:T(8,128)S(1)} %copy.67), channel_id=1, source_target_pairs={{0,48},{16,64},{32,80},{48,96},{64,112},{80,0},{96,16},{112,32},{1... | collective-permute-start | bytes 196616 | tf_op jit(solution)/shard_map/ppermute | solution.py:172
  369.5 6.5 %collective-permute-start.7 = (f32[128,128]{0,1:T(8,128)S(1)}, f32[128,128]{0,1:T(8,128)S(1)}, u32[]{:S(2)}, u32[]{:S(2)}) collective-permute-start(f32[128,128]{0,1:T(8,128)S(1)} %copy.68), channel_id=1, source_target_pairs={{0,32},{16,48},{32,64},{48,80},{64,96},{80,112},{96,0},{112,16},{1... | collective-permute-start | bytes 196616 | tf_op jit(solution)/shard_map/ppermute | solution.py:172
  369.7 6.3 %collective-permute-start.8 = (f32[128,128]{0,1:T(8,128)S(1)}, f32[128,128]{0,1:T(8,128)S(1)}, u32[]{:S(2)}, u32[]{:S(2)}) collective-permute-start(f32[128,128]{0,1:T(8,128)S(1)} %copy.69), channel_id=1, source_target_pairs={{0,16},{16,32},{32,48},{48,64},{64,80},{80,96},{96,112},{112,0},{1... | collective-permute-start | bytes 196616 | tf_op jit(solution)/shard_map/ppermute | solution.py:172
Sparse Core Ops, SparseCore 0:
  110.8 41.5 reduce-scatter.6
  186.4 36.9 reduce-scatter.4
  248.5 36.2 reduce-scatter.10
  326.5 41.7 reduce-scatter.8

commit v6 on v2

--- a/solution.py
+++ b/solution.py
@@ -12,35 +12,25 @@
 LANES = 256
 
 
-def _transform_kernel(slot_ref, empty_ref, tc_ref, w_ref, *rest):
-    chunks = (len(rest) - 3)
-    outs, (buf, zero, sems) = rest[:chunks], rest[chunks:]
-    chunk_slots = outs[0].shape[0]
+def _transform_kernel(out_ref, slot_ref, tc_ref, w_ref, *rest):
+    chunks = len(rest) - 2
+    outs, (buf, sems) = rest[:chunks], rest[chunks:]
     step = pl.program_id(0)
     steps = pl.num_programs(0)
     per = tc_ref.shape[0]
-    epr = sems.shape[1] - per
     rows, width = tc_ref.shape[1], tc_ref.shape[2]
     groups = width // LANES
     half = w_ref.shape[1]
     side = buf.at[step % 2]
 
-    @pl.when(step == 0)
-    def _():
-        zero[...] = jnp.zeros_like(zero)
-
     def each_copy(at, parity, act):
         held = buf.at[parity]
-        for j in range(per + epr):
-            if j < per:
-                src, g = held.at[j], slot_ref[at * per + j]
-            else:
-                src, g = zero, empty_ref[at * epr + j - per]
-            chunk, local = g // chunk_slots, g % chunk_slots
+        for j in range(per):
+            chunk, local = out_ref[at * per + j], slot_ref[at * per + j]
             for kk in range(chunks):
                 @pl.when(chunk == kk)
                 def _():
-                    act(pltpu.make_async_copy(src, outs[kk].at[local], sems.at[parity, j]))
+                    act(pltpu.make_async_copy(held.at[j], outs[kk].at[local], sems.at[parity, j]))
 
     def start(cp):
         cp.start()
@@ -72,14 +62,11 @@
         each_copy(step, step % 2, wait)
 
 
-def transform_into_slots(three_center, coefficients, buffer_slot, empty_slot, slot_count, chunks):
+def transform_into_slots(three_center, coefficients, out_index, slot_index, group_slots):
     pair_count, rows, width = three_center.shape
     tile = coefficients.shape[1]
-    empty_count = empty_slot.shape[0]
-    steps = math.gcd(pair_count, empty_count)
-    steps = 8 if steps % 8 == 0 else steps
+    steps = 8 if pair_count % 8 == 0 else 1
     per = pair_count // steps
-    epr = empty_count // steps
     zeros = jnp.zeros_like(coefficients)
     w2 = jnp.concatenate(
         [
@@ -92,29 +79,27 @@
         num_scalar_prefetch=2,
         grid=(steps,),
         in_specs=[
-            pl.BlockSpec((per, rows, width), lambda i, s, e: (i, 0, 0)),
-            pl.BlockSpec((per, 2 * tile, 2 * tile), lambda i, s, e: (i, 0, 0)),
+            pl.BlockSpec((per, rows, width), lambda i, o, s: (i, 0, 0)),
+            pl.BlockSpec((per, 2 * tile, 2 * tile), lambda i, o, s: (i, 0, 0)),
         ],
-        out_specs=[pl.BlockSpec(memory_space=pl.ANY)] * chunks,
+        out_specs=[pl.BlockSpec(memory_space=pl.ANY)] * len(group_slots),
         scratch_shapes=[
             pltpu.VMEM((2, per, rows, width), three_center.dtype),
-            pltpu.VMEM((rows, width), three_center.dtype),
-            pltpu.SemaphoreType.DMA((2, per + epr)),
+            pltpu.SemaphoreType.DMA((2, per)),
         ],
     )
     block_bytes = rows * width * 2
-    chunk_shape = jax.ShapeDtypeStruct((slot_count // chunks, rows, width), three_center.dtype)
     return pl.pallas_call(
         _transform_kernel,
         grid_spec=grid_spec,
-        out_shape=[chunk_shape] * chunks,
+        out_shape=[jax.ShapeDtypeStruct((n, rows, width), three_center.dtype) for n in group_slots],
         compiler_params=pltpu.CompilerParams(dimension_semantics=("arbitrary",)),
         cost_estimate=pl.CostEstimate(
             flops=2 * pair_count * rows * width * 4 * tile,
             transcendentals=0,
-            bytes_accessed=(pair_count + slot_count) * block_bytes,
+            bytes_accessed=2 * pair_count * block_bytes,
         ),
-    )(buffer_slot, empty_slot, three_center, w2)
+    )(out_index, slot_index, three_center, w2)
 
 
 def _gram_kernel(lab_ref, x_ref, o_ref, acc):
@@ -166,6 +151,7 @@
 def per_device(three_center, coefficients, target, domain_slot, owner_order):
     pair_count, tile_width, col_width = three_center.shape
     occ_count = lax.axis_size("occ")
+    aux_count = lax.axis_size("aux")
     tile_count = owner_order.shape[0]
     owned_tiles = tile_count // occ_count
     slot_count = tile_count * CAP
@@ -177,15 +163,14 @@
     earlier = (target[:, None] == target[None, :]) & (pair_ids[:, None] > pair_ids[None, :])
     rank = jnp.sum(earlier.astype(jnp.int32), axis=1)
     pos = jnp.take(position, target)
-    buffer_slot = ((pos % owned_tiles) * occ_count + pos // owned_tiles) * CAP + rank
-    labels = jnp.full((slot_count,), -1, jnp.int32).at[buffer_slot].set(domain_slot)
-    empty_count = slot_count - pair_count
-    empty_slot = jnp.nonzero(labels < 0, size=empty_count, fill_value=0)[0].astype(jnp.int32)
+    out_index = pos % owned_tiles
+    slot_index = (pos // owned_tiles) * CAP + rank
+    labels = jnp.full((slot_count,), -1, jnp.int32).at[out_index * occ_count * CAP + slot_index].set(domain_slot)
     labels = labels.reshape(owned_tiles, occ_count, CAP).transpose(1, 0, 2)
     received_labels = lax.all_to_all(labels, "occ", split_axis=0, concat_axis=0, tiled=True)
 
     buffers = transform_into_slots(
-        three_center, coefficients, buffer_slot, empty_slot, slot_count, owned_tiles
+        three_center, coefficients, out_index, slot_index, [occ_count * CAP] * owned_tiles
     )
     pieces = []
     for k in range(owned_tiles):

time: 369 us -> 363 us (0.984)
  other arithmetic: 11.1 us -> 7.35 us
  transfers between devices with their start and end apart: 9 -> 9, of which waited for: 5 -> 5; matrix products, arithmetic and copies ran while one was open for 4% -> 3% of each run, Pallas kernels for 11% -> 11%
where the time goes in v6:
time: 363 us; the launch traced here: 362 us
  waiting for transfers between devices  243 us (67%)
  Pallas kernels  47.2 us (13%)
  starting transfers between devices  38.8 us (11%)
  between operations  13.3 us (4%)
  local copies, waits for them, and re-layouts  12.8 us (4%)
  other arithmetic  7.35 us (2%)
    all_to_all x4, waiting for transfers between devices, per_device(): lax.all_to_all(buffer, 'occ', split_axis=0, concat_axis=0, tiled=True)  205 us
    reduce_scatter x4, waiting for transfers between devices, per_device(): lax.psum_scatter(partial_gram, 'aux', scatter_dimension=0, tiled=True)  37.9 us
    pallas_call x4, Pallas kernels, domain_gram(): pl.pallas_call(_gram_kernel, grid_spec=grid_spec, out_shape=jax.ShapeDtyp...  32.6 us
    all_to_all x4, starting transfers between devices, per_device(): lax.all_to_all(buffer, 'occ', split_axis=0, concat_axis=0, tiled=True)  30.6 us
    pallas_call x1, Pallas kernels, transform_into_slots(): pl.pallas_call(_transform_kernel, grid_spec=grid_spec, out_shape=[jax.Sha...  14.5 us
    all_to_all x1, starting transfers between devices, per_device(): lax.all_to_all(labels, 'occ', split_axis=0, concat_axis=0, tiled=True)  7.99 us
  transfers between devices with their start and end apart: 9, of which 5 were waited for; matrix products, arithmetic and copies ran while one was open for 3% of the time, Pallas kernels for 11%

profile of v6, /device:TPU:0, one launch (start us, length us, event | category | flops | bytes accessed | tf_op | source)
XLA Modules:
  0.0 362.4 jit_solution(8696923401855861497)
XLA Ops:
  6.5 0.9 convert_reduce_fusion
  8.9 1.2 gather_fusion
  10.1 1.2 compare_select_fusion
  11.3 1.0 scatter_custom_fusion
  13.3 8.0 %all-to-all-start = ((s32[16,4,2]{1,2,0:T(2,128)}), s32[16,4,2]{1,2,0:T(2,128)S(1)}, u32[]{:S(2)}, u32[]{:S(2)}) async-start(s32[16,4,2]{1,2,0:T(2,128)} %copy.16), calls=%async_computation | async-start | bytes 32768 | tf_op jit(solution)/shard_map/all_to_all | solution.py:170
  21.3 3.3 copy.17
  24.6 2.2 fusion.2.w_ref
  26.8 14.5 %shard_map.55 = (bf16[32,64,1024]{2,1,0:T(8,128)(2,1)}, bf16[32,64,1024]{2,1,0:T(8,128)(2,1)}, bf16[32,64,1024]{2,1,0:T(8,128)(2,1)}, bf16[32,64,1024]{2,1,0:T(8,128)(2,1)}) custom-call(s32[96]{0:T(128)} %get-tuple-element.18.out_ref, s32[96]{0:T(128)} %get-tuple-element.19.slot_ref, bf16[96,64,1024]{2,1,0:T(8,128)(2,1)} %tc_ref.1, ...), custom_call_target="tpu_custom_call" | custom-call | flops 3221225472 | bytes 25165824 | tf_op jit(solution)/shard_map/pallas_call | solution.py:92
  41.3 7.3 %all-to-all-start.2 = ((bf16[16,128,1024]{2,1,0:T(8,128)(2,1)}), bf16[16,128,1024]{2,1,0:T(8,128)(2,1)}, u32[]{:S(2)}, u32[]{:S(2)}) async-start(bf16[16,128,1024]{2,1,0:T(8,128)(2,1)} %bitcast.17), calls=%async_computation.3 | async-start | bytes 8388608 | tf_op jit(solution)/shard_map/all_to_all | solution.py:178
  48.6 1.2 slice_reduce_fusion.3
  50.5 52.5 %all-to-all-done.2 = bf16[16,128,1024]{2,1,0:T(8,128)(2,1)} async-done(((bf16[16,128,1024]{2,1,0:T(8,128)(2,1)}), bf16[16,128,1024]{2,1,0:T(8,128)(2,1)}, u32[]{:S(2)}, u32[]{:S(2)}) %all-to-all-start.2) | async-done | bytes 4194336 | tf_op jit(solution)/shard_map/all_to_all | solution.py:178
  103.0 8.2 %shard_map.57 = f32[1024,1024]{1,0:T(8,128)} custom-call(s32[32]{0:T(128)} %reshape_squeeze.13.lab_ref, bf16[16,2,64,1024]{3,2,1,0:T(8,128)(2,1)} %bitcast.5.x_ref), custom_call_target="tpu_custom_call" | custom-call | flops 2147483648 | bytes 8388608 | tf_op jit(solution)/shard_map/pallas_call | solution.py:136
  111.1 11.6 %all-to-all-start.1 = ((bf16[16,128,1024]{2,1,0:T(8,128)(2,1)}), bf16[16,128,1024]{2,1,0:T(8,128)(2,1)}, u32[]{:S(2)}, u32[]{:S(2)}) async-start(bf16[16,128,1024]{2,1,0:T(8,128)(2,1)} %bitcast.16), calls=%async_computation.1 | async-start | bytes 8388608 | tf_op jit(solution)/shard_map/all_to_all | solution.py:178
  123.4 52.7 %all-to-all-done.1 = bf16[16,128,1024]{2,1,0:T(8,128)(2,1)} async-done(((bf16[16,128,1024]{2,1,0:T(8,128)(2,1)}), bf16[16,128,1024]{2,1,0:T(8,128)(2,1)}, u32[]{:S(2)}, u32[]{:S(2)}) %all-to-all-start.1) | async-done | bytes 4194336 | tf_op jit(solution)/shard_map/all_to_all | solution.py:178
  176.1 8.2 %shard_map.56 = f32[1024,1024]{1,0:T(8,128)} custom-call(s32[32]{0:T(128)} %reshape_squeeze.12.lab_ref, bf16[16,2,64,1024]{3,2,1,0:T(8,128)(2,1)} %bitcast.2.x_ref), custom_call_target="tpu_custom_call" | custom-call | flops 2147483648 | bytes 8388608 | tf_op jit(solution)/shard_map/pallas_call | solution.py:136
  184.3 4.5 %all-to-all-start.3 = ((bf16[16,128,1024]{2,1,0:T(8,128)(2,1)}), bf16[16,128,1024]{2,1,0:T(8,128)(2,1)}, u32[]{:S(2)}, u32[]{:S(2)}) async-start(bf16[16,128,1024]{2,1,0:T(8,128)(2,1)} %bitcast.15), calls=%async_computation.5 | async-start | bytes 8388608 | tf_op jit(solution)/shard_map/all_to_all | solution.py:178
  189.5 48.8 %all-to-all-done.3 = bf16[16,128,1024]{2,1,0:T(8,128)(2,1)} async-done(((bf16[16,128,1024]{2,1,0:T(8,128)(2,1)}), bf16[16,128,1024]{2,1,0:T(8,128)(2,1)}, u32[]{:S(2)}, u32[]{:S(2)}) %all-to-all-start.3) | async-done | bytes 4194336 | tf_op jit(solution)/shard_map/all_to_all | solution.py:178
  238.3 8.3 %shard_map.58 = f32[1024,1024]{1,0:T(8,128)} custom-call(s32[32]{0:T(128)} %reshape_squeeze.14.lab_ref, bf16[16,2,64,1024]{3,2,1,0:T(8,128)(2,1)} %bitcast.8.x_ref), custom_call_target="tpu_custom_call" | custom-call | flops 2147483648 | bytes 8388608 | tf_op jit(solution)/shard_map/pallas_call | solution.py:136
  246.7 7.2 %all-to-all-start.4 = ((bf16[16,128,1024]{2,1,0:T(8,128)(2,1)}), bf16[16,128,1024]{2,1,0:T(8,128)(2,1)}, u32[]{:S(2)}, u32[]{:S(2)}) async-start(bf16[16,128,1024]{2,1,0:T(8,128)(2,1)} %bitcast.14), calls=%async_computation.7 | async-start | bytes 8388608 | tf_op jit(solution)/shard_map/all_to_all | solution.py:178
  254.5 51.1 %all-to-all-done.4 = bf16[16,128,1024]{2,1,0:T(8,128)(2,1)} async-done(((bf16[16,128,1024]{2,1,0:T(8,128)(2,1)}), bf16[16,128,1024]{2,1,0:T(8,128)(2,1)}, u32[]{:S(2)}, u32[]{:S(2)}) %all-to-all-start.4) | async-done | bytes 4194336 | tf_op jit(solution)/shard_map/all_to_all | solution.py:178
  305.6 8.0 %shard_map.59 = f32[1024,1024]{1,0:T(8,128)} custom-call(s32[32]{0:T(128)} %reshape_squeeze.15.lab_ref, bf16[16,2,64,1024]{3,2,1,0:T(8,128)(2,1)} %bitcast.11.x_ref), custom_call_target="tpu_custom_call" | custom-call | flops 2147483648 | bytes 8388608 | tf_op jit(solution)/shard_map/pallas_call | solution.py:136
  313.7 37.9 %reduce-scatter.11.cloned.1.call-done = f32[128,1024]{1,0:T(8,128)} async-done(((f32[1024,1024]{1,0:T(8,128)}), f32[128,1024]{1,0:T(8,128)}) %reduce-scatter.11.cloned.1.call-update) | async-done | bytes 524304 | tf_op jit(solution)/shard_map/reduce_scatter | solution.py:181
  351.6 1.7 pad_maximum_fusion
  353.2 2.7 copy.19
  (21 shorter events, 5.1 us)
Async XLA Ops:
  13.3 28.0 %all-to-all-start = ((s32[16,4,2]{1,2,0:T(2,128)}), s32[16,4,2]{1,2,0:T(2,128)S(1)}, u32[]{:S(2)}, u32[]{:S(2)}) async-start(s32[16,4,2]{1,2,0:T(2,128)} %copy.16), calls=%async_computation | async-start | bytes 32768 | tf_op jit(solution)/shard_map/all_to_all | solution.py:170
  41.3 61.7 %all-to-all-start.2 = ((bf16[16,128,1024]{2,1,0:T(8,128)(2,1)}), bf16[16,128,1024]{2,1,0:T(8,128)(2,1)}, u32[]{:S(2)}, u32[]{:S(2)}) async-start(bf16[16,128,1024]{2,1,0:T(8,128)(2,1)} %bitcast.17), calls=%async_computation.3 | async-start | bytes 8388608 | tf_op jit(solution)/shard_map/all_to_all | solution.py:178
  48.6 265.1 %reduce-scatter.7.cloned.1.call-start = ((), (), s32[]{:S(2)}) async-start(), calls=%async_computation.10 | async-start | bytes 4718592 | tf_op jit(solution)/shard_map/reduce_scatter | solution.py:181
  111.1 65.0 %all-to-all-start.1 = ((bf16[16,128,1024]{2,1,0:T(8,128)(2,1)}), bf16[16,128,1024]{2,1,0:T(8,128)(2,1)}, u32[]{:S(2)}, u32[]{:S(2)}) async-start(bf16[16,128,1024]{2,1,0:T(8,128)(2,1)} %bitcast.16), calls=%async_computation.1 | async-start | bytes 8388608 | tf_op jit(solution)/shard_map/all_to_all | solution.py:178
  122.7 190.9 %reduce-scatter.5.cloned.1.call-start = ((), (), s32[]{:S(2)}) async-start(), calls=%async_computation.9 | async-start | bytes 4718592 | tf_op jit(solution)/shard_map/reduce_scatter | solution.py:181
  184.3 54.0 %all-to-all-start.3 = ((bf16[16,128,1024]{2,1,0:T(8,128)(2,1)}), bf16[16,128,1024]{2,1,0:T(8,128)(2,1)}, u32[]{:S(2)}, u32[]{:S(2)}) async-start(bf16[16,128,1024]{2,1,0:T(8,128)(2,1)} %bitcast.15), calls=%async_computation.5 | async-start | bytes 8388608 | tf_op jit(solution)/shard_map/all_to_all | solution.py:178
  188.8 124.8 %reduce-scatter.9.cloned.1.call-start = ((), (), s32[]{:S(2)}) async-start(), calls=%async_computation.11 | async-start | bytes 4718592 | tf_op jit(solution)/shard_map/reduce_scatter | solution.py:181
  246.7 58.9 %all-to-all-start.4 = ((bf16[16,128,1024]{2,1,0:T(8,128)(2,1)}), bf16[16,128,1024]{2,1,0:T(8,128)(2,1)}, u32[]{:S(2)}, u32[]{:S(2)}) async-start(bf16[16,128,1024]{2,1,0:T(8,128)(2,1)} %bitcast.14), calls=%async_computation.7 | async-start | bytes 8388608 | tf_op jit(solution)/shard_map/all_to_all | solution.py:178
  253.9 97.7 %reduce-scatter.11.cloned.1.call-start = ((), (), s32[]{:S(2)}) async-start(), calls=%async_computation.12 | async-start | bytes 4718592 | tf_op jit(solution)/shard_map/reduce_scatter | solution.py:181
Sparse Core Ops, SparseCore 0:
  111.3 44.7 reduce-scatter.6
  184.4 37.4 reduce-scatter.4
  246.8 40.3 reduce-scatter.8
  313.7 37.7 reduce-scatter.10

commit v7 on v6

--- a/solution.py
+++ b/solution.py
@@ -102,50 +102,50 @@
     )(out_index, slot_index, three_center, w2)
 
 
-def _gram_kernel(lab_ref, x_ref, o_ref, acc):
-    k = pl.program_id(0)
-    sources, cap = x_ref.shape[0], x_ref.shape[1]
-    per_source = lab_ref.shape[0] // sources
+def _gram_kernel(lab_ref, *refs):
+    x_refs, (o_ref, acc) = refs[:-2], refs[-2:]
+    cap = len(x_refs)
+    sources = x_refs[0].shape[0]
     acc[...] = jnp.zeros_like(acc)
     for s in range(sources):
         for c in range(cap):
-            e = lab_ref[s * per_source + k * cap + c]
+            e = lab_ref[s * cap + c]
 
             @pl.when(e >= 0)
             def _():
-                acc[e] += x_ref[s, c].astype(jnp.float32)
+                acc[e] += x_refs[c][s].astype(jnp.float32)
 
     dom, rows, width = acc.shape
-    fitted = acc[...].astype(x_ref.dtype).reshape(dom * rows, width)
+    fitted = acc[...].astype(x_refs[0].dtype).reshape(dom * rows, width)
     o_ref[...] = lax.dot_general(
         fitted, fitted, (((1,), (1,)), ((), ())), preferred_element_type=jnp.float32
     )
 
 
 def domain_gram(received, labels, dom):
-    sources, slots, rows, width = received.shape
-    owned = slots // CAP
+    sources, rows, width = received[0].shape
+    cap = len(received)
     domain_rows = dom * rows
     grid_spec = pltpu.PrefetchScalarGridSpec(
         num_scalar_prefetch=1,
-        grid=(owned,),
-        in_specs=[pl.BlockSpec((sources, CAP, rows, width), lambda k, lab: (0, k, 0, 0))],
-        out_specs=pl.BlockSpec((domain_rows, domain_rows), lambda k, lab: (0, k)),
+        grid=(1,),
+        in_specs=[pl.BlockSpec((sources, rows, width), lambda k, lab: (0, 0, 0))] * cap,
+        out_specs=pl.BlockSpec((domain_rows, domain_rows), lambda k, lab: (0, 0)),
         scratch_shapes=[pltpu.VMEM((dom, rows, width), jnp.float32)],
     )
     return pl.pallas_call(
         _gram_kernel,
         grid_spec=grid_spec,
-        out_shape=jax.ShapeDtypeStruct((domain_rows, owned * domain_rows), jnp.float32),
+        out_shape=jax.ShapeDtypeStruct((domain_rows, domain_rows), jnp.float32),
         compiler_params=pltpu.CompilerParams(
             dimension_semantics=("arbitrary",), vmem_limit_bytes=60 * 1024 * 1024
         ),
         cost_estimate=pl.CostEstimate(
-            flops=2 * owned * domain_rows * domain_rows * width,
+            flops=2 * domain_rows * domain_rows * width,
             transcendentals=0,
-            bytes_accessed=sources * slots * rows * width * 2 + owned * domain_rows * domain_rows * 4,
+            bytes_accessed=cap * sources * rows * width * 2 + domain_rows * domain_rows * 4,
         ),
-    )(labels.reshape(-1), received)
+    )(labels.reshape(-1), *received)
 
 
 def per_device(three_center, coefficients, target, domain_slot, owner_order):
@@ -163,20 +163,21 @@
     earlier = (target[:, None] == target[None, :]) & (pair_ids[:, None] > pair_ids[None, :])
     rank = jnp.sum(earlier.astype(jnp.int32), axis=1)
     pos = jnp.take(position, target)
-    out_index = pos % owned_tiles
-    slot_index = (pos // owned_tiles) * CAP + rank
-    labels = jnp.full((slot_count,), -1, jnp.int32).at[out_index * occ_count * CAP + slot_index].set(domain_slot)
+    out_index = (pos % owned_tiles) * CAP + rank
+    slot_index = pos // owned_tiles
+    labels = jnp.full((slot_count,), -1, jnp.int32).at[((pos % owned_tiles) * occ_count + slot_index) * CAP + rank].set(domain_slot)
     labels = labels.reshape(owned_tiles, occ_count, CAP).transpose(1, 0, 2)
     received_labels = lax.all_to_all(labels, "occ", split_axis=0, concat_axis=0, tiled=True)
 
     buffers = transform_into_slots(
-        three_center, coefficients, out_index, slot_index, [occ_count * CAP] * owned_tiles
+        three_center, coefficients, out_index, slot_index, [occ_count] * (owned_tiles * CAP)
     )
     pieces = []
     for k in range(owned_tiles):
-        buffer = buffers[k].reshape(occ_count, CAP * tile_width, col_width)
-        received = lax.all_to_all(buffer, "occ", split_axis=0, concat_axis=0, tiled=True)
-        received = received.reshape(occ_count, CAP, tile_width, col_width)
+        received = [
+            lax.all_to_all(buffers[k * CAP + c], "occ", split_axis=0, concat_axis=0, tiled=True)
+            for c in range(CAP)
+        ]
         partial_gram = domain_gram(received, received_labels[:, k], DOM)
         pieces.append(lax.psum_scatter(partial_gram, "aux", scatter_dimension=0, tiled=True))
     return jnp.stack(pieces, axis=1)

time: 363 us -> 378 us (1.041)
  blocking collectives: 0 us -> 123 us
  waiting for transfers between devices: 243 us -> 139 us
  starting transfers between devices: 38.8 us -> 23.2 us
  local copies, waits for them, and re-layouts: 12.8 us -> 22.8 us
    all_to_all x0 -> x4, blocking collectives: none -> 123 us  [per_device(): lax.all_to_all(buffers[k * CAP + c], 'occ', split_axis=0, concat_axis=0,...]
    all_to_all x4, waiting for transfers between devices: 205 us -> 102 us  [per_device(): lax.all_to_all(buffers[k * CAP + c], 'occ', split_axis=0, concat_axis=0,...]
    all_to_all x4, starting transfers between devices: 30.6 us -> 15 us  [per_device(): lax.all_to_all(buffers[k * CAP + c], 'occ', split_axis=0, concat_axis=0,...]
    unnamed x1 -> x15, local copies, waits for them, and re-layouts: 3.3 us -> 13.3 us
  transfers between devices with their start and end apart: 9 -> 9, of which waited for: 5 -> 5; matrix products, arithmetic and copies ran while one was open for 3% -> 2% of each run, Pallas kernels for 11% -> 10%
where the time goes in v7:
time: 378 us; the launch traced here: 377 us
  waiting for transfers between devices  139 us (37%)
  blocking collectives  123 us (33%)
  Pallas kernels  47.5 us (13%)
  starting transfers between devices  23.2 us (6%)
  local copies, waits for them, and re-layouts  22.8 us (6%)
  between operations  13.3 us (4%)
  other arithmetic  8.49 us (2%)
    all_to_all x4, blocking collectives, per_device(): lax.all_to_all(buffers[k * CAP + c], 'occ', split_axis=0, concat_axis=0,...  123 us
    all_to_all x4, waiting for transfers between devices, per_device(): lax.all_to_all(buffers[k * CAP + c], 'occ', split_axis=0, concat_axis=0,...  102 us
    reduce_scatter x4, waiting for transfers between devices, per_device(): lax.psum_scatter(partial_gram, 'aux', scatter_dimension=0, tiled=True)  36.2 us
    pallas_call x4, Pallas kernels, domain_gram(): pl.pallas_call(_gram_kernel, grid_spec=grid_spec, out_shape=jax.ShapeDtyp...  32.9 us
    all_to_all x4, starting transfers between devices, per_device(): lax.all_to_all(buffers[k * CAP + c], 'occ', split_axis=0, concat_axis=0,...  15 us
    pallas_call x1, Pallas kernels, transform_into_slots(): pl.pallas_call(_transform_kernel, grid_spec=grid_spec, out_shape=[jax.Sha...  14.6 us
    unnamed x15, local copies, waits for them, and re-layouts  13.3 us
    all_to_all x1, starting transfers between devices, per_device(): lax.all_to_all(labels, 'occ', split_axis=0, concat_axis=0, tiled=True)  7.99 us
  transfers between devices with their start and end apart: 9, of which 5 were waited for; matrix products, arithmetic and copies ran while one was open for 2% of the time, Pallas kernels for 10%

profile of v7, /device:TPU:0, one launch (start us, length us, event | category | flops | bytes accessed | tf_op | source)
XLA Modules:
  0.0 377.0 jit_solution(9319599871166419395)
XLA Ops:
  14.4 8.0 %all-to-all-start = ((s32[16,4,2]{1,2,0:T(2,128)}), s32[16,4,2]{1,2,0:T(2,128)S(1)}, u32[]{:S(2)}, u32[]{:S(2)}) async-start(s32[16,4,2]{1,2,0:T(2,128)} %copy.16), calls=%async_computation | async-start | bytes 32768 | tf_op jit(solution)/shard_map/all_to_all | solution.py:170
  22.4 3.3 copy.17
  25.7 2.2 fusion.2.w_ref
  27.9 14.6 %shard_map.55 = (bf16[16,64,1024]{2,1,0:T(8,128)(2,1)}, bf16[16,64,1024]{2,1,0:T(8,128)(2,1)}, bf16[16,64,1024]{2,1,0:T(8,128)(2,1)}, bf16[16,64,1024]{2,1,0:T(8...) custom-call(s32[96]{0:T(128)} %get-tuple-element.25.out_ref, ...), custom_call_target="tpu_custom_call" | custom-call | flops 3221225472 | bytes 25165824 | tf_op jit(solution)/shard_map/pallas_call | solution.py:92
  42.5 35.1 %all_to_all.45.refs_0_ = bf16[16,64,1024]{2,1,0:T(8,128)(2,1)} all-to-all(bf16[16,64,1024]{2,1,0:T(8,128)(2,1)} %get-tuple-element.13), channel_id=1, replica_groups=mesh['aux'=8,'occ'=16] {'occ'}, dimensions={0} | all-to-all | bytes 4194304 | tf_op jit(solution)/shard_map/all_to_all | solution.py:178
  77.6 3.7 all-to-all-start.2
  83.2 26.3 %all-to-all-done.2.refs_1_ = bf16[16,64,1024]{2,1,0:T(8,128)(2,1)S(1)} async-done(((bf16[16,64,1024]{2,1,0:T(8,128)(2,1)}), bf16[16,64,1024]{2,1,0:T(8,128)(2,1)S(1)}, u32[]{:S(2)}, u32[]{:S(2)}) %all-to-all-start.2) | async-done | bytes 2097184 | tf_op jit(solution)/shard_map/all_to_all | solution.py:178
  110.8 8.1 %shard_map.56 = f32[1024,1024]{1,0:T(8,128)} custom-call(s32[32]{0:T(128)} %reshape_squeeze.12.lab_ref, bf16[16,64,1024]{2,1,0:T(8,128)(2,1)} %all_to_all.45.refs_0_, bf16[16,64,1024]{2,1,0:T(8,128)(2,1)} %copy-done), custom_call_target="tpu_custom_call" | custom-call | flops 2147483648 | bytes 8388608 | tf_op jit(solution)/shard_map/pallas_call | solution.py:136
  119.0 1.6 copy-done.6
  120.5 29.9 %all_to_all.46.refs_0_ = bf16[16,64,1024]{2,1,0:T(8,128)(2,1)} all-to-all(bf16[16,64,1024]{2,1,0:T(8,128)(2,1)S(1)} %copy-done.6), channel_id=1, replica_groups=mesh['aux'=8,'occ'=16] {'occ'}, dimensions={0} | all-to-all | bytes 4194304 | tf_op jit(solution)/shard_map/all_to_all | solution.py:178
  150.4 3.7 all-to-all-start.4
  154.9 25.5 %all-to-all-done.4.refs_1_ = bf16[16,64,1024]{2,1,0:T(8,128)(2,1)S(1)} async-done(((bf16[16,64,1024]{2,1,0:T(8,128)(2,1)}), bf16[16,64,1024]{2,1,0:T(8,128)(2,1)S(1)}, u32[]{:S(2)}, u32[]{:S(2)}) %all-to-all-start.4) | async-done | bytes 2097184 | tf_op jit(solution)/shard_map/all_to_all | solution.py:178
  181.7 8.4 %shard_map.57 = f32[1024,1024]{1,0:T(8,128)} custom-call(s32[32]{0:T(128)} %reshape_squeeze.13.lab_ref, bf16[16,64,1024]{2,1,0:T(8,128)(2,1)} %all_to_all.46.refs_0_, bf16[16,64,1024]{2,1,0:T(8,128)(2,1)} %copy-done.2), custom_call_target="tpu_custom_call" | custom-call | flops 2147483648 | bytes 8388608 | tf_op jit(solution)/shard_map/pallas_call | solution.py:136
  191.6 29.1 %all_to_all.47.refs_0_ = bf16[16,64,1024]{2,1,0:T(8,128)(2,1)} all-to-all(bf16[16,64,1024]{2,1,0:T(8,128)(2,1)S(1)} %copy-done.5), channel_id=1, replica_groups=mesh['aux'=8,'occ'=16] {'occ'}, dimensions={0} | all-to-all | bytes 4194304 | tf_op jit(solution)/shard_map/all_to_all | solution.py:178
  220.7 3.7 all-to-all-start.6
  225.1 25.4 %all-to-all-done.6.refs_1_ = bf16[16,64,1024]{2,1,0:T(8,128)(2,1)S(1)} async-done(((bf16[16,64,1024]{2,1,0:T(8,128)(2,1)}), bf16[16,64,1024]{2,1,0:T(8,128)(2,1)S(1)}, u32[]{:S(2)}, u32[]{:S(2)}) %all-to-all-start.6) | async-done | bytes 2097184 | tf_op jit(solution)/shard_map/all_to_all | solution.py:178
  251.8 8.2 %shard_map.58 = f32[1024,1024]{1,0:T(8,128)} custom-call(s32[32]{0:T(128)} %reshape_squeeze.14.lab_ref, bf16[16,64,1024]{2,1,0:T(8,128)(2,1)} %all_to_all.47.refs_0_, bf16[16,64,1024]{2,1,0:T(8,128)(2,1)} %copy-done.3), custom_call_target="tpu_custom_call" | custom-call | flops 2147483648 | bytes 8388608 | tf_op jit(solution)/shard_map/pallas_call | solution.py:136
  261.5 29.1 %all_to_all.48.refs_0_ = bf16[16,64,1024]{2,1,0:T(8,128)(2,1)} all-to-all(bf16[16,64,1024]{2,1,0:T(8,128)(2,1)S(1)} %copy-done.4), channel_id=1, replica_groups=mesh['aux'=8,'occ'=16] {'occ'}, dimensions={0} | all-to-all | bytes 4194304 | tf_op jit(solution)/shard_map/all_to_all | solution.py:178
  290.6 3.8 %all-to-all-start.8 = ((bf16[16,64,1024]{2,1,0:T(8,128)(2,1)}), bf16[16,64,1024]{2,1,0:T(8,128)(2,1)S(1)}, u32[]{:S(2)}, u32[]{:S(2)}) async-start(bf16[16,64,1024]{2,1,0:T(8,128)(2,1)} %get-tuple-element.20), calls=%async_computation.11 | async-start | bytes 4194304 | tf_op jit(solution)/shard_map/all_to_all | solution.py:178
  295.1 25.1 %all-to-all-done.8.refs_1_ = bf16[16,64,1024]{2,1,0:T(8,128)(2,1)S(1)} async-done(((bf16[16,64,1024]{2,1,0:T(8,128)(2,1)}), bf16[16,64,1024]{2,1,0:T(8,128)(2,1)S(1)}, u32[]{:S(2)}, u32[]{:S(2)}) %all-to-all-start.8) | async-done | bytes 2097184 | tf_op jit(solution)/shard_map/all_to_all | solution.py:178
  321.6 8.3 %shard_map.59 = f32[1024,1024]{1,0:T(8,128)} custom-call(s32[32]{0:T(128)} %reshape_squeeze.15.lab_ref, bf16[16,64,1024]{2,1,0:T(8,128)(2,1)} %all_to_all.48.refs_0_, bf16[16,64,1024]{2,1,0:T(8,128)(2,1)} %copy-done.1), custom_call_target="tpu_custom_call" | custom-call | flops 2147483648 | bytes 8388608 | tf_op jit(solution)/shard_map/pallas_call | solution.py:136
  329.9 36.2 %reduce-scatter.11.cloned.1.call-done = f32[128,1024]{1,0:T(8,128)} async-done(((f32[1024,1024]{1,0:T(8,128)}), f32[128,1024]{1,0:T(8,128)}) %reduce-scatter.11.cloned.1.call-update) | async-done | bytes 524304 | tf_op jit(solution)/shard_map/reduce_scatter | solution.py:182
  366.1 1.7 pad_maximum_fusion
  367.8 2.7 copy.19
  (40 shorter events, 20.2 us)
Async XLA Ops:
  14.4 28.1 %all-to-all-start = ((s32[16,4,2]{1,2,0:T(2,128)}), s32[16,4,2]{1,2,0:T(2,128)S(1)}, u32[]{:S(2)}, u32[]{:S(2)}) async-start(s32[16,4,2]{1,2,0:T(2,128)} %copy.16), calls=%async_computation | async-start | bytes 32768 | tf_op jit(solution)/shard_map/all_to_all | solution.py:170
  77.6 31.9 %all-to-all-start.2 = ((bf16[16,64,1024]{2,1,0:T(8,128)(2,1)}), bf16[16,64,1024]{2,1,0:T(8,128)(2,1)S(1)}, u32[]{:S(2)}, u32[]{:S(2)}) async-start(bf16[16,64,1024]{2,1,0:T(8,128)(2,1)} %get-tuple-element.14), calls=%async_computation.2 | async-start | bytes 4194304 | tf_op jit(solution)/shard_map/all_to_all | solution.py:178
  81.3 248.5 %reduce-scatter.5.cloned.1.call-start = ((), (), s32[]{:S(2)}) async-start(), calls=%async_computation.13 | async-start | bytes 4718592 | tf_op jit(solution)/shard_map/reduce_scatter | solution.py:182
  109.5 1.3 copy-start
  118.9 1.6 copy-start.6
  150.4 29.9 %all-to-all-start.4 = ((bf16[16,64,1024]{2,1,0:T(8,128)(2,1)}), bf16[16,64,1024]{2,1,0:T(8,128)(2,1)S(1)}, u32[]{:S(2)}, u32[]{:S(2)}) async-start(bf16[16,64,1024]{2,1,0:T(8,128)(2,1)} %get-tuple-element.16), calls=%async_computation.5 | async-start | bytes 4194304 | tf_op jit(solution)/shard_map/all_to_all | solution.py:178
  154.2 175.7 %reduce-scatter.7.cloned.1.call-start = ((), (), s32[]{:S(2)}) async-start(), calls=%async_computation.14 | async-start | bytes 4718592 | tf_op jit(solution)/shard_map/reduce_scatter | solution.py:182
  180.4 1.3 copy-start.2
  190.0 1.6 copy-start.5
  220.7 29.7 %all-to-all-start.6 = ((bf16[16,64,1024]{2,1,0:T(8,128)(2,1)}), bf16[16,64,1024]{2,1,0:T(8,128)(2,1)S(1)}, u32[]{:S(2)}, u32[]{:S(2)}) async-start(bf16[16,64,1024]{2,1,0:T(8,128)(2,1)} %get-tuple-element.18), calls=%async_computation.8 | async-start | bytes 4194304 | tf_op jit(solution)/shard_map/all_to_all | solution.py:178
  224.4 105.5 %reduce-scatter.9.cloned.1.call-start = ((), (), s32[]{:S(2)}) async-start(), calls=%async_computation.15 | async-start | bytes 4718592 | tf_op jit(solution)/shard_map/reduce_scatter | solution.py:182
  250.5 1.3 copy-start.3
  259.9 1.6 copy-start.4
  290.6 29.6 %all-to-all-start.8 = ((bf16[16,64,1024]{2,1,0:T(8,128)(2,1)}), bf16[16,64,1024]{2,1,0:T(8,128)(2,1)S(1)}, u32[]{:S(2)}, u32[]{:S(2)}) async-start(bf16[16,64,1024]{2,1,0:T(8,128)(2,1)} %get-tuple-element.20), calls=%async_computation.11 | async-start | bytes 4194304 | tf_op jit(solution)/shard_map/all_to_all | solution.py:178
  294.4 71.7 %reduce-scatter.11.cloned.1.call-start = ((), (), s32[]{:S(2)}) async-start(), calls=%async_computation.16 | async-start | bytes 4718592 | tf_op jit(solution)/shard_map/reduce_scatter | solution.py:182
  320.2 1.3 copy-start.1
Sparse Core Ops, SparseCore 0:
  119.1 37.3 reduce-scatter.4
  190.2 36.6 reduce-scatter.6
  260.1 36.9 reduce-scatter.8
  330.0 36.0 reduce-scatter.10

commit v8 on v6

--- a/solution.py
+++ b/solution.py
@@ -102,48 +102,68 @@
     )(out_index, slot_index, three_center, w2)
 
 
-def _gram_kernel(lab_ref, x_ref, o_ref, acc):
-    k = pl.program_id(0)
-    sources, cap = x_ref.shape[0], x_ref.shape[1]
-    per_source = lab_ref.shape[0] // sources
-    acc[...] = jnp.zeros_like(acc)
-    for s in range(sources):
-        for c in range(cap):
-            e = lab_ref[s * per_source + k * cap + c]
-
-            @pl.when(e >= 0)
-            def _():
-                acc[e] += x_ref[s, c].astype(jnp.float32)
-
+def _gram_kernel(lab_ref, x_ref, o_ref, acc, fs):
+    step = pl.program_id(0)
+    half, cap = x_ref.shape[0], x_ref.shape[1]
     dom, rows, width = acc.shape
-    fitted = acc[...].astype(x_ref.dtype).reshape(dom * rows, width)
-    o_ref[...] = lax.dot_general(
-        fitted, fitted, (((1,), (1,)), ((), ())), preferred_element_type=jnp.float32
-    )
+    block = o_ref.shape[0]
+
+    @pl.when(step == 0)
+    def _():
+        acc[...] = jnp.zeros_like(acc)
+
+    def accumulate(part):
+        for s in range(half):
+            for c in range(cap):
+                e = lab_ref[(part * half + s) * cap + c]
+
+                @pl.when(e >= 0)
+                def _():
+                    acc[e] += x_ref[s, c].astype(jnp.float32)
+
+    @pl.when(step == 0)
+    def _():
+        accumulate(0)
+
+    @pl.when(step == 1)
+    def _():
+        accumulate(1)
+        fs[...] = acc[...].astype(fs.dtype).reshape(dom * rows, width)
+
+    for part in range(2):
+        @pl.when(step == part + 1)
+        def _():
+            lhs = fs[part * block:(part + 1) * block, :]
+            o_ref[...] = lax.dot_general(
+                lhs, fs[...], (((1,), (1,)), ((), ())), preferred_element_type=jnp.float32
+            )
 
 
 def domain_gram(received, labels, dom):
     sources, slots, rows, width = received.shape
-    owned = slots // CAP
     domain_rows = dom * rows
+    half = sources // 2
     grid_spec = pltpu.PrefetchScalarGridSpec(
         num_scalar_prefetch=1,
-        grid=(owned,),
-        in_specs=[pl.BlockSpec((sources, CAP, rows, width), lambda k, lab: (0, k, 0, 0))],
-        out_specs=pl.BlockSpec((domain_rows, domain_rows), lambda k, lab: (0, k)),
-        scratch_shapes=[pltpu.VMEM((dom, rows, width), jnp.float32)],
+        grid=(3,),
+        in_specs=[pl.BlockSpec((half, CAP, rows, width), lambda i, lab: (jnp.minimum(i, 1), 0, 0, 0))],
+        out_specs=pl.BlockSpec((domain_rows // 2, domain_rows), lambda i, lab: (jnp.maximum(i - 1, 0), 0)),
+        scratch_shapes=[
+            pltpu.VMEM((dom, rows, width), jnp.float32),
+            pltpu.VMEM((domain_rows, width), received.dtype),
+        ],
     )
     return pl.pallas_call(
         _gram_kernel,
         grid_spec=grid_spec,
-        out_shape=jax.ShapeDtypeStruct((domain_rows, owned * domain_rows), jnp.float32),
+        out_shape=jax.ShapeDtypeStruct((domain_rows, domain_rows), jnp.float32),
         compiler_params=pltpu.CompilerParams(
             dimension_semantics=("arbitrary",), vmem_limit_bytes=60 * 1024 * 1024
         ),
         cost_estimate=pl.CostEstimate(
-            flops=2 * owned * domain_rows * domain_rows * width,
+            flops=2 * domain_rows * domain_rows * width,
             transcendentals=0,
-            bytes_accessed=sources * slots * rows * width * 2 + owned * domain_rows * domain_rows * 4,
+            bytes_accessed=sources * slots * rows * width * 2 + domain_rows * domain_rows * 4,
         ),
     )(labels.reshape(-1), received)
 

time: 363 us -> 359 us (0.989)
  Pallas kernels: 47.2 us -> 43.5 us
    pallas_call x4, Pallas kernels: 32.6 us -> 29 us  [domain_gram(): pl.pallas_call(_gram_kernel, grid_spec=grid_spec, out_shape=jax.ShapeDtyp...]
  transfers between devices with their start and end apart: 9 -> 9, of which waited for: 5 -> 5; matrix products, arithmetic and copies ran while one was open for 3% -> 3% of each run, Pallas kernels for 11% -> 10%
where the time goes in v8:
time: 359 us; the launch traced here: 358 us
  waiting for transfers between devices  242 us (67%)
  Pallas kernels  43.5 us (12%)
  starting transfers between devices  38.8 us (11%)
  between operations  13.3 us (4%)
  local copies, waits for them, and re-layouts  12.8 us (4%)
  other arithmetic  7.35 us (2%)
    all_to_all x4, waiting for transfers between devices, per_device(): lax.all_to_all(buffer, 'occ', split_axis=0, concat_axis=0, tiled=True)  205 us
    reduce_scatter x4, waiting for transfers between devices, per_device(): lax.psum_scatter(partial_gram, 'aux', scatter_dimension=0, tiled=True)  37.7 us
    all_to_all x4, starting transfers between devices, per_device(): lax.all_to_all(buffer, 'occ', split_axis=0, concat_axis=0, tiled=True)  30.6 us
    pallas_call x4, Pallas kernels, domain_gram(): pl.pallas_call(_gram_kernel, grid_spec=grid_spec, out_shape=jax.ShapeDtyp...  29 us
    pallas_call x1, Pallas kernels, transform_into_slots(): pl.pallas_call(_transform_kernel, grid_spec=grid_spec, out_shape=[jax.Sha...  14.6 us
    all_to_all x1, starting transfers between devices, per_device(): lax.all_to_all(labels, 'occ', split_axis=0, concat_axis=0, tiled=True)  7.99 us
  transfers between devices with their start and end apart: 9, of which 5 were waited for; matrix products, arithmetic and copies ran while one was open for 3% of the time, Pallas kernels for 10%

profile of v8, /device:TPU:0, one launch (start us, length us, event | category | flops | bytes accessed | tf_op | source)
XLA Modules:
  0.0 358.1 jit_solution(18001283294220935976)
XLA Ops:
  6.5 0.9 convert_reduce_fusion
  8.9 1.2 gather_fusion
  10.1 1.2 compare_select_fusion
  11.3 1.0 scatter_custom_fusion
  13.3 8.0 %all-to-all-start = ((s32[16,4,2]{1,2,0:T(2,128)}), s32[16,4,2]{1,2,0:T(2,128)S(1)}, u32[]{:S(2)}, u32[]{:S(2)}) async-start(s32[16,4,2]{1,2,0:T(2,128)} %copy.16), calls=%async_computation | async-start | bytes 32768 | tf_op jit(solution)/shard_map/all_to_all | solution.py:190
  21.3 3.3 copy.17
  24.6 2.2 fusion.2.w_ref
  26.8 14.6 %shard_map.55 = (bf16[32,64,1024]{2,1,0:T(8,128)(2,1)}, bf16[32,64,1024]{2,1,0:T(8,128)(2,1)}, bf16[32,64,1024]{2,1,0:T(8,128)(2,1)}, bf16[32,64,1024]{2,1,0:T(8,128)(2,1)}) custom-call(s32[96]{0:T(128)} %get-tuple-element.18.out_ref, s32[96]{0:T(128)} %get-tuple-element.19.slot_ref, bf16[96,64,1024]{2,1,0:T(8,128)(2,1)} %tc_ref.1, ...), custom_call_target="tpu_custom_call" | custom-call | flops 3221225472 | bytes 25165824 | tf_op jit(solution)/shard_map/pallas_call | solution.py:92
  41.3 7.2 %all-to-all-start.2 = ((bf16[16,128,1024]{2,1,0:T(8,128)(2,1)}), bf16[16,128,1024]{2,1,0:T(8,128)(2,1)}, u32[]{:S(2)}, u32[]{:S(2)}) async-start(bf16[16,128,1024]{2,1,0:T(8,128)(2,1)} %bitcast.17), calls=%async_computation.3 | async-start | bytes 8388608 | tf_op jit(solution)/shard_map/all_to_all | solution.py:198
  48.6 1.2 slice_reduce_fusion.3
  50.5 52.5 %all-to-all-done.2 = bf16[16,128,1024]{2,1,0:T(8,128)(2,1)} async-done(((bf16[16,128,1024]{2,1,0:T(8,128)(2,1)}), bf16[16,128,1024]{2,1,0:T(8,128)(2,1)}, u32[]{:S(2)}, u32[]{:S(2)}) %all-to-all-start.2) | async-done | bytes 4194336 | tf_op jit(solution)/shard_map/all_to_all | solution.py:198
  103.0 7.3 %shard_map.57 = f32[1024,1024]{1,0:T(8,128)} custom-call(s32[32]{0:T(128)} %reshape_squeeze.13.lab_ref, bf16[16,2,64,1024]{3,2,1,0:T(8,128)(2,1)} %bitcast.5.x_ref), custom_call_target="tpu_custom_call" | custom-call | flops 2147483648 | bytes 8388608 | tf_op jit(solution)/shard_map/pallas_call | solution.py:156
  110.3 11.4 %all-to-all-start.1 = ((bf16[16,128,1024]{2,1,0:T(8,128)(2,1)}), bf16[16,128,1024]{2,1,0:T(8,128)(2,1)}, u32[]{:S(2)}, u32[]{:S(2)}) async-start(bf16[16,128,1024]{2,1,0:T(8,128)(2,1)} %bitcast.16), calls=%async_computation.1 | async-start | bytes 8388608 | tf_op jit(solution)/shard_map/all_to_all | solution.py:198
  122.3 52.7 %all-to-all-done.1 = bf16[16,128,1024]{2,1,0:T(8,128)(2,1)} async-done(((bf16[16,128,1024]{2,1,0:T(8,128)(2,1)}), bf16[16,128,1024]{2,1,0:T(8,128)(2,1)}, u32[]{:S(2)}, u32[]{:S(2)}) %all-to-all-start.1) | async-done | bytes 4194336 | tf_op jit(solution)/shard_map/all_to_all | solution.py:198
  175.0 7.3 %shard_map.56 = f32[1024,1024]{1,0:T(8,128)} custom-call(s32[32]{0:T(128)} %reshape_squeeze.12.lab_ref, bf16[16,2,64,1024]{3,2,1,0:T(8,128)(2,1)} %bitcast.2.x_ref), custom_call_target="tpu_custom_call" | custom-call | flops 2147483648 | bytes 8388608 | tf_op jit(solution)/shard_map/pallas_call | solution.py:156
  182.3 4.7 %all-to-all-start.3 = ((bf16[16,128,1024]{2,1,0:T(8,128)(2,1)}), bf16[16,128,1024]{2,1,0:T(8,128)(2,1)}, u32[]{:S(2)}, u32[]{:S(2)}) async-start(bf16[16,128,1024]{2,1,0:T(8,128)(2,1)} %bitcast.15), calls=%async_computation.5 | async-start | bytes 8388608 | tf_op jit(solution)/shard_map/all_to_all | solution.py:198
  187.7 48.8 %all-to-all-done.3 = bf16[16,128,1024]{2,1,0:T(8,128)(2,1)} async-done(((bf16[16,128,1024]{2,1,0:T(8,128)(2,1)}), bf16[16,128,1024]{2,1,0:T(8,128)(2,1)}, u32[]{:S(2)}, u32[]{:S(2)}) %all-to-all-start.3) | async-done | bytes 4194336 | tf_op jit(solution)/shard_map/all_to_all | solution.py:198
  236.5 7.2 %shard_map.58 = f32[1024,1024]{1,0:T(8,128)} custom-call(s32[32]{0:T(128)} %reshape_squeeze.14.lab_ref, bf16[16,2,64,1024]{3,2,1,0:T(8,128)(2,1)} %bitcast.8.x_ref), custom_call_target="tpu_custom_call" | custom-call | flops 2147483648 | bytes 8388608 | tf_op jit(solution)/shard_map/pallas_call | solution.py:156
  243.7 7.3 %all-to-all-start.4 = ((bf16[16,128,1024]{2,1,0:T(8,128)(2,1)}), bf16[16,128,1024]{2,1,0:T(8,128)(2,1)}, u32[]{:S(2)}, u32[]{:S(2)}) async-start(bf16[16,128,1024]{2,1,0:T(8,128)(2,1)} %bitcast.14), calls=%async_computation.7 | async-start | bytes 8388608 | tf_op jit(solution)/shard_map/all_to_all | solution.py:198
  251.6 50.6 %all-to-all-done.4 = bf16[16,128,1024]{2,1,0:T(8,128)(2,1)} async-done(((bf16[16,128,1024]{2,1,0:T(8,128)(2,1)}), bf16[16,128,1024]{2,1,0:T(8,128)(2,1)}, u32[]{:S(2)}, u32[]{:S(2)}) %all-to-all-start.4) | async-done | bytes 4194336 | tf_op jit(solution)/shard_map/all_to_all | solution.py:198
  302.3 7.2 %shard_map.59 = f32[1024,1024]{1,0:T(8,128)} custom-call(s32[32]{0:T(128)} %reshape_squeeze.15.lab_ref, bf16[16,2,64,1024]{3,2,1,0:T(8,128)(2,1)} %bitcast.11.x_ref), custom_call_target="tpu_custom_call" | custom-call | flops 2147483648 | bytes 8388608 | tf_op jit(solution)/shard_map/pallas_call | solution.py:156
  309.6 37.7 %reduce-scatter.11.cloned.1.call-done = f32[128,1024]{1,0:T(8,128)} async-done(((f32[1024,1024]{1,0:T(8,128)}), f32[128,1024]{1,0:T(8,128)}) %reduce-scatter.11.cloned.1.call-update) | async-done | bytes 524304 | tf_op jit(solution)/shard_map/reduce_scatter | solution.py:201
  347.2 1.7 pad_maximum_fusion
  348.9 2.7 copy.19
  (21 shorter events, 5.1 us)
Async XLA Ops:
  13.3 28.0 %all-to-all-start = ((s32[16,4,2]{1,2,0:T(2,128)}), s32[16,4,2]{1,2,0:T(2,128)S(1)}, u32[]{:S(2)}, u32[]{:S(2)}) async-start(s32[16,4,2]{1,2,0:T(2,128)} %copy.16), calls=%async_computation | async-start | bytes 32768 | tf_op jit(solution)/shard_map/all_to_all | solution.py:190
  41.3 61.6 %all-to-all-start.2 = ((bf16[16,128,1024]{2,1,0:T(8,128)(2,1)}), bf16[16,128,1024]{2,1,0:T(8,128)(2,1)}, u32[]{:S(2)}, u32[]{:S(2)}) async-start(bf16[16,128,1024]{2,1,0:T(8,128)(2,1)} %bitcast.17), calls=%async_computation.3 | async-start | bytes 8388608 | tf_op jit(solution)/shard_map/all_to_all | solution.py:198
  48.6 261.0 %reduce-scatter.7.cloned.1.call-start = ((), (), s32[]{:S(2)}) async-start(), calls=%async_computation.10 | async-start | bytes 4718592 | tf_op jit(solution)/shard_map/reduce_scatter | solution.py:201
  110.3 64.8 %all-to-all-start.1 = ((bf16[16,128,1024]{2,1,0:T(8,128)(2,1)}), bf16[16,128,1024]{2,1,0:T(8,128)(2,1)}, u32[]{:S(2)}, u32[]{:S(2)}) async-start(bf16[16,128,1024]{2,1,0:T(8,128)(2,1)} %bitcast.16), calls=%async_computation.1 | async-start | bytes 8388608 | tf_op jit(solution)/shard_map/all_to_all | solution.py:198
  121.7 187.9 %reduce-scatter.5.cloned.1.call-start = ((), (), s32[]{:S(2)}) async-start(), calls=%async_computation.9 | async-start | bytes 4718592 | tf_op jit(solution)/shard_map/reduce_scatter | solution.py:201
  182.3 54.2 %all-to-all-start.3 = ((bf16[16,128,1024]{2,1,0:T(8,128)(2,1)}), bf16[16,128,1024]{2,1,0:T(8,128)(2,1)}, u32[]{:S(2)}, u32[]{:S(2)}) async-start(bf16[16,128,1024]{2,1,0:T(8,128)(2,1)} %bitcast.15), calls=%async_computation.5 | async-start | bytes 8388608 | tf_op jit(solution)/shard_map/all_to_all | solution.py:198
  187.0 122.5 %reduce-scatter.9.cloned.1.call-start = ((), (), s32[]{:S(2)}) async-start(), calls=%async_computation.11 | async-start | bytes 4718592 | tf_op jit(solution)/shard_map/reduce_scatter | solution.py:201
  243.7 58.6 %all-to-all-start.4 = ((bf16[16,128,1024]{2,1,0:T(8,128)(2,1)}), bf16[16,128,1024]{2,1,0:T(8,128)(2,1)}, u32[]{:S(2)}, u32[]{:S(2)}) async-start(bf16[16,128,1024]{2,1,0:T(8,128)(2,1)} %bitcast.14), calls=%async_computation.7 | async-start | bytes 8388608 | tf_op jit(solution)/shard_map/all_to_all | solution.py:198
  251.0 96.3 %reduce-scatter.11.cloned.1.call-start = ((), (), s32[]{:S(2)}) async-start(), calls=%async_computation.12 | async-start | bytes 4718592 | tf_op jit(solution)/shard_map/reduce_scatter | solution.py:201
Sparse Core Ops, SparseCore 0:
  110.4 44.5 reduce-scatter.6
  182.4 37.2 reduce-scatter.4
  243.8 40.4 reduce-scatter.8
  309.6 37.5 reduce-scatter.10

commit v9 on v8

--- a/solution.py
+++ b/solution.py
@@ -176,16 +176,15 @@
     owned_tiles = tile_count // occ_count
     slot_count = tile_count * CAP
     tile_ids = jnp.arange(tile_count, dtype=jnp.int32)
-    position = jnp.sum(
-        jnp.where(owner_order[None, :] == tile_ids[:, None], tile_ids[None, :], 0), axis=1
-    )
+    pos = jnp.sum(jnp.where(owner_order[None, :] == target[:, None], tile_ids[None, :], 0), axis=1)
     pair_ids = jnp.arange(pair_count, dtype=jnp.int32)
     earlier = (target[:, None] == target[None, :]) & (pair_ids[:, None] > pair_ids[None, :])
     rank = jnp.sum(earlier.astype(jnp.int32), axis=1)
-    pos = jnp.take(position, target)
     out_index = pos % owned_tiles
     slot_index = (pos // owned_tiles) * CAP + rank
-    labels = jnp.full((slot_count,), -1, jnp.int32).at[out_index * occ_count * CAP + slot_index].set(domain_slot)
+    tile_slot = out_index * occ_count * CAP + slot_index
+    slot_ids = jnp.arange(slot_count, dtype=jnp.int32)
+    labels = jnp.sum(jnp.where(tile_slot[None, :] == slot_ids[:, None], domain_slot[None, :] + 1, 0), axis=1) - 1
     labels = labels.reshape(owned_tiles, occ_count, CAP).transpose(1, 0, 2)
     received_labels = lax.all_to_all(labels, "occ", split_axis=0, concat_axis=0, tiled=True)
 

time: 359 us -> 356 us (level)
  no operation moved by 1% of the time
where the time goes in v9:
time: 356 us; the launch traced here: 355 us
  waiting for transfers between devices  242 us (68%)
  Pallas kernels  43.8 us (12%)
  starting transfers between devices  38.4 us (11%)
  between operations  13.3 us (4%)
  local copies, waits for them, and re-layouts  10.5 us (3%)
  other arithmetic  6.8 us (2%)
    all_to_all x4, waiting for transfers between devices, per_device(): lax.all_to_all(buffer, 'occ', split_axis=0, concat_axis=0, tiled=True)  205 us
    reduce_scatter x4, waiting for transfers between devices, per_device(): lax.psum_scatter(partial_gram, 'aux', scatter_dimension=0, tiled=True)  37.7 us
    all_to_all x4, starting transfers between devices, per_device(): lax.all_to_all(buffer, 'occ', split_axis=0, concat_axis=0, tiled=True)  30 us
    pallas_call x4, Pallas kernels, domain_gram(): pl.pallas_call(_gram_kernel, grid_spec=grid_spec, out_shape=jax.ShapeDtyp...  29.3 us
    pallas_call x1, Pallas kernels, transform_into_slots(): pl.pallas_call(_transform_kernel, grid_spec=grid_spec, out_shape=[jax.Sha...  14.5 us
    all_to_all x1, starting transfers between devices, per_device(): lax.all_to_all(labels, 'occ', split_axis=0, concat_axis=0, tiled=True)  7.99 us
  transfers between devices with their start and end apart: 9, of which 5 were waited for; matrix products, arithmetic and copies ran while one was open for 3% of the time, Pallas kernels for 10%

profile of v9, /device:TPU:0, one launch (start us, length us, event | category | flops | bytes accessed | tf_op | source)
XLA Modules:
  0.0 355.2 jit_solution(7736935463238914776)
XLA Ops:
  6.5 0.9 convert_reduce_fusion
  7.4 0.8 select_reduce_fusion.1
  8.2 1.2 multiply_add_fusion.1
  9.7 0.8 copy.16
  10.5 8.0 %all-to-all-start = ((s32[16,4,2]{1,2,0:T(2,128)}), s32[16,4,2]{1,2,0:T(2,128)S(1)}, u32[]{:S(2)}, u32[]{:S(2)}) async-start(s32[16,4,2]{1,2,0:T(2,128)} %copy.16), calls=%async_computation | async-start | bytes 32768 | tf_op jit(solution)/shard_map/all_to_all | solution.py:189
  18.5 3.3 copy.17
  21.8 2.2 fusion.2.w_ref
  23.9 14.5 %shard_map.55 = (bf16[32,64,1024]{2,1,0:T(8,128)(2,1)}, bf16[32,64,1024]{2,1,0:T(8,128)(2,1)}, bf16[32,64,1024]{2,1,0:T(8,128)(2,1)}, bf16[32,64,1024]{2,1,0:T(8,128)(2,1)}) custom-call(s32[96]{0:T(128)} %get-tuple-element.18.out_ref, s32[96]{0:T(128)} %get-tuple-element.19.slot_ref, bf16[96,64,1024]{2,1,0:T(8,128)(2,1)} %tc_ref.1, ...), custom_call_target="tpu_custom_call" | custom-call | flops 3221225472 | bytes 25165824 | tf_op jit(solution)/shard_map/pallas_call | solution.py:92
  38.5 7.3 %all-to-all-start.2 = ((bf16[16,128,1024]{2,1,0:T(8,128)(2,1)}), bf16[16,128,1024]{2,1,0:T(8,128)(2,1)}, u32[]{:S(2)}, u32[]{:S(2)}) async-start(bf16[16,128,1024]{2,1,0:T(8,128)(2,1)} %bitcast.16), calls=%async_computation.3 | async-start | bytes 8388608 | tf_op jit(solution)/shard_map/all_to_all | solution.py:197
  45.8 1.2 slice_reduce_fusion.3
  47.6 52.5 %all-to-all-done.2 = bf16[16,128,1024]{2,1,0:T(8,128)(2,1)} async-done(((bf16[16,128,1024]{2,1,0:T(8,128)(2,1)}), bf16[16,128,1024]{2,1,0:T(8,128)(2,1)}, u32[]{:S(2)}, u32[]{:S(2)}) %all-to-all-start.2) | async-done | bytes 4194336 | tf_op jit(solution)/shard_map/all_to_all | solution.py:197
  100.1 7.4 %shard_map.57 = f32[1024,1024]{1,0:T(8,128)} custom-call(s32[32]{0:T(128)} %reshape_squeeze.13.lab_ref, bf16[16,2,64,1024]{3,2,1,0:T(8,128)(2,1)} %bitcast.5.x_ref), custom_call_target="tpu_custom_call" | custom-call | flops 2147483648 | bytes 8388608 | tf_op jit(solution)/shard_map/pallas_call | solution.py:156
  107.6 11.2 %all-to-all-start.1 = ((bf16[16,128,1024]{2,1,0:T(8,128)(2,1)}), bf16[16,128,1024]{2,1,0:T(8,128)(2,1)}, u32[]{:S(2)}, u32[]{:S(2)}) async-start(bf16[16,128,1024]{2,1,0:T(8,128)(2,1)} %bitcast.15), calls=%async_computation.1 | async-start | bytes 8388608 | tf_op jit(solution)/shard_map/all_to_all | solution.py:197
  119.5 52.7 %all-to-all-done.1 = bf16[16,128,1024]{2,1,0:T(8,128)(2,1)} async-done(((bf16[16,128,1024]{2,1,0:T(8,128)(2,1)}), bf16[16,128,1024]{2,1,0:T(8,128)(2,1)}, u32[]{:S(2)}, u32[]{:S(2)}) %all-to-all-start.1) | async-done | bytes 4194336 | tf_op jit(solution)/shard_map/all_to_all | solution.py:197
  172.2 7.2 %shard_map.56 = f32[1024,1024]{1,0:T(8,128)} custom-call(s32[32]{0:T(128)} %reshape_squeeze.12.lab_ref, bf16[16,2,64,1024]{3,2,1,0:T(8,128)(2,1)} %bitcast.2.x_ref), custom_call_target="tpu_custom_call" | custom-call | flops 2147483648 | bytes 8388608 | tf_op jit(solution)/shard_map/pallas_call | solution.py:156
  179.4 4.5 %all-to-all-start.3 = ((bf16[16,128,1024]{2,1,0:T(8,128)(2,1)}), bf16[16,128,1024]{2,1,0:T(8,128)(2,1)}, u32[]{:S(2)}, u32[]{:S(2)}) async-start(bf16[16,128,1024]{2,1,0:T(8,128)(2,1)} %bitcast.14), calls=%async_computation.5 | async-start | bytes 8388608 | tf_op jit(solution)/shard_map/all_to_all | solution.py:197
  184.8 48.9 %all-to-all-done.3 = bf16[16,128,1024]{2,1,0:T(8,128)(2,1)} async-done(((bf16[16,128,1024]{2,1,0:T(8,128)(2,1)}), bf16[16,128,1024]{2,1,0:T(8,128)(2,1)}, u32[]{:S(2)}, u32[]{:S(2)}) %all-to-all-start.3) | async-done | bytes 4194336 | tf_op jit(solution)/shard_map/all_to_all | solution.py:197
  233.7 7.3 %shard_map.58 = f32[1024,1024]{1,0:T(8,128)} custom-call(s32[32]{0:T(128)} %reshape_squeeze.14.lab_ref, bf16[16,2,64,1024]{3,2,1,0:T(8,128)(2,1)} %bitcast.8.x_ref), custom_call_target="tpu_custom_call" | custom-call | flops 2147483648 | bytes 8388608 | tf_op jit(solution)/shard_map/pallas_call | solution.py:156
  241.0 7.0 %all-to-all-start.4 = ((bf16[16,128,1024]{2,1,0:T(8,128)(2,1)}), bf16[16,128,1024]{2,1,0:T(8,128)(2,1)}, u32[]{:S(2)}, u32[]{:S(2)}) async-start(bf16[16,128,1024]{2,1,0:T(8,128)(2,1)} %bitcast.13), calls=%async_computation.7 | async-start | bytes 8388608 | tf_op jit(solution)/shard_map/all_to_all | solution.py:197
  248.6 50.6 %all-to-all-done.4 = bf16[16,128,1024]{2,1,0:T(8,128)(2,1)} async-done(((bf16[16,128,1024]{2,1,0:T(8,128)(2,1)}), bf16[16,128,1024]{2,1,0:T(8,128)(2,1)}, u32[]{:S(2)}, u32[]{:S(2)}) %all-to-all-start.4) | async-done | bytes 4194336 | tf_op jit(solution)/shard_map/all_to_all | solution.py:197
  299.2 7.4 %shard_map.59 = f32[1024,1024]{1,0:T(8,128)} custom-call(s32[32]{0:T(128)} %reshape_squeeze.15.lab_ref, bf16[16,2,64,1024]{3,2,1,0:T(8,128)(2,1)} %bitcast.11.x_ref), custom_call_target="tpu_custom_call" | custom-call | flops 2147483648 | bytes 8388608 | tf_op jit(solution)/shard_map/pallas_call | solution.py:156
  306.7 37.6 %reduce-scatter.11.cloned.1.call-done = f32[128,1024]{1,0:T(8,128)} async-done(((f32[1024,1024]{1,0:T(8,128)}), f32[128,1024]{1,0:T(8,128)}) %reduce-scatter.11.cloned.1.call-update) | async-done | bytes 524304 | tf_op jit(solution)/shard_map/reduce_scatter | solution.py:200
  344.3 1.7 pad_maximum_fusion
  346.0 2.7 copy.19
  (19 shorter events, 3.1 us)
Async XLA Ops:
  10.5 28.0 %all-to-all-start = ((s32[16,4,2]{1,2,0:T(2,128)}), s32[16,4,2]{1,2,0:T(2,128)S(1)}, u32[]{:S(2)}, u32[]{:S(2)}) async-start(s32[16,4,2]{1,2,0:T(2,128)} %copy.16), calls=%async_computation | async-start | bytes 32768 | tf_op jit(solution)/shard_map/all_to_all | solution.py:189
  38.5 61.7 %all-to-all-start.2 = ((bf16[16,128,1024]{2,1,0:T(8,128)(2,1)}), bf16[16,128,1024]{2,1,0:T(8,128)(2,1)}, u32[]{:S(2)}, u32[]{:S(2)}) async-start(bf16[16,128,1024]{2,1,0:T(8,128)(2,1)} %bitcast.16), calls=%async_computation.3 | async-start | bytes 8388608 | tf_op jit(solution)/shard_map/all_to_all | solution.py:197
  45.7 260.9 %reduce-scatter.7.cloned.1.call-start = ((), (), s32[]{:S(2)}) async-start(), calls=%async_computation.10 | async-start | bytes 4718592 | tf_op jit(solution)/shard_map/reduce_scatter | solution.py:200
  107.6 64.6 %all-to-all-start.1 = ((bf16[16,128,1024]{2,1,0:T(8,128)(2,1)}), bf16[16,128,1024]{2,1,0:T(8,128)(2,1)}, u32[]{:S(2)}, u32[]{:S(2)}) async-start(bf16[16,128,1024]{2,1,0:T(8,128)(2,1)} %bitcast.15), calls=%async_computation.1 | async-start | bytes 8388608 | tf_op jit(solution)/shard_map/all_to_all | solution.py:197
  118.8 187.8 %reduce-scatter.5.cloned.1.call-start = ((), (), s32[]{:S(2)}) async-start(), calls=%async_computation.9 | async-start | bytes 4718592 | tf_op jit(solution)/shard_map/reduce_scatter | solution.py:200
  179.4 54.3 %all-to-all-start.3 = ((bf16[16,128,1024]{2,1,0:T(8,128)(2,1)}), bf16[16,128,1024]{2,1,0:T(8,128)(2,1)}, u32[]{:S(2)}, u32[]{:S(2)}) async-start(bf16[16,128,1024]{2,1,0:T(8,128)(2,1)} %bitcast.14), calls=%async_computation.5 | async-start | bytes 8388608 | tf_op jit(solution)/shard_map/all_to_all | solution.py:197
  184.0 122.7 %reduce-scatter.9.cloned.1.call-start = ((), (), s32[]{:S(2)}) async-start(), calls=%async_computation.11 | async-start | bytes 4718592 | tf_op jit(solution)/shard_map/reduce_scatter | solution.py:200
  241.0 58.2 %all-to-all-start.4 = ((bf16[16,128,1024]{2,1,0:T(8,128)(2,1)}), bf16[16,128,1024]{2,1,0:T(8,128)(2,1)}, u32[]{:S(2)}, u32[]{:S(2)}) async-start(bf16[16,128,1024]{2,1,0:T(8,128)(2,1)} %bitcast.13), calls=%async_computation.7 | async-start | bytes 8388608 | tf_op jit(solution)/shard_map/all_to_all | solution.py:197
  248.0 96.3 %reduce-scatter.11.cloned.1.call-start = ((), (), s32[]{:S(2)}) async-start(), calls=%async_computation.12 | async-start | bytes 4718592 | tf_op jit(solution)/shard_map/reduce_scatter | solution.py:200
Sparse Core Ops, SparseCore 0:
  107.7 44.4 reduce-scatter.6
  179.6 37.3 reduce-scatter.4
  241.1 40.2 reduce-scatter.8
  306.7 37.5 reduce-scatter.10

commit v10 on v9

--- a/solution.py
+++ b/solution.py
@@ -1,3 +1,4 @@
+import functools
 import math
 
 import jax
@@ -102,7 +103,7 @@
     )(out_index, slot_index, three_center, w2)
 
 
-def _gram_kernel(lab_ref, x_ref, o_ref, acc, fs):
+def _gram_kernel(lab_ref, x_ref, o_ref, acc, fs, *, tile, per_source):
     step = pl.program_id(0)
     half, cap = x_ref.shape[0], x_ref.shape[1]
     dom, rows, width = acc.shape
@@ -115,7 +116,7 @@
     def accumulate(part):
         for s in range(half):
             for c in range(cap):
-                e = lab_ref[(part * half + s) * cap + c]
+                e = lab_ref[(part * half + s) * per_source + tile * cap + c]
 
                 @pl.when(e >= 0)
                 def _():
@@ -139,7 +140,7 @@
             )
 
 
-def domain_gram(received, labels, dom):
+def domain_gram(received, labels, dom, tile):
     sources, slots, rows, width = received.shape
     domain_rows = dom * rows
     half = sources // 2
@@ -154,7 +155,7 @@
         ],
     )
     return pl.pallas_call(
-        _gram_kernel,
+        functools.partial(_gram_kernel, tile=tile, per_source=labels.size // sources),
         grid_spec=grid_spec,
         out_shape=jax.ShapeDtypeStruct((domain_rows, domain_rows), jnp.float32),
         compiler_params=pltpu.CompilerParams(
@@ -196,7 +197,7 @@
         buffer = buffers[k].reshape(occ_count, CAP * tile_width, col_width)
         received = lax.all_to_all(buffer, "occ", split_axis=0, concat_axis=0, tiled=True)
         received = received.reshape(occ_count, CAP, tile_width, col_width)
-        partial_gram = domain_gram(received, received_labels[:, k], DOM)
+        partial_gram = domain_gram(received, received_labels, DOM, k)
         pieces.append(lax.psum_scatter(partial_gram, "aux", scatter_dimension=0, tiled=True))
     return jnp.stack(pieces, axis=1)
 

time: 356 us -> 339 us (0.952)
  blocking collectives: 0 us -> 162 us
  waiting for transfers between devices: 242 us -> 88.8 us
  starting transfers between devices: 38.4 us -> 15.5 us
    all_to_all x0 -> x3, blocking collectives: none -> 162 us  [per_device(): lax.all_to_all(buffer, 'occ', split_axis=0, concat_axis=0, tiled=True)]
    all_to_all x4 -> x1, waiting for transfers between devices: 205 us -> 53.5 us  [per_device(): lax.all_to_all(buffer, 'occ', split_axis=0, concat_axis=0, tiled=True)]
    all_to_all x4 -> x1, starting transfers between devices: 30 us -> 7.32 us  [per_device(): lax.all_to_all(buffer, 'occ', split_axis=0, concat_axis=0, tiled=True)]
  transfers between devices with their start and end apart: 9 -> 6, of which waited for: 5 -> 2; matrix products, arithmetic and copies ran while one was open for 3% -> 2% of each run, Pallas kernels for 10% -> 11%
where the time goes in v10:
time: 339 us; the launch traced here: 338 us
  blocking collectives  162 us (48%)
  waiting for transfers between devices  88.8 us (26%)
  Pallas kernels  43.4 us (13%)
  starting transfers between devices  15.5 us (5%)
  between operations  13.2 us (4%)
  local copies, waits for them, and re-layouts  7.78 us (2%)
  other arithmetic  6.8 us (2%)
    all_to_all x3, blocking collectives, per_device(): lax.all_to_all(buffer, 'occ', split_axis=0, concat_axis=0, tiled=True)  162 us
    all_to_all x1, waiting for transfers between devices, per_device(): lax.all_to_all(buffer, 'occ', split_axis=0, concat_axis=0, tiled=True)  53.5 us
    reduce_scatter x4, waiting for transfers between devices, per_device(): lax.psum_scatter(partial_gram, 'aux', scatter_dimension=0, tiled=True)  35.3 us
    pallas_call x4, Pallas kernels, domain_gram(): pl.pallas_call(functools.partial(_gram_kernel, tile=tile, per_source=labe...  28.9 us
    pallas_call x1, Pallas kernels, transform_into_slots(): pl.pallas_call(_transform_kernel, grid_spec=grid_spec, out_shape=[jax.Sha...  14.5 us
    all_to_all x1, starting transfers between devices, per_device(): lax.all_to_all(labels, 'occ', split_axis=0, concat_axis=0, tiled=True)  7.99 us
    all_to_all x1, starting transfers between devices, per_device(): lax.all_to_all(buffer, 'occ', split_axis=0, concat_axis=0, tiled=True)  7.32 us
  transfers between devices with their start and end apart: 6, of which 2 were waited for; matrix products, arithmetic and copies ran while one was open for 2% of the time, Pallas kernels for 11%

profile of v10, /device:TPU:0, one launch (start us, length us, event | category | flops | bytes accessed | tf_op | source)
XLA Modules:
  0.0 337.7 jit_solution(17355802258148081329)
XLA Ops:
  6.5 0.9 convert_reduce_fusion
  7.4 0.8 select_reduce_fusion.1
  8.2 1.2 multiply_add_fusion.1
  9.4 0.1 select_reduce_fusion
  9.5 0.1 sub.14
  9.7 0.8 copy.19
  10.5 8.0 %all-to-all-start = ((s32[16,4,2]{1,2,0:T(2,128)}), s32[16,4,2]{1,2,0:T(2,128)S(1)}, u32[]{:S(2)}, u32[]{:S(2)}) async-start(s32[16,4,2]{1,2,0:T(2,128)} %copy.19), calls=%async_computation | async-start | bytes 32768 | tf_op jit(solution)/shard_map/all_to_all | solution.py:190
  18.5 3.3 copy.21
  21.8 2.2 fusion.2.w_ref
  23.9 14.5 %shard_map.55 = (bf16[32,64,1024]{2,1,0:T(8,128)(2,1)}, bf16[32,64,1024]{2,1,0:T(8,128)(2,1)}, bf16[32,64,1024]{2,1,0:T(8,128)(2,1)}, bf16[32,64,1024]{2,1,0:T(8,128)(2,1)}) custom-call(s32[96]{0:T(128)} %get-tuple-element.14.out_ref, s32[96]{0:T(128)} %get-tuple-element.15.slot_ref, bf16[96,64,1024]{2,1,0:T(8,128)(2,1)} %tc_ref.1, ...), custom_call_target="tpu_custom_call" | custom-call | flops 3221225472 | bytes 25165824 | tf_op jit(solution)/shard_map/pallas_call | solution.py:93
  38.5 7.3 %all-to-all-start.2 = ((bf16[16,128,1024]{2,1,0:T(8,128)(2,1)}), bf16[16,128,1024]{2,1,0:T(8,128)(2,1)}, u32[]{:S(2)}, u32[]{:S(2)}) async-start(bf16[16,128,1024]{2,1,0:T(8,128)(2,1)} %bitcast.19), calls=%async_computation.3 | async-start | bytes 8388608 | tf_op jit(solution)/shard_map/all_to_all | solution.py:198
  45.8 0.2 copy.20
  46.0 0.7 reshape.73.lab_ref
  46.7 53.5 %all-to-all-done.2 = bf16[16,128,1024]{2,1,0:T(8,128)(2,1)} async-done(((bf16[16,128,1024]{2,1,0:T(8,128)(2,1)}), bf16[16,128,1024]{2,1,0:T(8,128)(2,1)}, u32[]{:S(2)}, u32[]{:S(2)}) %all-to-all-start.2) | async-done | bytes 4194336 | tf_op jit(solution)/shard_map/all_to_all | solution.py:198
  100.2 7.3 %shard_map.57 = f32[1024,1024]{1,0:T(8,128)} custom-call(s32[128]{0:T(128)} %reshape.73.lab_ref, bf16[16,2,64,1024]{3,2,1,0:T(8,128)(2,1)} %bitcast.5.x_ref), custom_call_target="tpu_custom_call" | custom-call | flops 2147483648 | bytes 8388608 | tf_op jit(solution)/shard_map/pallas_call | solution.py:157
  107.5 60.3 %all_to_all.25 = bf16[16,128,1024]{2,1,0:T(8,128)(2,1)} all-to-all(bf16[16,128,1024]{2,1,0:T(8,128)(2,1)} %bitcast.18), channel_id=1, replica_groups=mesh['aux'=8,'occ'=16] {'occ'}, dimensions={0} | all-to-all | bytes 8388608 | tf_op jit(solution)/shard_map/all_to_all | solution.py:198
  167.8 7.3 %shard_map.56 = f32[1024,1024]{1,0:T(8,128)} custom-call(s32[128]{0:T(128)} %reshape.73.lab_ref, bf16[16,2,64,1024]{3,2,1,0:T(8,128)(2,1)} %bitcast.14), custom_call_target="tpu_custom_call" | custom-call | flops 2147483648 | bytes 8388608 | tf_op jit(solution)/shard_map/pallas_call | solution.py:157
  175.2 51.6 %all_to_all.26 = bf16[16,128,1024]{2,1,0:T(8,128)(2,1)} all-to-all(bf16[16,128,1024]{2,1,0:T(8,128)(2,1)} %bitcast.17), channel_id=1, replica_groups=mesh['aux'=8,'occ'=16] {'occ'}, dimensions={0} | all-to-all | bytes 8388608 | tf_op jit(solution)/shard_map/all_to_all | solution.py:198
  226.7 7.1 %shard_map.58 = f32[1024,1024]{1,0:T(8,128)} custom-call(s32[128]{0:T(128)} %reshape.73.lab_ref, bf16[16,2,64,1024]{3,2,1,0:T(8,128)(2,1)} %bitcast.15), custom_call_target="tpu_custom_call" | custom-call | flops 2147483648 | bytes 8388608 | tf_op jit(solution)/shard_map/pallas_call | solution.py:157
  233.9 50.4 %all_to_all.27 = bf16[16,128,1024]{2,1,0:T(8,128)(2,1)} all-to-all(bf16[16,128,1024]{2,1,0:T(8,128)(2,1)} %bitcast.16), channel_id=1, replica_groups=mesh['aux'=8,'occ'=16] {'occ'}, dimensions={0} | all-to-all | bytes 8388608 | tf_op jit(solution)/shard_map/all_to_all | solution.py:198
  284.3 7.2 %shard_map.59 = f32[1024,1024]{1,0:T(8,128)} custom-call(s32[128]{0:T(128)} %reshape.73.lab_ref, bf16[16,2,64,1024]{3,2,1,0:T(8,128)(2,1)} %bitcast.13), custom_call_target="tpu_custom_call" | custom-call | flops 2147483648 | bytes 8388608 | tf_op jit(solution)/shard_map/pallas_call | solution.py:157
  291.7 35.2 %reduce-scatter.11.cloned.1.call-done = f32[128,1024]{1,0:T(8,128)} async-done(((f32[1024,1024]{1,0:T(8,128)}), f32[128,1024]{1,0:T(8,128)}) %reduce-scatter.11.cloned.1.call-update) | async-done | bytes 524304 | tf_op jit(solution)/shard_map/reduce_scatter | solution.py:201
  326.9 1.7 pad_maximum_fusion
  328.5 2.7 copy.23
  (13 shorter events, 0.3 us)
Async XLA Ops:
  10.5 28.0 %all-to-all-start = ((s32[16,4,2]{1,2,0:T(2,128)}), s32[16,4,2]{1,2,0:T(2,128)S(1)}, u32[]{:S(2)}, u32[]{:S(2)}) async-start(s32[16,4,2]{1,2,0:T(2,128)} %copy.19), calls=%async_computation | async-start | bytes 32768 | tf_op jit(solution)/shard_map/all_to_all | solution.py:190
  38.5 61.7 %all-to-all-start.2 = ((bf16[16,128,1024]{2,1,0:T(8,128)(2,1)}), bf16[16,128,1024]{2,1,0:T(8,128)(2,1)}, u32[]{:S(2)}, u32[]{:S(2)}) async-start(bf16[16,128,1024]{2,1,0:T(8,128)(2,1)} %bitcast.19), calls=%async_computation.3 | async-start | bytes 8388608 | tf_op jit(solution)/shard_map/all_to_all | solution.py:198
  45.8 245.8 %reduce-scatter.7.cloned.1.call-start = ((), (), s32[]{:S(2)}) async-start(), calls=%async_computation.10 | async-start | bytes 4718592 | tf_op jit(solution)/shard_map/reduce_scatter | solution.py:201
  107.5 184.1 %reduce-scatter.5.cloned.1.call-start = ((), (), s32[]{:S(2)}) async-start(), calls=%async_computation.9 | async-start | bytes 4718592 | tf_op jit(solution)/shard_map/reduce_scatter | solution.py:201
  175.1 116.5 %reduce-scatter.9.cloned.1.call-start = ((), (), s32[]{:S(2)}) async-start(), calls=%async_computation.11 | async-start | bytes 4718592 | tf_op jit(solution)/shard_map/reduce_scatter | solution.py:201
  233.9 93.0 %reduce-scatter.11.cloned.1.call-start = ((), (), s32[]{:S(2)}) async-start(), calls=%async_computation.12 | async-start | bytes 4718592 | tf_op jit(solution)/shard_map/reduce_scatter | solution.py:201
Sparse Core Ops, SparseCore 0:
  107.6 44.5 reduce-scatter.6
  175.3 36.7 reduce-scatter.4
  234.0 37.0 reduce-scatter.8
  291.7 35.1 reduce-scatter.10

commit v11 on v10

--- a/solution.py
+++ b/solution.py
@@ -187,8 +187,8 @@
     slot_ids = jnp.arange(slot_count, dtype=jnp.int32)
     labels = jnp.sum(jnp.where(tile_slot[None, :] == slot_ids[:, None], domain_slot[None, :] + 1, 0), axis=1) - 1
     labels = labels.reshape(owned_tiles, occ_count, CAP).transpose(1, 0, 2)
-    received_labels = lax.all_to_all(labels, "occ", split_axis=0, concat_axis=0, tiled=True)
-
+
+    labels, three_center = lax.optimization_barrier((labels, three_center))
     buffers = transform_into_slots(
         three_center, coefficients, out_index, slot_index, [occ_count * CAP] * owned_tiles
     )
@@ -196,6 +196,9 @@
     for k in range(owned_tiles):
         buffer = buffers[k].reshape(occ_count, CAP * tile_width, col_width)
         received = lax.all_to_all(buffer, "occ", split_axis=0, concat_axis=0, tiled=True)
+        if k == 0:
+            labels, received = lax.optimization_barrier((labels, received))
+            received_labels = lax.all_to_all(labels, "occ", split_axis=0, concat_axis=0, tiled=True)
         received = received.reshape(occ_count, CAP, tile_width, col_width)
         partial_gram = domain_gram(received, received_labels, DOM, k)
         pieces.append(lax.psum_scatter(partial_gram, "aux", scatter_dimension=0, tiled=True))

time: 339 us -> 333 us (0.982)
  blocking collectives: 162 us -> 226 us
  waiting for transfers between devices: 88.8 us -> 36.3 us
  starting transfers between devices: 15.5 us -> 0.13 us
    all_to_all x2 -> x0, waiting for transfers between devices: 53.5 us -> none  [the longest x1 53.5 us: per_device(): lax.all_to_all(buffer, 'occ', split_axis=0, concat_axis=0, tiled=True)]
    all_to_all x3 -> x4, blocking collectives: 162 us -> 214 us  [per_device(): lax.all_to_all(buffer, 'occ', split_axis=0, concat_axis=0, tiled=True)]
    all_to_all x2 -> x0, starting transfers between devices: 15.3 us -> none  [the longest x1 7.99 us: per_device(): lax.all_to_all(labels, 'occ', split_axis=0, concat_axis=0, tiled=True)]
    all_to_all x0 -> x1, blocking collectives: none -> 11.6 us  [per_device(): lax.all_to_all(labels, 'occ', split_axis=0, concat_axis=0, tiled=True)]
  transfers between devices with their start and end apart: 6 -> 4, of which waited for: 2 -> 1; matrix products, arithmetic and copies ran while one was open for 2% -> 0% of each run, Pallas kernels for 11% -> 7%
where the time goes in v11:
time: 333 us
  blocking collectives  226 us (68%)
  Pallas kernels  43.6 us (13%)
  waiting for transfers between devices  36.3 us (11%)
  between operations  13.2 us (4%)
  local copies, waits for them, and re-layouts  7.18 us (2%)
  other arithmetic  6.8 us (2%)
    all_to_all x4, blocking collectives, per_device(): lax.all_to_all(buffer, 'occ', split_axis=0, concat_axis=0, tiled=True)  214 us
    reduce_scatter x4, waiting for transfers between devices, per_device(): lax.psum_scatter(partial_gram, 'aux', scatter_dimension=0, tiled=True)  36.2 us
    pallas_call x4, Pallas kernels, domain_gram(): pl.pallas_call(functools.partial(_gram_kernel, tile=tile, per_source=labe...  29.1 us
    pallas_call x1, Pallas kernels, transform_into_slots(): pl.pallas_call(_transform_kernel, grid_spec=grid_spec, out_shape=[jax.Sha...  14.5 us
    all_to_all x1, blocking collectives, per_device(): lax.all_to_all(labels, 'occ', split_axis=0, concat_axis=0, tiled=True)  11.6 us
  transfers between devices with their start and end apart: 4, of which 1 were waited for; matrix products, arithmetic and copies ran while one was open for 0% of the time, Pallas kernels for 7%

profile of v11, /device:TPU:0, one launch (start us, length us, event | category | flops | bytes accessed | tf_op | source)
XLA Modules:
  0.0 332.7 jit_solution(586754032018488716)
XLA Ops:
  6.5 0.9 convert_reduce_fusion
  7.5 0.8 select_reduce_fusion.1
  8.2 1.2 multiply_add_fusion.1
  9.4 0.1 select_reduce_fusion
  9.5 0.1 sub.14
  9.7 3.3 copy.19
  13.0 2.2 fusion.2.w_ref
  15.2 14.5 %shard_map.55 = (bf16[32,64,1024]{2,1,0:T(8,128)(2,1)}, bf16[32,64,1024]{2,1,0:T(8,128)(2,1)}, bf16[32,64,1024]{2,1,0:T(8,128)(2,1)}, bf16[32,64,1024]{2,1,0:T(8,128)(2,1)}) custom-call(s32[96]{0:T(128)} %get-tuple-element.22.out_ref, s32[96]{0:T(128)} %get-tuple-element.23.slot_ref, bf16[96,64,1024]{2,1,0:T(8,128)(2,1)} %tc_ref, ...), custom_call_target="tpu_custom_call" | custom-call | flops 3221225472 | bytes 25165824 | tf_op jit(solution)/shard_map/pallas_call | solution.py:93
  29.7 58.8 %all_to_all.25 = bf16[16,128,1024]{2,1,0:T(8,128)(2,1)} all-to-all(bf16[16,128,1024]{2,1,0:T(8,128)(2,1)} %bitcast.20), channel_id=1, replica_groups=mesh['aux'=8,'occ'=16] {'occ'}, dimensions={0} | all-to-all | bytes 8388608 | tf_op jit(solution)/shard_map/all_to_all | solution.py:198
  88.5 0.2 copy.21
  88.7 11.6 %all_to_all.26 = s32[16,4,2]{1,2,0:T(2,128)S(1)} all-to-all(s32[16,4,2]{1,2,0:T(2,128)S(1)} %copy.21), channel_id=1, replica_groups=mesh['aux'=8,'occ'=16] {'occ'}, dimensions={0} | all-to-all | bytes 1024 | tf_op jit(solution)/shard_map/all_to_all | solution.py:201
  100.3 0.2 copy.22
  100.5 0.7 reshape.74.lab_ref
  101.2 7.4 %shard_map.56 = f32[1024,1024]{1,0:T(8,128)} custom-call(s32[128]{0:T(128)} %reshape.74.lab_ref, bf16[16,2,64,1024]{3,2,1,0:T(8,128)(2,1)} %bitcast.13), custom_call_target="tpu_custom_call" | custom-call | flops 2147483648 | bytes 8388608 | tf_op jit(solution)/shard_map/pallas_call | solution.py:157
  108.6 0.0 reduce-scatter.7.cloned.1.call-start
  108.7 53.1 %all_to_all.27 = bf16[16,128,1024]{2,1,0:T(8,128)(2,1)} all-to-all(bf16[16,128,1024]{2,1,0:T(8,128)(2,1)} %bitcast.19), channel_id=1, replica_groups=mesh['aux'=8,'occ'=16] {'occ'}, dimensions={0} | all-to-all | bytes 8388608 | tf_op jit(solution)/shard_map/all_to_all | solution.py:198
  161.8 7.2 %shard_map.57 = f32[1024,1024]{1,0:T(8,128)} custom-call(s32[128]{0:T(128)} %reshape.74.lab_ref, bf16[16,2,64,1024]{3,2,1,0:T(8,128)(2,1)} %bitcast.15), custom_call_target="tpu_custom_call" | custom-call | flops 2147483648 | bytes 8388608 | tf_op jit(solution)/shard_map/pallas_call | solution.py:157
  169.0 51.8 %all_to_all.28 = bf16[16,128,1024]{2,1,0:T(8,128)(2,1)} all-to-all(bf16[16,128,1024]{2,1,0:T(8,128)(2,1)} %bitcast.18), channel_id=1, replica_groups=mesh['aux'=8,'occ'=16] {'occ'}, dimensions={0} | all-to-all | bytes 8388608 | tf_op jit(solution)/shard_map/all_to_all | solution.py:198
  220.8 7.2 %shard_map.58 = f32[1024,1024]{1,0:T(8,128)} custom-call(s32[128]{0:T(128)} %reshape.74.lab_ref, bf16[16,2,64,1024]{3,2,1,0:T(8,128)(2,1)} %bitcast.16), custom_call_target="tpu_custom_call" | custom-call | flops 2147483648 | bytes 8388608 | tf_op jit(solution)/shard_map/pallas_call | solution.py:157
  228.1 50.2 %all_to_all.29 = bf16[16,128,1024]{2,1,0:T(8,128)(2,1)} all-to-all(bf16[16,128,1024]{2,1,0:T(8,128)(2,1)} %bitcast.17), channel_id=1, replica_groups=mesh['aux'=8,'occ'=16] {'occ'}, dimensions={0} | all-to-all | bytes 8388608 | tf_op jit(solution)/shard_map/all_to_all | solution.py:198
  278.4 7.2 %shard_map.59 = f32[1024,1024]{1,0:T(8,128)} custom-call(s32[128]{0:T(128)} %reshape.74.lab_ref, bf16[16,2,64,1024]{3,2,1,0:T(8,128)(2,1)} %bitcast.14), custom_call_target="tpu_custom_call" | custom-call | flops 2147483648 | bytes 8388608 | tf_op jit(solution)/shard_map/pallas_call | solution.py:157
  285.7 36.2 %reduce-scatter.11.cloned.1.call-done = f32[128,1024]{1,0:T(8,128)} async-done(((f32[1024,1024]{1,0:T(8,128)}), f32[128,1024]{1,0:T(8,128)}) %reduce-scatter.11.cloned.1.call-update) | async-done | bytes 524304 | tf_op jit(solution)/shard_map/reduce_scatter | solution.py:204
  321.9 1.7 pad_maximum_fusion
  323.5 2.7 copy.23
  (11 shorter events, 0.2 us)
Async XLA Ops:
  6.5 279.1 %reduce-scatter.5.cloned.1.call-start = ((), (), s32[]{:S(2)}) async-start(), calls=%async_computation.9 | async-start | bytes 4718592 | tf_op jit(solution)/shard_map/reduce_scatter | solution.py:204
  108.6 177.0 %reduce-scatter.7.cloned.1.call-start = ((), (), s32[]{:S(2)}) async-start(), calls=%async_computation.10 | async-start | bytes 4718592 | tf_op jit(solution)/shard_map/reduce_scatter | solution.py:204
  169.0 116.7 %reduce-scatter.9.cloned.1.call-start = ((), (), s32[]{:S(2)}) async-start(), calls=%async_computation.11 | async-start | bytes 4718592 | tf_op jit(solution)/shard_map/reduce_scatter | solution.py:204
  228.1 93.8 %reduce-scatter.11.cloned.1.call-start = ((), (), s32[]{:S(2)}) async-start(), calls=%async_computation.12 | async-start | bytes 4718592 | tf_op jit(solution)/shard_map/reduce_scatter | solution.py:204
Sparse Core Ops, SparseCore 0:
  108.7 36.5 reduce-scatter.4
  169.1 36.9 reduce-scatter.6
  228.2 36.7 reduce-scatter.8
  285.7 36.0 reduce-scatter.10

commit v12 on v10

--- a/solution.py
+++ b/solution.py
@@ -187,8 +187,10 @@
     slot_ids = jnp.arange(slot_count, dtype=jnp.int32)
     labels = jnp.sum(jnp.where(tile_slot[None, :] == slot_ids[:, None], domain_slot[None, :] + 1, 0), axis=1) - 1
     labels = labels.reshape(owned_tiles, occ_count, CAP).transpose(1, 0, 2)
+
     received_labels = lax.all_to_all(labels, "occ", split_axis=0, concat_axis=0, tiled=True)
-
+    label_table = received_labels.reshape(-1)
+    label_table, three_center = lax.optimization_barrier((label_table, three_center))
     buffers = transform_into_slots(
         three_center, coefficients, out_index, slot_index, [occ_count * CAP] * owned_tiles
     )
@@ -197,7 +199,7 @@
         buffer = buffers[k].reshape(occ_count, CAP * tile_width, col_width)
         received = lax.all_to_all(buffer, "occ", split_axis=0, concat_axis=0, tiled=True)
         received = received.reshape(occ_count, CAP, tile_width, col_width)
-        partial_gram = domain_gram(received, received_labels, DOM, k)
+        partial_gram = domain_gram(received, label_table, DOM, k)
         pieces.append(lax.psum_scatter(partial_gram, "aux", scatter_dimension=0, tiled=True))
     return jnp.stack(pieces, axis=1)
 

time: 339 us -> 329 us (0.971)
  waiting for transfers between devices: 88.8 us -> 38.8 us
  blocking collectives: 162 us -> 210 us
  starting transfers between devices: 15.5 us -> 8.16 us
    all_to_all x1 -> x0, waiting for transfers between devices: 53.5 us -> none  [per_device(): lax.all_to_all(buffer, 'occ', split_axis=0, concat_axis=0, tiled=True)]
    all_to_all x3 -> x4, blocking collectives: 162 us -> 210 us  [per_device(): lax.all_to_all(buffer, 'occ', split_axis=0, concat_axis=0, tiled=True)]
    all_to_all x1 -> x0, starting transfers between devices: 7.32 us -> none  [per_device(): lax.all_to_all(buffer, 'occ', split_axis=0, concat_axis=0, tiled=True)]
  transfers between devices with their start and end apart: 6 -> 5, of which waited for: 2 -> 2; matrix products, arithmetic and copies ran while one was open for 2% -> 2% of each run, Pallas kernels for 11% -> 7%
where the time goes in v12:
time: 329 us; the launch traced here: 328 us
  blocking collectives  210 us (64%)
  Pallas kernels  43.9 us (13%)
  waiting for transfers between devices  38.8 us (12%)
  between operations  13.2 us (4%)
  starting transfers between devices  8.16 us (2%)
  local copies, waits for them, and re-layouts  7.78 us (2%)
  other arithmetic  6.8 us (2%)
    all_to_all x4, blocking collectives, per_device(): lax.all_to_all(buffer, 'occ', split_axis=0, concat_axis=0, tiled=True)  210 us
    reduce_scatter x4, waiting for transfers between devices, per_device(): lax.psum_scatter(partial_gram, 'aux', scatter_dimension=0, tiled=True)  36.6 us
    pallas_call x4, Pallas kernels, domain_gram(): pl.pallas_call(functools.partial(_gram_kernel, tile=tile, per_source=labe...  29.4 us
    pallas_call x1, Pallas kernels, transform_into_slots(): pl.pallas_call(_transform_kernel, grid_spec=grid_spec, out_shape=[jax.Sha...  14.5 us
    all_to_all x1, starting transfers between devices, per_device(): lax.all_to_all(labels, 'occ', split_axis=0, concat_axis=0, tiled=True)  7.99 us
  transfers between devices with their start and end apart: 5, of which 2 were waited for; matrix products, arithmetic and copies ran while one was open for 2% of the time, Pallas kernels for 7%

profile of v12, /device:TPU:0, one launch (start us, length us, event | category | flops | bytes accessed | tf_op | source)
XLA Modules:
  0.0 328.1 jit_solution(5255022313284999351)
XLA Ops:
  6.5 0.9 convert_reduce_fusion
  7.4 0.8 select_reduce_fusion.1
  8.2 1.2 multiply_add_fusion.1
  9.4 0.1 select_reduce_fusion
  9.5 0.1 sub.14
  9.7 0.8 copy.19
  10.5 8.0 %all-to-all-start = ((s32[16,4,2]{1,2,0:T(2,128)}), s32[16,4,2]{1,2,0:T(2,128)S(1)}, u32[]{:S(2)}, u32[]{:S(2)}) async-start(s32[16,4,2]{1,2,0:T(2,128)} %copy.19), calls=%async_computation | async-start | bytes 32768 | tf_op jit(solution)/shard_map/all_to_all | solution.py:191
  18.5 3.3 %copy.21 = bf16[96,64,64]{2,1,0:T(8,128)(2,1)S(1)} copy(bf16[96,64,64]{0,2,1:T(8,128)(2,1)} %param.6) | data formatting | bytes 1572864 | tf_op args[1]
  21.8 2.2 fusion.2.w_ref
  24.0 2.1 all-to-all-done
  26.1 0.2 copy.20
  26.3 0.7 reshape.70.lab_ref
  26.9 14.5 %shard_map.55 = (bf16[32,64,1024]{2,1,0:T(8,128)(2,1)}, bf16[32,64,1024]{2,1,0:T(8,128)(2,1)}, bf16[32,64,1024]{2,1,0:T(8,128)(2,1)}, bf16[32,64,1024]{2,1,0:T(8,128)(2,1)}) custom-call(s32[96]{0:T(128)} %get-tuple-element.18.out_ref, s32[96]{0:T(128)} %get-tuple-element.19.slot_ref, bf16[96,64,1024]{2,1,0:T(8,128)(2,1)} %tc_ref, ...), custom_call_target="tpu_custom_call" | custom-call | flops 3221225472 | bytes 25165824 | tf_op jit(solution)/shard_map/pallas_call | solution.py:93
  41.5 55.5 %all_to_all.25 = bf16[16,128,1024]{2,1,0:T(8,128)(2,1)} all-to-all(bf16[16,128,1024]{2,1,0:T(8,128)(2,1)} %bitcast.20), channel_id=1, replica_groups=mesh['aux'=8,'occ'=16] {'occ'}, dimensions={0} | all-to-all | bytes 8388608 | tf_op jit(solution)/shard_map/all_to_all | solution.py:200
  97.0 7.4 %shard_map.57 = f32[1024,1024]{1,0:T(8,128)} custom-call(s32[128]{0:T(128)} %reshape.70.lab_ref, bf16[16,2,64,1024]{3,2,1,0:T(8,128)(2,1)} %bitcast.14), custom_call_target="tpu_custom_call" | custom-call | flops 2147483648 | bytes 8388608 | tf_op jit(solution)/shard_map/pallas_call | solution.py:157
  104.5 53.3 %all_to_all.26 = bf16[16,128,1024]{2,1,0:T(8,128)(2,1)} all-to-all(bf16[16,128,1024]{2,1,0:T(8,128)(2,1)} %bitcast.19), channel_id=1, replica_groups=mesh['aux'=8,'occ'=16] {'occ'}, dimensions={0} | all-to-all | bytes 8388608 | tf_op jit(solution)/shard_map/all_to_all | solution.py:200
  157.8 7.4 %shard_map.56 = f32[1024,1024]{1,0:T(8,128)} custom-call(s32[128]{0:T(128)} %reshape.70.lab_ref, bf16[16,2,64,1024]{3,2,1,0:T(8,128)(2,1)} %bitcast.15), custom_call_target="tpu_custom_call" | custom-call | flops 2147483648 | bytes 8388608 | tf_op jit(solution)/shard_map/pallas_call | solution.py:157
  165.3 51.1 %all_to_all.27 = bf16[16,128,1024]{2,1,0:T(8,128)(2,1)} all-to-all(bf16[16,128,1024]{2,1,0:T(8,128)(2,1)} %bitcast.18), channel_id=1, replica_groups=mesh['aux'=8,'occ'=16] {'occ'}, dimensions={0} | all-to-all | bytes 8388608 | tf_op jit(solution)/shard_map/all_to_all | solution.py:200
  216.4 7.4 %shard_map.58 = f32[1024,1024]{1,0:T(8,128)} custom-call(s32[128]{0:T(128)} %reshape.70.lab_ref, bf16[16,2,64,1024]{3,2,1,0:T(8,128)(2,1)} %bitcast.16), custom_call_target="tpu_custom_call" | custom-call | flops 2147483648 | bytes 8388608 | tf_op jit(solution)/shard_map/pallas_call | solution.py:157
  223.8 49.6 %all_to_all.28 = bf16[16,128,1024]{2,1,0:T(8,128)(2,1)} all-to-all(bf16[16,128,1024]{2,1,0:T(8,128)(2,1)} %bitcast.17), channel_id=1, replica_groups=mesh['aux'=8,'occ'=16] {'occ'}, dimensions={0} | all-to-all | bytes 8388608 | tf_op jit(solution)/shard_map/all_to_all | solution.py:200
  273.5 7.1 %shard_map.59 = f32[1024,1024]{1,0:T(8,128)} custom-call(s32[128]{0:T(128)} %reshape.70.lab_ref, bf16[16,2,64,1024]{3,2,1,0:T(8,128)(2,1)} %bitcast.13), custom_call_target="tpu_custom_call" | custom-call | flops 2147483648 | bytes 8388608 | tf_op jit(solution)/shard_map/pallas_call | solution.py:157
  280.7 36.6 %reduce-scatter.11.cloned.1.call-done = f32[128,1024]{1,0:T(8,128)} async-done(((f32[1024,1024]{1,0:T(8,128)}), f32[128,1024]{1,0:T(8,128)}) %reduce-scatter.11.cloned.1.call-update) | async-done | bytes 524304 | tf_op jit(solution)/shard_map/reduce_scatter | solution.py:203
  317.3 1.7 pad_maximum_fusion
  318.9 2.7 copy.23
  (12 shorter events, 0.3 us)
Async XLA Ops:
  10.5 15.6 %all-to-all-start = ((s32[16,4,2]{1,2,0:T(2,128)}), s32[16,4,2]{1,2,0:T(2,128)S(1)}, u32[]{:S(2)}, u32[]{:S(2)}) async-start(s32[16,4,2]{1,2,0:T(2,128)} %copy.19), calls=%async_computation | async-start | bytes 32768 | tf_op jit(solution)/shard_map/all_to_all | solution.py:191
  18.5 262.2 %reduce-scatter.7.cloned.1.call-start = ((), (), s32[]{:S(2)}) async-start(), calls=%async_computation.10 | async-start | bytes 4718592 | tf_op jit(solution)/shard_map/reduce_scatter | solution.py:203
  104.4 176.3 %reduce-scatter.5.cloned.1.call-start = ((), (), s32[]{:S(2)}) async-start(), calls=%async_computation.9 | async-start | bytes 4718592 | tf_op jit(solution)/shard_map/reduce_scatter | solution.py:203
  165.2 115.5 %reduce-scatter.9.cloned.1.call-start = ((), (), s32[]{:S(2)}) async-start(), calls=%async_computation.11 | async-start | bytes 4718592 | tf_op jit(solution)/shard_map/reduce_scatter | solution.py:203
  223.8 93.5 %reduce-scatter.11.cloned.1.call-start = ((), (), s32[]{:S(2)}) async-start(), calls=%async_computation.12 | async-start | bytes 4718592 | tf_op jit(solution)/shard_map/reduce_scatter | solution.py:203
Sparse Core Ops, SparseCore 0:
  104.5 36.7 reduce-scatter.6
  165.3 36.5 reduce-scatter.4
  223.9 37.2 reduce-scatter.8
  280.8 36.4 reduce-scatter.10

commit v13 on v12

--- a/solution.py
+++ b/solution.py
@@ -66,7 +66,7 @@
 def transform_into_slots(three_center, coefficients, out_index, slot_index, group_slots):
     pair_count, rows, width = three_center.shape
     tile = coefficients.shape[1]
-    steps = 8 if pair_count % 8 == 0 else 1
+    steps = 4 if pair_count % 4 == 0 else 1
     per = pair_count // steps
     zeros = jnp.zeros_like(coefficients)
     w2 = jnp.concatenate(

time: 329 us -> 327 us (level)
  no operation moved by 1% of the time
where the time goes in v13:
time: 327 us; the launch traced here: 326 us
  blocking collectives  211 us (65%)
  Pallas kernels  41.6 us (13%)
  waiting for transfers between devices  37.7 us (12%)
  between operations  13.2 us (4%)
  starting transfers between devices  8.16 us (2%)
  local copies, waits for them, and re-layouts  7.78 us (2%)
  other arithmetic  6.8 us (2%)
    all_to_all x4, blocking collectives, per_device(): lax.all_to_all(buffer, 'occ', split_axis=0, concat_axis=0, tiled=True)  211 us
    reduce_scatter x4, waiting for transfers between devices, per_device(): lax.psum_scatter(partial_gram, 'aux', scatter_dimension=0, tiled=True)  35.5 us
    pallas_call x4, Pallas kernels, domain_gram(): pl.pallas_call(functools.partial(_gram_kernel, tile=tile, per_source=labe...  29 us
    pallas_call x1, Pallas kernels, transform_into_slots(): pl.pallas_call(_transform_kernel, grid_spec=grid_spec, out_shape=[jax.Sha...  12.6 us
    all_to_all x1, starting transfers between devices, per_device(): lax.all_to_all(labels, 'occ', split_axis=0, concat_axis=0, tiled=True)  7.99 us
  transfers between devices with their start and end apart: 5, of which 2 were waited for; matrix products, arithmetic and copies ran while one was open for 2% of the time, Pallas kernels for 7%

profile of v13, /device:TPU:0, one launch (start us, length us, event | category | flops | bytes accessed | tf_op | source)
XLA Modules:
  0.0 326.0 jit_solution(13988402407747931005)
XLA Ops:
  6.5 0.9 convert_reduce_fusion
  7.4 0.8 select_reduce_fusion.1
  8.2 1.2 multiply_add_fusion.1
  9.4 0.1 select_reduce_fusion
  9.5 0.1 sub.14
  9.7 0.8 copy.19
  10.5 8.0 %all-to-all-start = ((s32[16,4,2]{1,2,0:T(2,128)}), s32[16,4,2]{1,2,0:T(2,128)S(1)}, u32[]{:S(2)}, u32[]{:S(2)}) async-start(s32[16,4,2]{1,2,0:T(2,128)} %copy.19), calls=%async_computation | async-start | bytes 32768 | tf_op jit(solution)/shard_map/all_to_all | solution.py:191
  18.5 3.3 %copy.21 = bf16[96,64,64]{2,1,0:T(8,128)(2,1)S(1)} copy(bf16[96,64,64]{0,2,1:T(8,128)(2,1)} %param.6) | data formatting | bytes 1572864 | tf_op args[1]
  21.8 2.2 fusion.2.w_ref
  24.0 2.1 all-to-all-done
  26.1 0.2 copy.20
  26.3 0.7 reshape.70.lab_ref
  26.9 12.6 %shard_map.55 = (bf16[32,64,1024]{2,1,0:T(8,128)(2,1)}, bf16[32,64,1024]{2,1,0:T(8,128)(2,1)}, bf16[32,64,1024]{2,1,0:T(8,128)(2,1)}, bf16[32,64,1024]{2,1,0:T(8,128)(2,1)}) custom-call(s32[96]{0:T(128)} %get-tuple-element.18.out_ref, s32[96]{0:T(128)} %get-tuple-element.19.slot_ref, bf16[96,64,1024]{2,1,0:T(8,128)(2,1)} %tc_ref, ...), custom_call_target="tpu_custom_call" | custom-call | flops 3221225472 | bytes 25165824 | tf_op jit(solution)/shard_map/pallas_call | solution.py:93
  39.5 55.5 %all_to_all.25 = bf16[16,128,1024]{2,1,0:T(8,128)(2,1)} all-to-all(bf16[16,128,1024]{2,1,0:T(8,128)(2,1)} %bitcast.20), channel_id=1, replica_groups=mesh['aux'=8,'occ'=16] {'occ'}, dimensions={0} | all-to-all | bytes 8388608 | tf_op jit(solution)/shard_map/all_to_all | solution.py:200
  95.0 7.3 %shard_map.57 = f32[1024,1024]{1,0:T(8,128)} custom-call(s32[128]{0:T(128)} %reshape.70.lab_ref, bf16[16,2,64,1024]{3,2,1,0:T(8,128)(2,1)} %bitcast.14), custom_call_target="tpu_custom_call" | custom-call | flops 2147483648 | bytes 8388608 | tf_op jit(solution)/shard_map/pallas_call | solution.py:157
  102.4 53.4 %all_to_all.26 = bf16[16,128,1024]{2,1,0:T(8,128)(2,1)} all-to-all(bf16[16,128,1024]{2,1,0:T(8,128)(2,1)} %bitcast.19), channel_id=1, replica_groups=mesh['aux'=8,'occ'=16] {'occ'}, dimensions={0} | all-to-all | bytes 8388608 | tf_op jit(solution)/shard_map/all_to_all | solution.py:200
  155.8 7.2 %shard_map.56 = f32[1024,1024]{1,0:T(8,128)} custom-call(s32[128]{0:T(128)} %reshape.70.lab_ref, bf16[16,2,64,1024]{3,2,1,0:T(8,128)(2,1)} %bitcast.15), custom_call_target="tpu_custom_call" | custom-call | flops 2147483648 | bytes 8388608 | tf_op jit(solution)/shard_map/pallas_call | solution.py:157
  163.1 51.5 %all_to_all.27 = bf16[16,128,1024]{2,1,0:T(8,128)(2,1)} all-to-all(bf16[16,128,1024]{2,1,0:T(8,128)(2,1)} %bitcast.18), channel_id=1, replica_groups=mesh['aux'=8,'occ'=16] {'occ'}, dimensions={0} | all-to-all | bytes 8388608 | tf_op jit(solution)/shard_map/all_to_all | solution.py:200
  214.7 7.3 %shard_map.58 = f32[1024,1024]{1,0:T(8,128)} custom-call(s32[128]{0:T(128)} %reshape.70.lab_ref, bf16[16,2,64,1024]{3,2,1,0:T(8,128)(2,1)} %bitcast.16), custom_call_target="tpu_custom_call" | custom-call | flops 2147483648 | bytes 8388608 | tf_op jit(solution)/shard_map/pallas_call | solution.py:157
  222.0 50.4 %all_to_all.28 = bf16[16,128,1024]{2,1,0:T(8,128)(2,1)} all-to-all(bf16[16,128,1024]{2,1,0:T(8,128)(2,1)} %bitcast.17), channel_id=1, replica_groups=mesh['aux'=8,'occ'=16] {'occ'}, dimensions={0} | all-to-all | bytes 8388608 | tf_op jit(solution)/shard_map/all_to_all | solution.py:200
  272.4 7.2 %shard_map.59 = f32[1024,1024]{1,0:T(8,128)} custom-call(s32[128]{0:T(128)} %reshape.70.lab_ref, bf16[16,2,64,1024]{3,2,1,0:T(8,128)(2,1)} %bitcast.13), custom_call_target="tpu_custom_call" | custom-call | flops 2147483648 | bytes 8388608 | tf_op jit(solution)/shard_map/pallas_call | solution.py:157
  279.7 35.5 %reduce-scatter.11.cloned.1.call-done = f32[128,1024]{1,0:T(8,128)} async-done(((f32[1024,1024]{1,0:T(8,128)}), f32[128,1024]{1,0:T(8,128)}) %reduce-scatter.11.cloned.1.call-update) | async-done | bytes 524304 | tf_op jit(solution)/shard_map/reduce_scatter | solution.py:203
  315.2 1.7 pad_maximum_fusion
  316.8 2.7 copy.23
  (12 shorter events, 0.3 us)
Async XLA Ops:
  10.5 15.6 %all-to-all-start = ((s32[16,4,2]{1,2,0:T(2,128)}), s32[16,4,2]{1,2,0:T(2,128)S(1)}, u32[]{:S(2)}, u32[]{:S(2)}) async-start(s32[16,4,2]{1,2,0:T(2,128)} %copy.19), calls=%async_computation | async-start | bytes 32768 | tf_op jit(solution)/shard_map/all_to_all | solution.py:191
  18.5 261.2 %reduce-scatter.7.cloned.1.call-start = ((), (), s32[]{:S(2)}) async-start(), calls=%async_computation.10 | async-start | bytes 4718592 | tf_op jit(solution)/shard_map/reduce_scatter | solution.py:203
  102.3 177.3 %reduce-scatter.5.cloned.1.call-start = ((), (), s32[]{:S(2)}) async-start(), calls=%async_computation.9 | async-start | bytes 4718592 | tf_op jit(solution)/shard_map/reduce_scatter | solution.py:203
  163.1 116.6 %reduce-scatter.9.cloned.1.call-start = ((), (), s32[]{:S(2)}) async-start(), calls=%async_computation.11 | async-start | bytes 4718592 | tf_op jit(solution)/shard_map/reduce_scatter | solution.py:203
  222.0 93.2 %reduce-scatter.11.cloned.1.call-start = ((), (), s32[]{:S(2)}) async-start(), calls=%async_computation.12 | async-start | bytes 4718592 | tf_op jit(solution)/shard_map/reduce_scatter | solution.py:203
Sparse Core Ops, SparseCore 0:
  102.5 36.7 reduce-scatter.6
  163.2 36.7 reduce-scatter.4
  222.1 36.8 reduce-scatter.8
  279.7 35.3 reduce-scatter.10

commit v14 on v13

--- a/solution.py
+++ b/solution.py
@@ -201,7 +201,7 @@
         received = received.reshape(occ_count, CAP, tile_width, col_width)
         partial_gram = domain_gram(received, label_table, DOM, k)
         pieces.append(lax.psum_scatter(partial_gram, "aux", scatter_dimension=0, tiled=True))
-    return jnp.stack(pieces, axis=1)
+    return jnp.concatenate(pieces, axis=1).reshape(pieces[0].shape[0], owned_tiles, -1)
 
 
 def solution(mesh):

time: 327 us -> 327 us (level)
  no operation moved by 1% of the time
where the time goes in v14:
time: 327 us; the launch traced here: 326 us
  blocking collectives  211 us (65%)
  Pallas kernels  41.5 us (13%)
  waiting for transfers between devices  38.2 us (12%)
  between operations  13.2 us (4%)
  starting transfers between devices  8.16 us (2%)
  local copies, waits for them, and re-layouts  7.53 us (2%)
  other arithmetic  6.81 us (2%)
    all_to_all x4, blocking collectives, per_device(): lax.all_to_all(buffer, 'occ', split_axis=0, concat_axis=0, tiled=True)  211 us
    reduce_scatter x4, waiting for transfers between devices, per_device(): lax.psum_scatter(partial_gram, 'aux', scatter_dimension=0, tiled=True)  36.1 us
    pallas_call x4, Pallas kernels, domain_gram(): pl.pallas_call(functools.partial(_gram_kernel, tile=tile, per_source=labe...  28.9 us
    pallas_call x1, Pallas kernels, transform_into_slots(): pl.pallas_call(_transform_kernel, grid_spec=grid_spec, out_shape=[jax.Sha...  12.5 us
    all_to_all x1, starting transfers between devices, per_device(): lax.all_to_all(labels, 'occ', split_axis=0, concat_axis=0, tiled=True)  7.99 us
  transfers between devices with their start and end apart: 5, of which 2 were waited for; matrix products, arithmetic and copies ran while one was open for 2% of the time, Pallas kernels for 7%

profile of v14, /device:TPU:0, one launch (start us, length us, event | category | flops | bytes accessed | tf_op | source)
XLA Modules:
  0.0 326.3 jit_solution(16917703842174117037)
XLA Ops:
  6.5 0.9 convert_reduce_fusion
  7.4 0.8 select_reduce_fusion.1
  8.2 1.2 multiply_add_fusion.1
  9.4 0.1 select_reduce_fusion
  9.5 0.1 sub.14
  9.7 0.8 copy.16
  10.5 8.0 %all-to-all-start = ((s32[16,4,2]{1,2,0:T(2,128)}), s32[16,4,2]{1,2,0:T(2,128)S(1)}, u32[]{:S(2)}, u32[]{:S(2)}) async-start(s32[16,4,2]{1,2,0:T(2,128)} %copy.16), calls=%async_computation | async-start | bytes 32768 | tf_op jit(solution)/shard_map/all_to_all | solution.py:191
  18.5 3.3 %copy.18 = bf16[96,64,64]{2,1,0:T(8,128)(2,1)S(1)} copy(bf16[96,64,64]{0,2,1:T(8,128)(2,1)} %param.6) | data formatting | bytes 1572864 | tf_op args[1]
  21.8 2.2 fusion.2.w_ref
  24.0 2.1 all-to-all-done
  26.1 0.2 copy.17
  26.3 0.7 reshape.73.lab_ref
  26.9 12.5 %shard_map.55 = (bf16[32,64,1024]{2,1,0:T(8,128)(2,1)}, bf16[32,64,1024]{2,1,0:T(8,128)(2,1)}, bf16[32,64,1024]{2,1,0:T(8,128)(2,1)}, bf16[32,64,1024]{2,1,0:T(8,128)(2,1)}) custom-call(s32[96]{0:T(128)} %get-tuple-element.18.out_ref, s32[96]{0:T(128)} %get-tuple-element.19.slot_ref, bf16[96,64,1024]{2,1,0:T(8,128)(2,1)} %tc_ref, ...), custom_call_target="tpu_custom_call" | custom-call | flops 3221225472 | bytes 25165824 | tf_op jit(solution)/shard_map/pallas_call | solution.py:93
  39.5 55.5 %all_to_all.25 = bf16[16,128,1024]{2,1,0:T(8,128)(2,1)} all-to-all(bf16[16,128,1024]{2,1,0:T(8,128)(2,1)} %bitcast.16), channel_id=1, replica_groups=mesh['aux'=8,'occ'=16] {'occ'}, dimensions={0} | all-to-all | bytes 8388608 | tf_op jit(solution)/shard_map/all_to_all | solution.py:200
  95.0 7.2 %shard_map.57 = f32[1024,1024]{1,0:T(8,128)} custom-call(s32[128]{0:T(128)} %reshape.73.lab_ref, bf16[16,2,64,1024]{3,2,1,0:T(8,128)(2,1)} %bitcast.10), custom_call_target="tpu_custom_call" | custom-call | flops 2147483648 | bytes 8388608 | tf_op jit(solution)/shard_map/pallas_call | solution.py:157
  102.3 53.5 %all_to_all.26 = bf16[16,128,1024]{2,1,0:T(8,128)(2,1)} all-to-all(bf16[16,128,1024]{2,1,0:T(8,128)(2,1)} %bitcast.15), channel_id=1, replica_groups=mesh['aux'=8,'occ'=16] {'occ'}, dimensions={0} | all-to-all | bytes 8388608 | tf_op jit(solution)/shard_map/all_to_all | solution.py:200
  155.7 7.3 %shard_map.56 = f32[1024,1024]{1,0:T(8,128)} custom-call(s32[128]{0:T(128)} %reshape.73.lab_ref, bf16[16,2,64,1024]{3,2,1,0:T(8,128)(2,1)} %bitcast.11), custom_call_target="tpu_custom_call" | custom-call | flops 2147483648 | bytes 8388608 | tf_op jit(solution)/shard_map/pallas_call | solution.py:157
  163.1 51.6 %all_to_all.27 = bf16[16,128,1024]{2,1,0:T(8,128)(2,1)} all-to-all(bf16[16,128,1024]{2,1,0:T(8,128)(2,1)} %bitcast.14), channel_id=1, replica_groups=mesh['aux'=8,'occ'=16] {'occ'}, dimensions={0} | all-to-all | bytes 8388608 | tf_op jit(solution)/shard_map/all_to_all | solution.py:200
  214.6 7.2 %shard_map.58 = f32[1024,1024]{1,0:T(8,128)} custom-call(s32[128]{0:T(128)} %reshape.73.lab_ref, bf16[16,2,64,1024]{3,2,1,0:T(8,128)(2,1)} %bitcast.12), custom_call_target="tpu_custom_call" | custom-call | flops 2147483648 | bytes 8388608 | tf_op jit(solution)/shard_map/pallas_call | solution.py:157
  221.9 50.4 %all_to_all.28 = bf16[16,128,1024]{2,1,0:T(8,128)(2,1)} all-to-all(bf16[16,128,1024]{2,1,0:T(8,128)(2,1)} %bitcast.13), channel_id=1, replica_groups=mesh['aux'=8,'occ'=16] {'occ'}, dimensions={0} | all-to-all | bytes 8388608 | tf_op jit(solution)/shard_map/all_to_all | solution.py:200
  272.3 7.3 %shard_map.59 = f32[1024,1024]{1,0:T(8,128)} custom-call(s32[128]{0:T(128)} %reshape.73.lab_ref, bf16[16,2,64,1024]{3,2,1,0:T(8,128)(2,1)} %bitcast.9), custom_call_target="tpu_custom_call" | custom-call | flops 2147483648 | bytes 8388608 | tf_op jit(solution)/shard_map/pallas_call | solution.py:157
  279.7 36.0 %reduce-scatter.11.cloned.1.call-done = f32[128,1024]{1,0:T(8,128)} async-done(((f32[1024,1024]{1,0:T(8,128)}), f32[128,1024]{1,0:T(8,128)}) %reduce-scatter.11.cloned.1.call-update) | async-done | bytes 524304 | tf_op jit(solution)/shard_map/reduce_scatter | solution.py:203
  315.7 1.7 pad_maximum_fusion
  317.4 2.4 reshape.82
  (12 shorter events, 0.3 us)
Async XLA Ops:
  10.5 15.6 %all-to-all-start = ((s32[16,4,2]{1,2,0:T(2,128)}), s32[16,4,2]{1,2,0:T(2,128)S(1)}, u32[]{:S(2)}, u32[]{:S(2)}) async-start(s32[16,4,2]{1,2,0:T(2,128)} %copy.16), calls=%async_computation | async-start | bytes 32768 | tf_op jit(solution)/shard_map/all_to_all | solution.py:191
  18.5 261.1 %reduce-scatter.7.cloned.1.call-start = ((), (), s32[]{:S(2)}) async-start(), calls=%async_computation.10 | async-start | bytes 4718592 | tf_op jit(solution)/shard_map/reduce_scatter | solution.py:203
  102.2 177.4 %reduce-scatter.5.cloned.1.call-start = ((), (), s32[]{:S(2)}) async-start(), calls=%async_computation.9 | async-start | bytes 4718592 | tf_op jit(solution)/shard_map/reduce_scatter | solution.py:203
  163.0 116.6 %reduce-scatter.9.cloned.1.call-start = ((), (), s32[]{:S(2)}) async-start(), calls=%async_computation.11 | async-start | bytes 4718592 | tf_op jit(solution)/shard_map/reduce_scatter | solution.py:203
  221.9 93.8 %reduce-scatter.11.cloned.1.call-start = ((), (), s32[]{:S(2)}) async-start(), calls=%async_computation.12 | async-start | bytes 4718592 | tf_op jit(solution)/shard_map/reduce_scatter | solution.py:203
Sparse Core Ops, SparseCore 0:
  102.3 36.7 reduce-scatter.6
  163.1 36.7 reduce-scatter.4
  222.0 36.7 reduce-scatter.8
  279.7 35.9 reduce-scatter.10

commit v15 on v14

--- a/solution.py
+++ b/solution.py
@@ -66,7 +66,7 @@
 def transform_into_slots(three_center, coefficients, out_index, slot_index, group_slots):
     pair_count, rows, width = three_center.shape
     tile = coefficients.shape[1]
-    steps = 4 if pair_count % 4 == 0 else 1
+    steps = 3 if pair_count % 3 == 0 else 1
     per = pair_count // steps
     zeros = jnp.zeros_like(coefficients)
     w2 = jnp.concatenate(

time: 327 us -> 328 us (level)
  no operation moved by 1% of the time
where the time goes in v15:
time: 328 us; the launch traced here: 327 us
  blocking collectives  211 us (64%)
  Pallas kernels  42.8 us (13%)
  waiting for transfers between devices  38.2 us (12%)
  between operations  13.2 us (4%)
  starting transfers between devices  8.16 us (2%)
  local copies, waits for them, and re-layouts  7.53 us (2%)
  other arithmetic  6.81 us (2%)
    all_to_all x4, blocking collectives, per_device(): lax.all_to_all(buffer, 'occ', split_axis=0, concat_axis=0, tiled=True)  211 us
    reduce_scatter x4, waiting for transfers between devices, per_device(): lax.psum_scatter(partial_gram, 'aux', scatter_dimension=0, tiled=True)  36.1 us
    pallas_call x4, Pallas kernels, domain_gram(): pl.pallas_call(functools.partial(_gram_kernel, tile=tile, per_source=labe...  29.1 us
    pallas_call x1, Pallas kernels, transform_into_slots(): pl.pallas_call(_transform_kernel, grid_spec=grid_spec, out_shape=[jax.Sha...  13.8 us
    all_to_all x1, starting transfers between devices, per_device(): lax.all_to_all(labels, 'occ', split_axis=0, concat_axis=0, tiled=True)  7.99 us
  transfers between devices with their start and end apart: 5, of which 2 were waited for; matrix products, arithmetic and copies ran while one was open for 2% of the time, Pallas kernels for 7%

profile of v15, /device:TPU:0, one launch (start us, length us, event | category | flops | bytes accessed | tf_op | source)
XLA Modules:
  0.0 327.4 jit_solution(5467831021449449220)
XLA Ops:
  6.5 0.9 convert_reduce_fusion
  7.4 0.8 select_reduce_fusion.1
  8.2 1.2 multiply_add_fusion.1
  9.4 0.1 select_reduce_fusion
  9.5 0.1 sub.14
  9.7 0.8 copy.16
  10.5 8.0 %all-to-all-start = ((s32[16,4,2]{1,2,0:T(2,128)}), s32[16,4,2]{1,2,0:T(2,128)S(1)}, u32[]{:S(2)}, u32[]{:S(2)}) async-start(s32[16,4,2]{1,2,0:T(2,128)} %copy.16), calls=%async_computation | async-start | bytes 32768 | tf_op jit(solution)/shard_map/all_to_all | solution.py:191
  18.5 3.3 %copy.18 = bf16[96,64,64]{2,1,0:T(8,128)(2,1)S(1)} copy(bf16[96,64,64]{0,2,1:T(8,128)(2,1)} %param.6) | data formatting | bytes 1572864 | tf_op args[1]
  21.8 2.2 fusion.2.w_ref
  24.0 2.1 all-to-all-done
  26.1 0.2 copy.17
  26.3 0.7 reshape.73.lab_ref
  26.9 13.8 %shard_map.55 = (bf16[32,64,1024]{2,1,0:T(8,128)(2,1)}, bf16[32,64,1024]{2,1,0:T(8,128)(2,1)}, bf16[32,64,1024]{2,1,0:T(8,128)(2,1)}, bf16[32,64,1024]{2,1,0:T(8,128)(2,1)}) custom-call(s32[96]{0:T(128)} %get-tuple-element.18.out_ref, s32[96]{0:T(128)} %get-tuple-element.19.slot_ref, bf16[96,64,1024]{2,1,0:T(8,128)(2,1)} %tc_ref, ...), custom_call_target="tpu_custom_call" | custom-call | flops 3221225472 | bytes 25165824 | tf_op jit(solution)/shard_map/pallas_call | solution.py:93
  40.7 55.5 %all_to_all.25 = bf16[16,128,1024]{2,1,0:T(8,128)(2,1)} all-to-all(bf16[16,128,1024]{2,1,0:T(8,128)(2,1)} %bitcast.16), channel_id=1, replica_groups=mesh['aux'=8,'occ'=16] {'occ'}, dimensions={0} | all-to-all | bytes 8388608 | tf_op jit(solution)/shard_map/all_to_all | solution.py:200
  96.2 7.4 %shard_map.57 = f32[1024,1024]{1,0:T(8,128)} custom-call(s32[128]{0:T(128)} %reshape.73.lab_ref, bf16[16,2,64,1024]{3,2,1,0:T(8,128)(2,1)} %bitcast.10), custom_call_target="tpu_custom_call" | custom-call | flops 2147483648 | bytes 8388608 | tf_op jit(solution)/shard_map/pallas_call | solution.py:157
  103.8 53.3 %all_to_all.26 = bf16[16,128,1024]{2,1,0:T(8,128)(2,1)} all-to-all(bf16[16,128,1024]{2,1,0:T(8,128)(2,1)} %bitcast.15), channel_id=1, replica_groups=mesh['aux'=8,'occ'=16] {'occ'}, dimensions={0} | all-to-all | bytes 8388608 | tf_op jit(solution)/shard_map/all_to_all | solution.py:200
  157.0 7.2 %shard_map.56 = f32[1024,1024]{1,0:T(8,128)} custom-call(s32[128]{0:T(128)} %reshape.73.lab_ref, bf16[16,2,64,1024]{3,2,1,0:T(8,128)(2,1)} %bitcast.11), custom_call_target="tpu_custom_call" | custom-call | flops 2147483648 | bytes 8388608 | tf_op jit(solution)/shard_map/pallas_call | solution.py:157
  164.3 51.4 %all_to_all.27 = bf16[16,128,1024]{2,1,0:T(8,128)(2,1)} all-to-all(bf16[16,128,1024]{2,1,0:T(8,128)(2,1)} %bitcast.14), channel_id=1, replica_groups=mesh['aux'=8,'occ'=16] {'occ'}, dimensions={0} | all-to-all | bytes 8388608 | tf_op jit(solution)/shard_map/all_to_all | solution.py:200
  215.8 7.2 %shard_map.58 = f32[1024,1024]{1,0:T(8,128)} custom-call(s32[128]{0:T(128)} %reshape.73.lab_ref, bf16[16,2,64,1024]{3,2,1,0:T(8,128)(2,1)} %bitcast.12), custom_call_target="tpu_custom_call" | custom-call | flops 2147483648 | bytes 8388608 | tf_op jit(solution)/shard_map/pallas_call | solution.py:157
  223.1 50.4 %all_to_all.28 = bf16[16,128,1024]{2,1,0:T(8,128)(2,1)} all-to-all(bf16[16,128,1024]{2,1,0:T(8,128)(2,1)} %bitcast.13), channel_id=1, replica_groups=mesh['aux'=8,'occ'=16] {'occ'}, dimensions={0} | all-to-all | bytes 8388608 | tf_op jit(solution)/shard_map/all_to_all | solution.py:200
  273.5 7.2 %shard_map.59 = f32[1024,1024]{1,0:T(8,128)} custom-call(s32[128]{0:T(128)} %reshape.73.lab_ref, bf16[16,2,64,1024]{3,2,1,0:T(8,128)(2,1)} %bitcast.9), custom_call_target="tpu_custom_call" | custom-call | flops 2147483648 | bytes 8388608 | tf_op jit(solution)/shard_map/pallas_call | solution.py:157
  280.8 36.0 %reduce-scatter.11.cloned.1.call-done = f32[128,1024]{1,0:T(8,128)} async-done(((f32[1024,1024]{1,0:T(8,128)}), f32[128,1024]{1,0:T(8,128)}) %reduce-scatter.11.cloned.1.call-update) | async-done | bytes 524304 | tf_op jit(solution)/shard_map/reduce_scatter | solution.py:203
  316.8 1.7 pad_maximum_fusion
  318.5 2.4 reshape.82
  (12 shorter events, 0.3 us)
Async XLA Ops:
  10.5 15.6 %all-to-all-start = ((s32[16,4,2]{1,2,0:T(2,128)}), s32[16,4,2]{1,2,0:T(2,128)S(1)}, u32[]{:S(2)}, u32[]{:S(2)}) async-start(s32[16,4,2]{1,2,0:T(2,128)} %copy.16), calls=%async_computation | async-start | bytes 32768 | tf_op jit(solution)/shard_map/all_to_all | solution.py:191
  18.5 262.3 %reduce-scatter.7.cloned.1.call-start = ((), (), s32[]{:S(2)}) async-start(), calls=%async_computation.10 | async-start | bytes 4718592 | tf_op jit(solution)/shard_map/reduce_scatter | solution.py:203
  103.7 177.1 %reduce-scatter.5.cloned.1.call-start = ((), (), s32[]{:S(2)}) async-start(), calls=%async_computation.9 | async-start | bytes 4718592 | tf_op jit(solution)/shard_map/reduce_scatter | solution.py:203
  164.3 116.5 %reduce-scatter.9.cloned.1.call-start = ((), (), s32[]{:S(2)}) async-start(), calls=%async_computation.11 | async-start | bytes 4718592 | tf_op jit(solution)/shard_map/reduce_scatter | solution.py:203
  223.0 93.8 %reduce-scatter.11.cloned.1.call-start = ((), (), s32[]{:S(2)}) async-start(), calls=%async_computation.12 | async-start | bytes 4718592 | tf_op jit(solution)/shard_map/reduce_scatter | solution.py:203
Sparse Core Ops, SparseCore 0:
  103.8 36.5 reduce-scatter.6
  164.4 37.0 reduce-scatter.4
  223.1 36.9 reduce-scatter.8
  280.9 35.9 reduce-scatter.10
